TPU v7x, 512 devices: a whole 4x8x8 slice. The times are simulated.
512 devices in a mesh: dp: 16 (over x, y_hi, core), ctx: 32 (over z, y_lo).
Axes of the slice: x: 4, y: 8 (y_hi: 2, y_lo: 4; y = y_hi * 4 + y_lo), z: 8, core: 2. Of those that a mesh axis runs over, the one named last changes fastest.
Arguments:
- queries: bfloat16 [16, 4096, 512], P('dp', 'ctx'), may hold values from -6 to 6
- keys: bfloat16 [16, 4096, 512], P('dp', 'ctx'), may hold values from -6 to 6
- values: bfloat16 [16, 4096, 512], P('dp', 'ctx'), may hold values from -6 to 6
- grad_out: bfloat16 [16, 4096, 8192], P('dp', 'ctx'), may hold values from -6 to 6
- out_weight: bfloat16 [512, 8192], P(None, 'ctx'), may hold values from -0.25 to 0.25
- residues: float32 [512, 16], P('ctx'), may hold values from -0.125 to 0.125
- decays: float32 [512, 16], P('ctx'), may hold values from 1.2207031e-05 to 0.1
Outputs:
- grad_queries: bfloat16 [16, 4096, 512], P('dp', None, 'ctx')
- grad_keys: bfloat16 [16, 4096, 512], P('dp', None, 'ctx')
- grad_values: bfloat16 [16, 4096, 512], P('dp', None, 'ctx')
- grad_weight: float32 [512, 8192], P(None, 'ctx')
- grad_residues: float32 [512, 16], P('ctx')
- grad_decays: float32 [512, 16], P('ctx')
All inputs are finite; a program needn't handle non-finite values.
Results may differ from a plain program's by a relative error of at most 0.017.
Values may be sent and summed in bfloat16 or wider, within the bound.
No kernel may reach another device: no remote copies, remote signals or barrier semaphores. Data moves between devices by JAX's collectives and lax.ppermute only.
A program may use at most 128 MiB of HBM per device.

v0:
```python
import math

import jax
import jax.numpy as jnp
from jax import lax
from jax.sharding import PartitionSpec as P

FFT_COLS = 128


HIGHEST = lax.Precision.HIGHEST


def fourier_tables(fft_rows, fft_cols):
    total = fft_rows * fft_cols
    row_index = jnp.arange(fft_rows, dtype=jnp.int32)
    col_index = jnp.arange(fft_cols, dtype=jnp.int32)
    first = (row_index[:, None] * row_index[None, :] % fft_rows).astype(jnp.float32) * (
        2.0 * math.pi / fft_rows
    )
    twist = (row_index[:, None] * col_index[None, :] % total).astype(jnp.float32) * (
        2.0 * math.pi / total
    )
    second = (col_index[:, None] * col_index[None, :] % fft_cols).astype(jnp.float32) * (
        2.0 * math.pi / fft_cols
    )
    return (
        (jnp.cos(first), -jnp.sin(first)),
        (jnp.cos(twist), -jnp.sin(twist)),
        (jnp.cos(second), -jnp.sin(second)),
    )


def complex_product(left_re, left_im, right_re, right_im):
    return (left_re * right_re - left_im * right_im, left_re * right_im + left_im * right_re)


def apply_middle(table_re, table_im, data_re):

    def single(table, data):
        return jnp.einsum("kn,cnm->ckm", table, data, precision=HIGHEST)

    return (single(table_re, data_re), single(table_im, data_re))


def apply_last(table_re, table_im, data_re, data_im):

    def single(data, table):
        return jnp.einsum("ckm,mj->ckj", data, table, precision=HIGHEST)

    return (
        single(data_re, table_re) - single(data_im, table_im),
        single(data_im, table_re) + single(data_re, table_im),
    )


def forward_transform(signal, tables):
    (first_re, first_im), (twist_re, twist_im), (second_re, second_im) = tables
    section_re, section_im = apply_middle(first_re, first_im, signal)
    section_re, section_im = complex_product(section_re, section_im, twist_re, twist_im)
    return apply_last(second_re, second_im, section_re, section_im)


def inverse_transform(spec_re, spec_im, tables):
    (first_re, first_im), (twist_re, twist_im), (second_re, second_im) = tables
    section_re, section_im = apply_last(second_re, -second_im, spec_re, spec_im)
    section_re, section_im = complex_product(section_re, section_im, twist_re, -twist_im)
    result = jnp.einsum("kn,cnm->ckm", first_re, section_re, precision=HIGHEST) + jnp.einsum(
        "kn,cnm->ckm", first_im, section_im, precision=HIGHEST
    )
    total = first_re.shape[0] * second_re.shape[0]
    return result / float(total)


def padded_grid(signal, fft_rows, fft_cols):
    channels, seq_len = signal.shape
    padded = jnp.concatenate(
        [signal, jnp.zeros((channels, fft_rows * fft_cols - seq_len), jnp.float32)], axis=1
    )
    return padded.reshape(channels, fft_rows, fft_cols)


def leading_part(grid, seq_len):
    return grid.reshape(grid.shape[0], -1)[:, :seq_len]


def channels_first(block):
    return block[0].astype(jnp.float32).T


def rounded_sum(terms):
    rounded = lax.optimization_barrier(terms.astype(jnp.bfloat16))
    return jnp.sum(rounded.astype(jnp.float32), axis=0)


def body(queries, keys, values, grad_out, out_weight, residues, decays):
    channels = out_weight.shape[0]
    block_width = out_weight.shape[1]
    tok_rows = grad_out.shape[1]
    grad_cols = lax.all_to_all(grad_out, "ctx", split_axis=2, concat_axis=1, tiled=True)
    shard_piece = lax.all_gather(out_weight, "ctx", axis=1, tiled=True)
    blocks = shard_piece.shape[1] // block_width
    partial_value = grad_out[0]
    partial_value = partial_value.reshape(tok_rows, blocks, block_width)
    weight_part = shard_piece.reshape(channels, blocks, block_width)
    terms = jnp.einsum(
        "tks,cks->ktc", partial_value, weight_part, preferred_element_type=jnp.float32
    )
    gated_sum = rounded_sum(terms)
    grad_gated = gated_sum.astype(jnp.bfloat16)[None]
    query_ch, key_ch, value_ch, gated_grad_ch = (
        lax.all_to_all(queries, "ctx", split_axis=2, concat_axis=1, tiled=True),
        lax.all_to_all(keys, "ctx", split_axis=2, concat_axis=1, tiled=True),
        lax.all_to_all(values, "ctx", split_axis=2, concat_axis=1, tiled=True),
        lax.all_to_all(grad_gated, "ctx", split_axis=2, concat_axis=1, tiled=True),
    )
    grad_gated_full = channels_first(gated_grad_ch)
    seq_len = query_ch.shape[1]
    fft_rows = 2 * seq_len // FFT_COLS
    tables = fourier_tables(fft_rows, FFT_COLS)
    query_full = channels_first(query_ch)
    key_full = channels_first(key_ch)
    value_full = channels_first(value_ch)
    positions = jnp.arange(seq_len).astype(jnp.float32)
    decay_terms = jnp.exp(-decays[:, :, None] * positions[None, None, :])
    filter_taps = jnp.sum(residues[:, :, None] * decay_terms, axis=1)
    product = key_full * value_full
    grad_conv = grad_gated_full * query_full
    prod_re, prod_im = forward_transform(padded_grid(product, fft_rows, FFT_COLS), tables)
    taps_re, taps_im = forward_transform(padded_grid(filter_taps, fft_rows, FFT_COLS), tables)
    grad_re, grad_im = forward_transform(padded_grid(grad_conv, fft_rows, FFT_COLS), tables)
    conv_out = leading_part(
        inverse_transform(*complex_product(prod_re, prod_im, taps_re, taps_im), tables), seq_len
    )
    grad_product = leading_part(
        inverse_transform(*complex_product(taps_re, -taps_im, grad_re, grad_im), tables), seq_len
    )
    grad_taps = leading_part(
        inverse_transform(*complex_product(prod_re, -prod_im, grad_re, grad_im), tables), seq_len
    )
    gated = (query_full * conv_out).T.astype(jnp.bfloat16)[None]
    grad_queries = (grad_gated_full * conv_out).T.astype(jnp.bfloat16)[None]
    grad_keys = (grad_product * value_full).T.astype(jnp.bfloat16)[None]
    grad_values = (grad_product * key_full).T.astype(jnp.bfloat16)[None]
    partial_value = lax.dot_general(
        lax.all_gather(gated, "ctx", axis=2, tiled=True)[0],
        grad_cols[0],
        (((0,), (0,)), ((), ())),
        preferred_element_type=jnp.float32,
    )
    grad_weight = partial_value
    grad_residues = jnp.sum(grad_taps[:, None, :] * decay_terms, axis=2)
    grad_decays = -residues * jnp.sum(
        (grad_taps * positions[None, :])[:, None, :] * decay_terms, axis=2
    )
    grad_weight, grad_residues, grad_decays = (
        lax.psum(grad_weight.astype(jnp.bfloat16), "dp").astype(jnp.float32),
        lax.psum(grad_residues.astype(jnp.bfloat16), "dp").astype(jnp.float32),
        lax.psum(grad_decays.astype(jnp.bfloat16), "dp").astype(jnp.float32),
    )
    return (grad_queries, grad_keys, grad_values, grad_weight, grad_residues, grad_decays)


def solution(mesh):
    placed = (
        P("dp", "ctx", None),
        P("dp", "ctx", None),
        P("dp", "ctx", None),
        P("dp", "ctx", None),
        P(None, "ctx"),
        P("ctx", None),
        P("ctx", None),
    )
    return jax.shard_map(
        body,
        mesh=mesh,
        in_specs=placed,
        out_specs=(
            P("dp", None, "ctx"),
            P("dp", None, "ctx"),
            P("dp", None, "ctx"),
            P(None, "ctx"),
            P("ctx", None),
            P("ctx", None),
        ),
        check_vma=False,
    )
```

profile of v0, /device:TPU:1, one launch (start us, length us, event | category | flops | bytes accessed | tf_op | source)
XLA Modules:
  0.0 643.5 jit_solution(12135610993121922258)
XLA Ops:
  7.2 1.8 copy.52
  10.7 1.4 reduce.3
  12.8 14.3 %all-to-all-start.3 = ((bf16[32,2,1024]{2,1,0:T(2,128)(2,1)}), bf16[32,2,1024]{2,1,0:T(2,128)(2,1)S(1)}, u32[]{:S(2)}, u32[]{:S(2)}) async-start(bf16[32,2,1024]{2,1,0:T(2,128)(2,1)} %reshape.139), calls=%async_computation.3 | async-start | bytes 262144 | tf_op jit(solution)/shard_map/all_to_all | solution.py:112
  28.1 1.4 reduce.2
  30.2 6.9 %all-to-all-done.3 = bf16[32,2,1024]{2,1,0:T(2,128)(2,1)S(1)} async-done(((bf16[32,2,1024]{2,1,0:T(2,128)(2,1)}), bf16[32,2,1024]{2,1,0:T(2,128)(2,1)S(1)}, u32[]{:S(2)}, u32[]{:S(2)}) %all-to-all-start.3) | async-done | bytes 131104 | tf_op jit(solution)/shard_map/all_to_all | solution.py:112
  37.1 3.9 all-to-all-start.1
  42.8 1.4 reduce.1
  44.9 2.2 copy.71
  47.5 5.4 all-to-all-done.1
  52.9 4.8 all-to-all-start.2
  58.8 10.7 %all-to-all-done.2 = bf16[32,2,1024]{2,1,0:T(2,128)(2,1)S(1)} async-done(((bf16[32,2,1024]{2,1,0:T(2,128)(2,1)}), bf16[32,2,1024]{2,1,0:T(2,128)(2,1)S(1)}, u32[]{:S(2)}, u32[]{:S(2)}) %all-to-all-start.2) | async-done | bytes 131104 | tf_op jit(solution)/shard_map/all_to_all | solution.py:114
  72.8 1.6 fusion.47
  74.4 1.7 convolution_add_fusion.8
  76.1 139.2 %all-gather.4.cloned.1.call-done = bf16[512,8192]{0,1:T(8,128)(2,1)} async-done(((bf16[512,256]{0,1:T(8,128)(2,1)}), bf16[512,8192]{0,1:T(8,128)(2,1)}) %all-gather.4.cloned.1.call-update) | async-done | bytes 8388624 | tf_op jit(solution)/shard_map/all_gather | solution.py:101
  215.3 8.2 %convolution_convert_fusion = bf16[32,128,512]{2,1,0:T(8,128)(2,1)} fusion(bf16[512,32,256]{0,2,1:T(8,128)(2,1)} %bitcast.283, bf16[128,32,256]{2,1,0:T(8,128)(2,1)S(1)} %bitcast.284), kind=kOutput, calls=%fused_computation.4 | convolution fusion | flops 1075838976 | bytes 14680064 | tf_op jit(solution)/shard_map/tks,cks->ktc/dot_general | solution.py:106
  223.5 2.9 reduce_sum.39
  226.5 1.4 reduce.4
  228.6 6.2 all-to-all-start
  236.0 8.8 %all-to-all-done = bf16[32,2,1024]{2,1,0:T(2,128)(2,1)S(1)} async-done(((bf16[32,2,1024]{2,1,0:T(2,128)(2,1)}), bf16[32,2,1024]{2,1,0:T(2,128)(2,1)S(1)}, u32[]{:S(2)}, u32[]{:S(2)}) %all-to-all-start) | async-done | bytes 131104 | tf_op jit(solution)/shard_map/all_to_all | solution.py:115
  255.6 2.5 multiply_reduce_fusion
  269.7 7.1 %copy.67 = bf16[1,128,8192]{1,0,2:T(2,128)(2,1)} copy(bf16[1,128,8192]{2,1,0:T(8,128)(2,1)S(1)} %copy-done) | data formatting | bytes 4194304 | tf_op args[3]
  276.8 45.2 %reduce.5 = bf16[8192,128]{1,0:T(8,128)(2,1)S(1)} reduce(bf16[8192,1,128]{2,1,0:T(2,128)(2,1)} %bitcast.285, bf16[]{:T(256)} %broadcast.247), dimensions={1}, to_apply=%bitcast.253.reduce_sub_computation | reduce | bytes 4194306
  321.9 2.1 reshape.143
  324.0 91.9 %all_to_all.51 = bf16[32,2,16384]{2,1,0:T(2,128)(2,1)S(1)} all-to-all(bf16[32,2,16384]{2,1,0:T(2,128)(2,1)} %reshape.143), channel_id=1, replica_groups=mesh['dp'=16,'ctx'=32] {'ctx'}, dimensions={0} | all-to-all | bytes 4194304 | tf_op jit(solution)/shard_map/all_to_all | solution.py:100
  415.9 6.8 %reshape.144 = bf16[8192,1,128]{2,1,0:T(2,128)(2,1)} reshape(bf16[32,2,16384]{2,1,0:T(2,128)(2,1)S(1)} %all_to_all.51) | data formatting | bytes 4194304
  422.7 2.5 copy.70
  425.2 2.9 copy.68
  433.3 1.5 all-gather.6.cloned.1.call-done
  434.8 4.8 convolution_convert_fusion.1
  440.7 58.5 %all-reduce.3 = (bf16[16,16]{1,0:T(8,128)(2,1)S(1)}, bf16[16,16]{1,0:T(8,128)(2,1)S(1)}) all-reduce(bf16[16,16]{1,0:T(8,128)(2,1)S(1)} %get-tuple-element.7, bf16[16,16]{1,0:T(8,128)(2,1)S(1)} %multiply_convert_fusion), channel_id=1, replica_groups=mesh['dp'=16,'ctx'=32] {'dp'}, use_global_device_ids=true, to_apply=%region_4.5 | all-reduce | flops 512 | bytes 2048 | tf_op jit(solution)/shard_map/psum | solution.py:158
  500.4 134.6 %all-reduce.6.cloned.1.call-done = bf16[512,256]{1,0:T(8,128)(2,1)} async-done(((bf16[512,256]{1,0:T(8,128)(2,1)}), bf16[512,256]{1,0:T(8,128)(2,1)}) %all-reduce.6.cloned.1.call-update) | async-done | bytes 262160 | tf_op jit(solution)/shard_map/psum | solution.py:157
  635.0 1.8 convert_element_type.259
  (102 shorter events, 42.5 us)
Async XLA Ops:
  7.2 208.1 %all-gather.4.cloned.1.call-start = ((), (), s32[]{:S(2)}) async-start(), calls=%async_computation.5 | async-start | bytes 8650752 | tf_op jit(solution)/shard_map/all_gather | solution.py:101
  12.8 24.3 %all-to-all-start.3 = ((bf16[32,2,1024]{2,1,0:T(2,128)(2,1)}), bf16[32,2,1024]{2,1,0:T(2,128)(2,1)S(1)}, u32[]{:S(2)}, u32[]{:S(2)}) async-start(bf16[32,2,1024]{2,1,0:T(2,128)(2,1)} %reshape.139), calls=%async_computation.3 | async-start | bytes 262144 | tf_op jit(solution)/shard_map/all_to_all | solution.py:112
  37.1 15.8 %all-to-all-start.1 = ((bf16[32,2,1024]{2,1,0:T(2,128)(2,1)}), bf16[32,2,1024]{2,1,0:T(2,128)(2,1)S(1)}, u32[]{:S(2)}, u32[]{:S(2)}) async-start(bf16[32,2,1024]{2,1,0:T(2,128)(2,1)} %reshape.137), calls=%async_computation.1 | async-start | bytes 262144 | tf_op jit(solution)/shard_map/all_to_all | solution.py:113
  52.9 16.6 %all-to-all-start.2 = ((bf16[32,2,1024]{2,1,0:T(2,128)(2,1)}), bf16[32,2,1024]{2,1,0:T(2,128)(2,1)S(1)}, u32[]{:S(2)}, u32[]{:S(2)}) async-start(bf16[32,2,1024]{2,1,0:T(2,128)(2,1)} %reshape.135), calls=%async_computation.2 | async-start | bytes 262144 | tf_op jit(solution)/shard_map/all_to_all | solution.py:114
  69.8 0.7 copy-start.2
  223.5 11.7 %copy-start.6 = (f32[16,64,128]{2,1,0:T(8,128)S(1)}, f32[16,64,128]{2,1,0:T(8,128)}, u32[]{:S(2)}) copy-start(f32[16,64,128]{2,1,0:T(8,128)} %fusion.47) | copy-start | bytes 1572868
  223.5 21.6 %copy-start.4 = (f32[1,32,128,16]{2,1,3,0:T(8,128)S(1)}, f32[1,32,128,16]{2,1,3,0:T(8,128)}, u32[]{:S(2)}) copy-start(f32[1,32,128,16]{2,1,3,0:T(8,128)} %copy.66) | copy-start | bytes 786436
  228.6 16.2 %all-to-all-start = ((bf16[32,2,1024]{2,1,0:T(2,128)(2,1)}), bf16[32,2,1024]{2,1,0:T(2,128)(2,1)S(1)}, u32[]{:S(2)}, u32[]{:S(2)}) async-start(bf16[32,2,1024]{2,1,0:T(2,128)(2,1)} %reshape.141), calls=%async_computation | async-start | bytes 262144 | tf_op jit(solution)/shard_map/all_to_all | solution.py:115
  234.9 199.9 %all-gather.6.cloned.1.call-start = ((), (), s32[]{:S(2)}) async-start(), calls=%async_computation.7 | async-start | bytes 4325376 | tf_op jit(solution)/shard_map/all_gather | solution.py:146
  245.4 4.1 copy-start.1
  252.0 3.6 copy-start.7
  265.0 3.6 copy-start.5
  265.9 3.8 copy-start
  269.6 365.4 %all-reduce.6.cloned.1.call-start = ((), (), s32[]{:S(2)}) async-start(), calls=%async_computation.6 | async-start | bytes 524288 | tf_op jit(solution)/shard_map/psum | solution.py:157
  433.3 6.3 copy-start.3
Sparse Core Ops, SparseCore 0:
  10.1 205.1 all-gather.3
  269.8 164.9 all-gather.5
  439.8 195.1 all-reduce.5
where the time goes:
time: 649 us; the launch traced here: 643 us
  waiting for transfers between devices  307 us (47%)
  blocking collectives  150 us (23%)
  other arithmetic  62.9 us (10%)
  matrix products  43.7 us (7%)
  local copies, waits for them, and re-layouts  35.2 us (5%)
  starting transfers between devices  29.6 us (5%)
  between operations  14.6 us (2%)
    all_gather x1, waiting for transfers between devices, body(): shard_piece = lax.all_gather(out_weight, 'ctx', axis=1, tiled=True)  139 us
    psum x1, waiting for transfers between devices, body(): lax.psum(grad_weight.astype(jnp.bfloat16), 'dp').astype(jnp.float32)  135 us
    all_to_all x1, blocking collectives, body(): lax.all_to_all(grad_out, 'ctx', split_axis=2, concat_axis=1, tiled=True)  91.9 us
    psum x1, blocking collectives, body(): lax.psum(grad_residues.astype(jnp.bfloat16), 'dp').astype(jnp.float32)  58.5 us
    unnamed x5, other arithmetic  50.8 us
    unnamed x43, local copies, waits for them, and re-layouts  31 us
    dot_general x24, matrix products, single(): return jnp.einsum('ckm,mj->ckj', data, table, precision=HIGHEST)  21.5 us
    all_to_all x1, starting transfers between devices, body(): lax.all_to_all(queries, 'ctx', split_axis=2, concat_axis=1, tiled=True)  14.3 us
  transfers between devices with their start and end apart: 7, of which 7 were waited for; matrix products, arithmetic and copies ran while one was open for 15% of the time, Pallas kernels for 0%

commit v1 on v0

--- a/solution.py
+++ b/solution.py
@@ -91,6 +91,71 @@
 def rounded_sum(terms):
     rounded = lax.optimization_barrier(terms.astype(jnp.bfloat16))
     return jnp.sum(rounded.astype(jnp.float32), axis=0)
+
+
+def axis_pairs(size, mask):
+    return [(index, index ^ mask) for index in range(size)]
+
+
+def ctx_masks(size):
+    bits = [1 << b for b in range(size.bit_length() - 1)]
+    low = [m for m in bits if m < 4]
+    high = [m for m in bits if m >= 4]
+    return tuple(reversed(high[1:])) + tuple(reversed(low[1:])) + tuple(high[:1]) + tuple(low[:1])
+
+
+def doubling_gather(block, axis, masks):
+    size = lax.axis_size(axis)
+    held = block
+    for mask in masks:
+        held = jnp.concatenate([held, lax.ppermute(held, axis, axis_pairs(size, mask))], axis=0)
+    return held
+
+
+def unpermute_blocks(rows, axis, masks):
+    size = lax.axis_size(axis)
+    me = lax.axis_index(axis)
+    wanted = me ^ jnp.arange(size, dtype=jnp.int32)
+    place = jnp.zeros_like(wanted)
+    for step, mask in enumerate(masks):
+        place = place | (((wanted & mask) != 0).astype(jnp.int32) << step)
+    blocks = rows.reshape(size, rows.shape[0] // size, rows.shape[1])
+    return jnp.take(blocks, place, axis=0).reshape(rows.shape)
+
+
+def dp_masks(size):
+    bits = [1 << b for b in range(size.bit_length() - 1)]
+    return tuple(bits[:1]) + tuple(bits[2:]) + tuple(bits[1:2])
+
+
+def summed_over_dp(grad_weight, grad_residues, grad_decays):
+    size = lax.axis_size("dp")
+    width = grad_weight.shape[1]
+    extra = jnp.stack([grad_residues.reshape(-1), grad_decays.reshape(-1)])
+    extra = jnp.pad(extra, ((0, 0), (0, width - extra.shape[1])))
+    rows = grad_weight.shape[0] + 2
+    padded_rows = -(-rows // size) * size
+    held = jnp.concatenate(
+        [grad_weight, extra, jnp.zeros((padded_rows - rows, width), jnp.float32)], axis=0
+    )
+    me = lax.axis_index("dp")
+    masks = dp_masks(size)
+    for mask in masks:
+        half = held.shape[0] // 2
+        low, high = held[:half], held[half:]
+        upper = (me & mask) != 0
+        keep = jnp.where(upper, high, low)
+        send = jnp.where(upper, low, high)
+        held = keep + lax.ppermute(send, "dp", axis_pairs(size, mask))
+    for mask in reversed(masks):
+        other = lax.ppermute(held, "dp", axis_pairs(size, mask))
+        upper = (me & mask) != 0
+        held = jnp.where(upper, jnp.concatenate([other, held]), jnp.concatenate([held, other]))
+    count = grad_residues.size
+    weight = held[: grad_weight.shape[0]]
+    residue_sum = held[grad_weight.shape[0], :count].reshape(grad_residues.shape)
+    decay_sum = held[grad_weight.shape[0] + 1, :count].reshape(grad_decays.shape)
+    return weight, residue_sum, decay_sum
 
 
 def body(queries, keys, values, grad_out, out_weight, residues, decays):
@@ -138,25 +203,26 @@
     grad_taps = leading_part(
         inverse_transform(*complex_product(prod_re, -prod_im, grad_re, grad_im), tables), seq_len
     )
-    gated = (query_full * conv_out).T.astype(jnp.bfloat16)[None]
+    gated_t = (query_full * conv_out).astype(jnp.bfloat16)
     grad_queries = (grad_gated_full * conv_out).T.astype(jnp.bfloat16)[None]
     grad_keys = (grad_product * value_full).T.astype(jnp.bfloat16)[None]
     grad_values = (grad_product * key_full).T.astype(jnp.bfloat16)[None]
+    ctx_size = lax.axis_size("ctx")
+    gather_masks = ctx_masks(ctx_size)
+    gathered = doubling_gather(gated_t, "ctx", gather_masks)
     partial_value = lax.dot_general(
-        lax.all_gather(gated, "ctx", axis=2, tiled=True)[0],
+        gathered,
         grad_cols[0],
-        (((0,), (0,)), ((), ())),
+        (((1,), (0,)), ((), ())),
         preferred_element_type=jnp.float32,
     )
-    grad_weight = partial_value
+    grad_weight = unpermute_blocks(partial_value, "ctx", gather_masks)
     grad_residues = jnp.sum(grad_taps[:, None, :] * decay_terms, axis=2)
     grad_decays = -residues * jnp.sum(
         (grad_taps * positions[None, :])[:, None, :] * decay_terms, axis=2
     )
-    grad_weight, grad_residues, grad_decays = (
-        lax.psum(grad_weight.astype(jnp.bfloat16), "dp").astype(jnp.float32),
-        lax.psum(grad_residues.astype(jnp.bfloat16), "dp").astype(jnp.float32),
-        lax.psum(grad_decays.astype(jnp.bfloat16), "dp").astype(jnp.float32),
+    grad_weight, grad_residues, grad_decays = summed_over_dp(
+        grad_weight, grad_residues, grad_decays
     )
     return (grad_queries, grad_keys, grad_values, grad_weight, grad_residues, grad_decays)
 

time: 649 us -> 566 us (0.87)
  blocking collectives: 150 us -> 0 us
  starting transfers between devices: 29.6 us -> 93 us
  local copies, waits for them, and re-layouts: 35.2 us -> 49.9 us
  waiting for transfers between devices: 307 us -> 295 us
    psum x1 -> x0, waiting for transfers between devices: 135 us -> none  [body(): lax.psum(grad_weight.astype(jnp.bfloat16), 'dp').astype(jnp.float32)]
    ppermute x0 -> x13, waiting for transfers between devices: none -> 123 us  [the longest x5 114 us: doubling_gather(): lax.ppermute(held, axis, axis_pairs(size, mask))]
    all_to_all x1 -> x0, blocking collectives: 91.9 us -> none  [body(): lax.all_to_all(grad_out, 'ctx', split_axis=2, concat_axis=1, tiled=True)]
    psum x1 -> x0, blocking collectives: 58.5 us -> none  [body(): lax.psum(grad_residues.astype(jnp.bfloat16), 'dp').astype(jnp.float32)]
    ppermute x0 -> x13, starting transfers between devices: none -> 57.1 us  [the longest x4 22.6 us: summed_over_dp(): other = lax.ppermute(held, 'dp', axis_pairs(size, mask))]
    unnamed x43 -> x65, local copies, waits for them, and re-layouts: 31 us -> 37.9 us
    unnamed x5 -> x6, other arithmetic: 50.8 us -> 51.7 us
  transfers between devices with their start and end apart: 7 -> 19, of which waited for: 7 -> 17; matrix products, arithmetic and copies ran while one was open for 15% -> 18% of each run, Pallas kernels for 0% -> 0%
where the time goes in v1:
time: 566 us; the launch traced here: 559 us
  waiting for transfers between devices  295 us (52%)
  starting transfers between devices  93 us (16%)
  other arithmetic  63.1 us (11%)
  local copies, waits for them, and re-layouts  49.9 us (9%)
  matrix products  43.1 us (8%)
  between operations  15.3 us (3%)
    all_gather x1, waiting for transfers between devices, body(): shard_piece = lax.all_gather(out_weight, 'ctx', axis=1, tiled=True)  139 us
    ppermute x5, waiting for transfers between devices, doubling_gather(): lax.ppermute(held, axis, axis_pairs(size, mask))  114 us
    unnamed x6, other arithmetic  51.7 us
    unnamed x65, local copies, waits for them, and re-layouts  37.9 us
    ppermute x4, starting transfers between devices, summed_over_dp(): other = lax.ppermute(held, 'dp', axis_pairs(size, mask))  22.6 us
    dot_general x24, matrix products, single(): return jnp.einsum('ckm,mj->ckj', data, table, precision=HIGHEST)  21.6 us
    ppermute x4, starting transfers between devices, summed_over_dp(): held = keep + lax.ppermute(send, 'dp', axis_pairs(size, mask))  21.5 us
    all_to_all x1, starting transfers between devices, body(): lax.all_to_all(queries, 'ctx', split_axis=2, concat_axis=1, tiled=True)  14.3 us
  transfers between devices with their start and end apart: 19, of which 17 were waited for; matrix products, arithmetic and copies ran while one was open for 18% of the time, Pallas kernels for 0%

profile of v1, /device:TPU:1, one launch (start us, length us, event | category | flops | bytes accessed | tf_op | source)
XLA Modules:
  0.0 559.3 jit_solution(7011197182111758625)
XLA Ops:
  12.7 14.3 %all-to-all-start.3 = ((bf16[32,2,1024]{2,1,0:T(2,128)(2,1)}), bf16[32,2,1024]{2,1,0:T(2,128)(2,1)S(1)}, u32[]{:S(2)}, u32[]{:S(2)}) async-start(bf16[32,2,1024]{2,1,0:T(2,128)(2,1)} %reshape.256), calls=%async_computation.3 | async-start | bytes 262144 | tf_op jit(solution)/shard_map/all_to_all | solution.py:177
  30.2 6.9 %all-to-all-done.3 = bf16[32,2,1024]{2,1,0:T(2,128)(2,1)S(1)} async-done(((bf16[32,2,1024]{2,1,0:T(2,128)(2,1)}), bf16[32,2,1024]{2,1,0:T(2,128)(2,1)S(1)}, u32[]{:S(2)}, u32[]{:S(2)}) %all-to-all-start.3) | async-done | bytes 131104 | tf_op jit(solution)/shard_map/all_to_all | solution.py:177
  37.1 3.9 all-to-all-start.1
  47.5 5.4 all-to-all-done.1
  52.9 4.9 all-to-all-start.2
  58.1 11.4 %all-to-all-done.2 = bf16[32,2,1024]{2,1,0:T(2,128)(2,1)S(1)} async-done(((bf16[32,2,1024]{2,1,0:T(2,128)(2,1)}), bf16[32,2,1024]{2,1,0:T(2,128)(2,1)S(1)}, u32[]{:S(2)}, u32[]{:S(2)}) %all-to-all-start.2) | async-done | bytes 131104 | tf_op jit(solution)/shard_map/all_to_all | solution.py:179
  76.1 139.1 %all-gather.2.cloned.1.call-done = bf16[512,8192]{0,1:T(8,128)(2,1)} async-done(((bf16[512,256]{0,1:T(8,128)(2,1)}), bf16[512,8192]{0,1:T(8,128)(2,1)}) %all-gather.2.cloned.1.call-update) | async-done | bytes 8388624 | tf_op jit(solution)/shard_map/all_gather | solution.py:166
  215.2 8.2 %convolution_convert_fusion = bf16[32,128,512]{2,1,0:T(8,128)(2,1)} fusion(bf16[512,32,256]{0,2,1:T(8,128)(2,1)} %bitcast.286, bf16[128,32,256]{2,1,0:T(8,128)(2,1)S(1)} %bitcast.287), kind=kOutput, calls=%fused_computation.5 | convolution fusion | flops 1075838976 | bytes 14680064 | tf_op jit(solution)/shard_map/tks,cks->ktc/dot_general | solution.py:171
  223.4 2.9 reduce_sum.39
  228.6 6.5 %all-to-all-start = ((bf16[32,2,1024]{2,1,0:T(2,128)(2,1)}), bf16[32,2,1024]{2,1,0:T(2,128)(2,1)S(1)}, u32[]{:S(2)}, u32[]{:S(2)}) async-start(bf16[32,2,1024]{2,1,0:T(2,128)(2,1)} %reshape.258), calls=%async_computation | async-start | bytes 262144 | tf_op jit(solution)/shard_map/all_to_all | solution.py:180
  235.9 9.0 %all-to-all-done = bf16[32,2,1024]{2,1,0:T(2,128)(2,1)S(1)} async-done(((bf16[32,2,1024]{2,1,0:T(2,128)(2,1)}), bf16[32,2,1024]{2,1,0:T(2,128)(2,1)S(1)}, u32[]{:S(2)}, u32[]{:S(2)}) %all-to-all-start) | async-done | bytes 131104 | tf_op jit(solution)/shard_map/all_to_all | solution.py:180
  272.1 7.5 %collective-permute-done = bf16[16,4096]{1,0:T(8,128)(2,1)S(1)} collective-permute-done((bf16[16,4096]{1,0:T(8,128)(2,1)S(1)}, bf16[16,4096]{1,0:T(8,128)(2,1)S(1)}, u32[]{:S(2)}, u32[]{:S(2)}) %collective-permute-start) | collective-permute-done | bytes 131104 | tf_op jit(solution)/shard_map/ppermute | solution.py:111
  281.7 12.7 %collective-permute-done.1 = bf16[32,4096]{1,0:T(8,128)(2,1)S(1)} collective-permute-done((bf16[32,4096]{1,0:T(8,128)(2,1)S(1)}, bf16[32,4096]{1,0:T(8,128)(2,1)S(1)}, u32[]{:S(2)}, u32[]{:S(2)}) %collective-permute-start.1) | collective-permute-done | bytes 262176 | tf_op jit(solution)/shard_map/ppermute | solution.py:111
  297.9 7.1 %copy.85 = bf16[1,128,8192]{1,0,2:T(2,128)(2,1)} copy(bf16[1,128,8192]{2,1,0:T(8,128)(2,1)S(1)} %copy-done) | data formatting | bytes 4194304 | tf_op args[3]
  304.9 45.2 %reduce.13 = bf16[8192,128]{1,0:T(8,128)(2,1)S(1)} reduce(bf16[8192,1,128]{2,1,0:T(2,128)(2,1)} %bitcast.288, bf16[]{:T(256)} %broadcast.471), dimensions={1}, to_apply=%bitcast.254.reduce_sub_computation | reduce | bytes 4194306
  352.2 6.4 %all-to-all-start.4 = ((bf16[32,2,16384]{2,1,0:T(2,128)(2,1)}), bf16[32,2,16384]{2,1,0:T(2,128)(2,1)S(1)}, u32[]{:S(2)}, u32[]{:S(2)}) async-start(bf16[32,2,16384]{2,1,0:T(2,128)(2,1)} %reshape.260), calls=%async_computation.4 | async-start | bytes 4194304 | tf_op jit(solution)/shard_map/all_to_all | solution.py:165
  359.8 3.1 collective-permute-start.3
  367.3 61.7 %collective-permute-done.3 = bf16[128,4096]{1,0:T(8,128)(2,1)S(1)} collective-permute-done((bf16[128,4096]{1,0:T(8,128)(2,1)S(1)}, bf16[128,4096]{1,0:T(8,128)(2,1)S(1)}, u32[]{:S(2)}, u32[]{:S(2)}) %collective-permute-start.3) | collective-permute-done | bytes 1048608 | tf_op jit(solution)/shard_map/ppermute | solution.py:111
  432.1 3.3 collective-permute-start.4
  435.7 6.8 %reshape.261 = bf16[8192,1,128]{2,1,0:T(2,128)(2,1)} reshape(bf16[32,2,16384]{2,1,0:T(2,128)(2,1)S(1)} %all-to-all-done.4) | data formatting | bytes 4194304
  445.0 2.9 copy.86
  448.1 32.0 %collective-permute-done.4 = bf16[256,4096]{1,0:T(8,128)(2,1)} collective-permute-done((bf16[256,4096]{1,0:T(8,128)(2,1)}, bf16[256,4096]{1,0:T(8,128)(2,1)}, u32[]{:S(2)}, u32[]{:S(2)}) %collective-permute-start.4) | collective-permute-done | bytes 2097184 | tf_op jit(solution)/shard_map/ppermute | solution.py:111
  480.1 3.1 constant_dynamic-update-slice_fusion.5
  483.2 4.2 fusion.323
  489.3 4.2 collective-permute-start.5
  494.8 3.1 collective-permute-start.6
  501.6 5.2 collective-permute-start.7
  508.6 9.0 %collective-permute-start.8 = (f32[33,256]{1,0:T(8,128)S(1)}, f32[33,256]{1,0:T(8,128)S(1)}, u32[]{:S(2)}, u32[]{:S(2)}) collective-permute-start(f32[33,256]{1,0:T(8,128)S(1)} %slice_select_fusion.3), channel_id=1, source_target_pairs={{0,64},{32,96},{64,0},{96,32},{128,192},{160,224},{192,128},{224,1... | collective-permute-start | bytes 101384 | tf_op jit(solution)/shard_map/ppermute | solution.py:149
  518.9 7.3 %collective-permute-start.9 = (f32[33,256]{1,0:T(8,128)S(1)}, f32[33,256]{1,0:T(8,128)S(1)}, u32[]{:S(2)}, u32[]{:S(2)}) collective-permute-start(f32[33,256]{1,0:T(8,128)S(1)} %select_add_fusion.3), channel_id=1, source_target_pairs={{0,64},{32,96},{64,0},{96,32},{128,192},{160,224},{192,128},{224,1... | collective-permute-start | bytes 101384 | tf_op jit(solution)/shard_map/ppermute | solution.py:151
  527.5 3.4 collective-permute-start.10
  534.1 3.1 collective-permute-start.11
  540.0 8.8 %collective-permute-start.12 = (f32[264,256]{1,0:T(8,128)S(1)}, f32[264,256]{1,0:T(8,128)S(1)}, u32[]{:S(2)}, u32[]{:S(2)}) collective-permute-start(f32[264,256]{1,0:T(8,128)S(1)} %maximum_select_fusion.1), channel_id=1, source_target_pairs={{0,32},{32,0},{64,96},{96,64},{128,160},{160,128},{192,224},{224,1... | collective-permute-start | bytes 811016 | tf_op jit(solution)/shard_map/ppermute | solution.py:151
  (174 shorter events, 91.2 us)
Async XLA Ops:
  7.2 208.1 %all-gather.2.cloned.1.call-start = ((), (), s32[]{:S(2)}) async-start(), calls=%async_computation.5 | async-start | bytes 8650752 | tf_op jit(solution)/shard_map/all_gather | solution.py:166
  12.7 24.3 %all-to-all-start.3 = ((bf16[32,2,1024]{2,1,0:T(2,128)(2,1)}), bf16[32,2,1024]{2,1,0:T(2,128)(2,1)S(1)}, u32[]{:S(2)}, u32[]{:S(2)}) async-start(bf16[32,2,1024]{2,1,0:T(2,128)(2,1)} %reshape.256), calls=%async_computation.3 | async-start | bytes 262144 | tf_op jit(solution)/shard_map/all_to_all | solution.py:177
  37.1 15.8 %all-to-all-start.1 = ((bf16[32,2,1024]{2,1,0:T(2,128)(2,1)}), bf16[32,2,1024]{2,1,0:T(2,128)(2,1)S(1)}, u32[]{:S(2)}, u32[]{:S(2)}) async-start(bf16[32,2,1024]{2,1,0:T(2,128)(2,1)} %reshape.254), calls=%async_computation.1 | async-start | bytes 262144 | tf_op jit(solution)/shard_map/all_to_all | solution.py:178
  52.9 16.7 %all-to-all-start.2 = ((bf16[32,2,1024]{2,1,0:T(2,128)(2,1)}), bf16[32,2,1024]{2,1,0:T(2,128)(2,1)S(1)}, u32[]{:S(2)}, u32[]{:S(2)}) async-start(bf16[32,2,1024]{2,1,0:T(2,128)(2,1)} %reshape.252), calls=%async_computation.2 | async-start | bytes 262144 | tf_op jit(solution)/shard_map/all_to_all | solution.py:179
  57.9 187.4 %copy-start.2 = (f32[1,32,128,16]{2,1,3,0:T(8,128)}, f32[1,32,128,16]{2,1,3,0:T(8,128)S(1)}, u32[]{:S(2)}) copy-start(f32[1,32,128,16]{2,1,3,0:T(8,128)S(1)} %copy.84) | copy-start | bytes 786436
  58.1 12.1 %copy-start.6 = (f32[1,32,128,16]{2,1,3,0:T(8,128)}, f32[1,32,128,16]{2,1,3,0:T(8,128)S(1)}, u32[]{:S(2)}) copy-start(f32[1,32,128,16]{2,1,3,0:T(8,128)S(1)} %copy.78) | copy-start | bytes 786436
  223.4 11.6 %copy-start.14 = (f32[16,64,128]{2,1,0:T(8,128)S(1)}, f32[16,64,128]{2,1,0:T(8,128)}, u32[]{:S(2)}) copy-start(f32[16,64,128]{2,1,0:T(8,128)} %fusion.48) | copy-start | bytes 1572868
  228.6 16.4 %all-to-all-start = ((bf16[32,2,1024]{2,1,0:T(2,128)(2,1)}), bf16[32,2,1024]{2,1,0:T(2,128)(2,1)S(1)}, u32[]{:S(2)}, u32[]{:S(2)}) async-start(bf16[32,2,1024]{2,1,0:T(2,128)(2,1)} %reshape.258), calls=%async_computation | async-start | bytes 262144 | tf_op jit(solution)/shard_map/all_to_all | solution.py:180
  245.2 4.4 copy-start.4
  245.6 4.1 copy-start.1
  252.2 3.6 copy-start.15
  265.9 31.9 %copy-start = (bf16[1,128,8192]{2,1,0:T(8,128)(2,1)S(1)}, bf16[1,128,8192]{2,1,0:T(8,128)(2,1)}, u32[]{:S(2)}) copy-start(bf16[1,128,8192]{2,1,0:T(8,128)(2,1)} %param.10) | copy-start | bytes 6291460
  268.7 11.0 %copy-start.11 = (f32[2,8,64,128]{3,1,2,0:T(8,128)}, f32[2,8,64,128]{3,1,2,0:T(8,128)S(1)}, u32[]{:S(2)}) copy-start(f32[2,8,64,128]{3,1,2,0:T(8,128)S(1)} %copy.122) | copy-start | bytes 1572868
  269.6 10.1 %collective-permute-start = (bf16[16,4096]{1,0:T(8,128)(2,1)S(1)}, bf16[16,4096]{1,0:T(8,128)(2,1)S(1)}, u32[]{:S(2)}, u32[]{:S(2)}) collective-permute-start(bf16[16,4096]{1,0:T(8,128)(2,1)S(1)} %get-tuple-element.12), channel_id=1, source_target_pairs={{0,16},{1,17},{2,18},{3,19},{4,20},{5,21},{6,22},{7,23},{8,24},{9,... | collective-permute-start | bytes 393224 | tf_op jit(solution)/shard_map/ppermute | solution.py:111
  279.7 14.8 %collective-permute-start.1 = (bf16[32,4096]{1,0:T(8,128)(2,1)S(1)}, bf16[32,4096]{1,0:T(8,128)(2,1)S(1)}, u32[]{:S(2)}, u32[]{:S(2)}) collective-permute-start(bf16[32,4096]{1,0:T(8,128)(2,1)S(1)} %pad_maximum_fusion.4), channel_id=1, source_target_pairs={{0,8},{1,9},{2,10},{3,11},{4,12},{5,13},{6,14},{7,15},{8,0},{9,1},... | collective-permute-start | bytes 786440 | tf_op jit(solution)/shard_map/ppermute | solution.py:111
  295.9 62.7 %collective-permute-start.2 = (bf16[64,4096]{1,0:T(8,128)(2,1)}, bf16[64,4096]{1,0:T(8,128)(2,1)}, u32[]{:S(2)}, u32[]{:S(2)}) collective-permute-start(bf16[64,4096]{1,0:T(8,128)(2,1)} %pad_maximum_fusion.1), channel_id=1, source_target_pairs={{0,2},{1,3},{2,0},{3,1},{4,6},{5,7},{6,4},{7,5},{8,10},{9,11},{10,... | collective-permute-start | bytes 1572872 | tf_op jit(solution)/shard_map/ppermute | solution.py:111
  352.2 83.5 %all-to-all-start.4 = ((bf16[32,2,16384]{2,1,0:T(2,128)(2,1)}), bf16[32,2,16384]{2,1,0:T(2,128)(2,1)S(1)}, u32[]{:S(2)}, u32[]{:S(2)}) async-start(bf16[32,2,16384]{2,1,0:T(2,128)(2,1)} %reshape.260), calls=%async_computation.4 | async-start | bytes 4194304 | tf_op jit(solution)/shard_map/all_to_all | solution.py:165
  359.8 69.2 %collective-permute-start.3 = (bf16[128,4096]{1,0:T(8,128)(2,1)S(1)}, bf16[128,4096]{1,0:T(8,128)(2,1)S(1)}, u32[]{:S(2)}, u32[]{:S(2)}) collective-permute-start(bf16[128,4096]{1,0:T(8,128)(2,1)S(1)} %pad_maximum_fusion), channel_id=1, source_target_pairs={{0,4},{1,5},{2,6},{3,7},{4,0},{5,1},{6,2},{7,3},{8,12},{9,13},{10,... | collective-permute-start | bytes 3145736 | tf_op jit(solution)/shard_map/ppermute | solution.py:111
  432.1 48.0 %collective-permute-start.4 = (bf16[256,4096]{1,0:T(8,128)(2,1)}, bf16[256,4096]{1,0:T(8,128)(2,1)}, u32[]{:S(2)}, u32[]{:S(2)}) collective-permute-start(bf16[256,4096]{1,0:T(8,128)(2,1)} %get-tuple-element.19), channel_id=1, source_target_pairs={{0,1},{1,0},{2,3},{3,2},{4,5},{5,4},{6,7},{7,6},{8,9},{9,8},{10,11... | collective-permute-start | bytes 6291464 | tf_op jit(solution)/shard_map/ppermute | solution.py:111
  447.9 35.3 %copy-start.13 = (bf16[1,32,128,256]{3,2,1,0:T(8,128)(2,1)S(1)}, bf16[1,32,128,256]{3,2,1,0:T(8,128)(2,1)}, u32[]{:S(2)}) copy-start(bf16[1,32,128,256]{3,2,1,0:T(8,128)(2,1)} %copy.86) | copy-start | bytes 6291460
  489.3 5.3 collective-permute-start.5
  494.8 6.8 %collective-permute-start.6 = (f32[132,256]{1,0:T(8,128)S(1)}, f32[132,256]{1,0:T(8,128)S(1)}, u32[]{:S(2)}, u32[]{:S(2)}) collective-permute-start(f32[132,256]{1,0:T(8,128)S(1)} %slice_select_fusion.1), channel_id=1, source_target_pairs={{0,128},{32,160},{64,192},{96,224},{128,0},{160,32},{192,64},{224,... | collective-permute-start | bytes 405512 | tf_op jit(solution)/shard_map/ppermute | solution.py:149
  501.6 35.7 %copy-start.7 = (f32[1,32,128,16]{2,1,3,0:T(8,128)S(1)}, f32[1,32,128,16]{2,1,3,0:T(8,128)}, u32[]{:S(2)}) copy-start(f32[1,32,128,16]{2,1,3,0:T(8,128)} %copy-done.6) | copy-start | bytes 786436
  501.6 35.7 %copy-start.9 = (f32[1,32,128,16]{2,1,3,0:T(8,128)S(1)}, f32[1,32,128,16]{2,1,3,0:T(8,128)}, u32[]{:S(2)}) copy-start(f32[1,32,128,16]{2,1,3,0:T(8,128)} %copy-done.8) | copy-start | bytes 786436
  501.6 6.9 %collective-permute-start.7 = (f32[66,256]{1,0:T(8,128)S(1)}, f32[66,256]{1,0:T(8,128)S(1)}, u32[]{:S(2)}, u32[]{:S(2)}) collective-permute-start(f32[66,256]{1,0:T(8,128)S(1)} %slice_select_fusion.2), channel_id=1, source_target_pairs={{0,256},{32,288},{64,320},{96,352},{128,384},{160,416},{192,448},{... | collective-permute-start | bytes 202760 | tf_op jit(solution)/shard_map/ppermute | solution.py:149
  508.6 40.2 %copy-start.5 = (f32[1,32,128,16]{2,1,3,0:T(8,128)S(1)}, f32[1,32,128,16]{2,1,3,0:T(8,128)}, u32[]{:S(2)}) copy-start(f32[1,32,128,16]{2,1,3,0:T(8,128)} %copy-done.4) | copy-start | bytes 786436
  508.6 40.2 %copy-start.12 = (f32[2,8,64,128]{3,1,2,0:T(8,128)S(1)}, f32[2,8,64,128]{3,1,2,0:T(8,128)}, u32[]{:S(2)}) copy-start(f32[2,8,64,128]{3,1,2,0:T(8,128)} %copy-done.11) | copy-start | bytes 1572868
  508.6 10.2 %collective-permute-start.8 = (f32[33,256]{1,0:T(8,128)S(1)}, f32[33,256]{1,0:T(8,128)S(1)}, u32[]{:S(2)}, u32[]{:S(2)}) collective-permute-start(f32[33,256]{1,0:T(8,128)S(1)} %slice_select_fusion.3), channel_id=1, source_target_pairs={{0,64},{32,96},{64,0},{96,32},{128,192},{160,224},{192,128},{224,1... | collective-permute-start | bytes 101384 | tf_op jit(solution)/shard_map/ppermute | solution.py:149
  518.9 8.7 %collective-permute-start.9 = (f32[33,256]{1,0:T(8,128)S(1)}, f32[33,256]{1,0:T(8,128)S(1)}, u32[]{:S(2)}, u32[]{:S(2)}) collective-permute-start(f32[33,256]{1,0:T(8,128)S(1)} %select_add_fusion.3), channel_id=1, source_target_pairs={{0,64},{32,96},{64,0},{96,32},{128,192},{160,224},{192,128},{224,1... | collective-permute-start | bytes 101384 | tf_op jit(solution)/shard_map/ppermute | solution.py:151
  527.5 6.6 %collective-permute-start.10 = (f32[66,256]{1,0:T(8,128)S(1)}, f32[66,256]{1,0:T(8,128)S(1)}, u32[]{:S(2)}, u32[]{:S(2)}) collective-permute-start(f32[66,256]{1,0:T(8,128)S(1)} %maximum_select_fusion.3), channel_id=1, source_target_pairs={{0,256},{32,288},{64,320},{96,352},{128,384},{160,416},{192,448},{... | collective-permute-start | bytes 202760 | tf_op jit(solution)/shard_map/ppermute | solution.py:151
  534.1 5.8 %collective-permute-start.11 = (f32[132,256]{1,0:T(8,128)S(1)}, f32[132,256]{1,0:T(8,128)S(1)}, u32[]{:S(2)}, u32[]{:S(2)}) collective-permute-start(f32[132,256]{1,0:T(8,128)S(1)} %maximum_select_fusion.2), channel_id=1, source_target_pairs={{0,128},{32,160},{64,192},{96,224},{128,0},{160,32},{192,64},{224,... | collective-permute-start | bytes 405512 | tf_op jit(solution)/shard_map/ppermute | solution.py:151
  540.0 10.0 %collective-permute-start.12 = (f32[264,256]{1,0:T(8,128)S(1)}, f32[264,256]{1,0:T(8,128)S(1)}, u32[]{:S(2)}, u32[]{:S(2)}) collective-permute-start(f32[264,256]{1,0:T(8,128)S(1)} %maximum_select_fusion.1), channel_id=1, source_target_pairs={{0,32},{32,0},{64,96},{96,64},{128,160},{160,128},{192,224},{224,1... | collective-permute-start | bytes 811016 | tf_op jit(solution)/shard_map/ppermute | solution.py:151
  (4 other events, 6.9 us)
Sparse Core Ops, SparseCore 0:
  10.1 205.1 all-gather.1

commit v2 on v1

--- a/solution.py
+++ b/solution.py
@@ -91,6 +91,14 @@
 def rounded_sum(terms):
     rounded = lax.optimization_barrier(terms.astype(jnp.bfloat16))
     return jnp.sum(rounded.astype(jnp.float32), axis=0)
+
+
+def columns_by_position(rows, block_width):
+    tok_rows = rows.shape[0]
+    blocks = rows.shape[1] // block_width
+    pieces = jnp.transpose(rows.reshape(tok_rows, blocks, block_width), (1, 0, 2))
+    moved = lax.all_to_all(pieces, "ctx", split_axis=0, concat_axis=0, tiled=True)
+    return moved.reshape(blocks * tok_rows, block_width)
 
 
 def axis_pairs(size, mask):
@@ -162,8 +170,9 @@
     channels = out_weight.shape[0]
     block_width = out_weight.shape[1]
     tok_rows = grad_out.shape[1]
-    grad_cols = lax.all_to_all(grad_out, "ctx", split_axis=2, concat_axis=1, tiled=True)
     shard_piece = lax.all_gather(out_weight, "ctx", axis=1, tiled=True)
+    grad_cols = columns_by_position(grad_out[0], block_width)
+    shard_piece, grad_cols = lax.optimization_barrier((shard_piece, grad_cols))
     blocks = shard_piece.shape[1] // block_width
     partial_value = grad_out[0]
     partial_value = partial_value.reshape(tok_rows, blocks, block_width)
@@ -212,7 +221,7 @@
     gathered = doubling_gather(gated_t, "ctx", gather_masks)
     partial_value = lax.dot_general(
         gathered,
-        grad_cols[0],
+        grad_cols,
         (((1,), (0,)), ((), ())),
         preferred_element_type=jnp.float32,
     )

time: 566 us -> 519 us (0.917)
  other arithmetic: 63.1 us -> 15.3 us
  local copies, waits for them, and re-layouts: 49.9 us -> 25.8 us
  waiting for transfers between devices: 295 us -> 310 us
  starting transfers between devices: 93 us -> 102 us
    all_to_all x1, waiting for transfers between devices: 0.01 us -> 79.6 us  [columns_by_position(): lax.all_to_all(pieces, 'ctx', split_axis=0, concat_axis=0, tiled=True)]
    unnamed x6 -> x5, other arithmetic: 51.7 us -> 6.45 us
    ppermute x5, waiting for transfers between devices: 114 us -> 75.9 us  [doubling_gather(): lax.ppermute(held, axis, axis_pairs(size, mask))]
    all_gather x1, waiting for transfers between devices: 139 us -> 108 us  [body(): shard_piece = lax.all_gather(out_weight, 'ctx', axis=1, tiled=True)]
    unnamed x65 -> x50, local copies, waits for them, and re-layouts: 37.9 us -> 14.3 us
    ppermute x4, starting transfers between devices: 21.5 us -> 32.8 us  [summed_over_dp(): held = keep + lax.ppermute(send, 'dp', axis_pairs(size, mask))]
  transfers between devices with their start and end apart: 19 -> 19, of which waited for: 17 -> 19; matrix products, arithmetic and copies ran while one was open for 18% -> 7% of each run, Pallas kernels for 0% -> 0%
where the time goes in v2:
time: 519 us; the launch traced here: 511 us
  waiting for transfers between devices  310 us (60%)
  starting transfers between devices  102 us (20%)
  matrix products  42.5 us (8%)
  local copies, waits for them, and re-layouts  25.8 us (5%)
  other arithmetic  15.3 us (3%)
  between operations  15.2 us (3%)
    all_gather x1, waiting for transfers between devices, body(): shard_piece = lax.all_gather(out_weight, 'ctx', axis=1, tiled=True)  108 us
    all_to_all x1, waiting for transfers between devices, columns_by_position(): lax.all_to_all(pieces, 'ctx', split_axis=0, concat_axis=0, tiled=True)  79.6 us
    ppermute x5, waiting for transfers between devices, doubling_gather(): lax.ppermute(held, axis, axis_pairs(size, mask))  75.9 us
    ppermute x4, starting transfers between devices, summed_over_dp(): held = keep + lax.ppermute(send, 'dp', axis_pairs(size, mask))  32.8 us
    ppermute x4, starting transfers between devices, summed_over_dp(): other = lax.ppermute(held, 'dp', axis_pairs(size, mask))  22.3 us
    dot_general x24, matrix products, single(): return jnp.einsum('ckm,mj->ckj', data, table, precision=HIGHEST)  21.6 us
    all_to_all x1, starting transfers between devices, body(): lax.all_to_all(queries, 'ctx', split_axis=2, concat_axis=1, tiled=True)  14.3 us
    unnamed x50, local copies, waits for them, and re-layouts  14.3 us
  transfers between devices with their start and end apart: 19, of which 19 were waited for; matrix products, arithmetic and copies ran while one was open for 7% of the time, Pallas kernels for 0%

profile of v2, /device:TPU:1, one launch (start us, length us, event | category | flops | bytes accessed | tf_op | source)
XLA Modules:
  0.0 510.6 jit_solution(14538432891788350819)
XLA Ops:
  11.6 14.3 %all-to-all-start.4 = ((bf16[32,2,1024]{2,1,0:T(2,128)(2,1)}), bf16[32,2,1024]{2,1,0:T(2,128)(2,1)S(1)}, u32[]{:S(2)}, u32[]{:S(2)}) async-start(bf16[32,2,1024]{2,1,0:T(2,128)(2,1)} %reshape.260), calls=%async_computation.4 | async-start | bytes 262144 | tf_op jit(solution)/shard_map/all_to_all | solution.py:186
  29.1 6.7 %all-to-all-done.4 = bf16[32,2,1024]{2,1,0:T(2,128)(2,1)S(1)} async-done(((bf16[32,2,1024]{2,1,0:T(2,128)(2,1)}), bf16[32,2,1024]{2,1,0:T(2,128)(2,1)S(1)}, u32[]{:S(2)}, u32[]{:S(2)}) %all-to-all-start.4) | async-done | bytes 131104 | tf_op jit(solution)/shard_map/all_to_all | solution.py:186
  35.8 3.9 all-to-all-start.2
  42.9 8.7 %all-to-all-done.2 = bf16[32,2,1024]{2,1,0:T(2,128)(2,1)S(1)} async-done(((bf16[32,2,1024]{2,1,0:T(2,128)(2,1)}), bf16[32,2,1024]{2,1,0:T(2,128)(2,1)S(1)}, u32[]{:S(2)}, u32[]{:S(2)}) %all-to-all-start.2) | async-done | bytes 131104 | tf_op jit(solution)/shard_map/all_to_all | solution.py:187
  51.6 3.9 all-to-all-start.3
  55.5 2.5 copy.81
  58.0 9.1 %all-to-all-done.3 = bf16[32,2,1024]{2,1,0:T(2,128)(2,1)S(1)} async-done(((bf16[32,2,1024]{2,1,0:T(2,128)(2,1)}), bf16[32,2,1024]{2,1,0:T(2,128)(2,1)S(1)}, u32[]{:S(2)}, u32[]{:S(2)}) %all-to-all-start.3) | async-done | bytes 131104 | tf_op jit(solution)/shard_map/all_to_all | solution.py:188
  67.1 4.9 all-to-all-start
  79.3 79.6 %all-to-all-done = bf16[32,128,256]{1,2,0:T(8,128)(2,1)S(1)} async-done(((bf16[32,128,256]{1,2,0:T(8,128)(2,1)}), bf16[32,128,256]{1,2,0:T(8,128)(2,1)S(1)}, u32[]{:S(2)}, u32[]{:S(2)}) %all-to-all-start) | async-done | bytes 2097184 | tf_op jit(solution)/shard_map/all_to_all | solution.py:100
  158.9 3.0 copy.82
  161.9 107.8 %all-gather.2.cloned.1.call-done = bf16[512,8192]{1,0:T(8,128)(2,1)} async-done(((bf16[512,256]{1,0:T(8,128)(2,1)}), bf16[512,8192]{1,0:T(8,128)(2,1)}) %all-gather.2.cloned.1.call-update) | async-done | bytes 8388624 | tf_op jit(solution)/shard_map/all_gather | solution.py:173
  269.7 8.3 %convert_bitcast_fusion = bf16[32,128,512]{1,2,0:T(8,128)(2,1)} fusion(bf16[128,32,256]{0,2,1:T(8,128)(2,1)} %bitcast, bf16[64,32,8,256]{3,2,1,0:T(8,128)(2,1)} %bitcast.324), kind=kOutput, calls=%fused_computation.8 | convolution fusion | flops 1075838976 | bytes 14680064 | tf_op jit(solution)/shard_map/tks,cks->ktc/dot_general | solution.py:180
  278.0 2.9 reduce_sum.39
  283.2 9.5 %all-to-all-start.1 = ((bf16[32,2,1024]{2,1,0:T(2,128)(2,1)}), bf16[32,2,1024]{2,1,0:T(2,128)(2,1)S(1)}, u32[]{:S(2)}, u32[]{:S(2)}) async-start(bf16[32,2,1024]{2,1,0:T(2,128)(2,1)} %reshape.262), calls=%async_computation.1 | async-start | bytes 262144 | tf_op jit(solution)/shard_map/all_to_all | solution.py:189
  293.6 9.0 %all-to-all-done.1 = bf16[32,2,1024]{2,1,0:T(2,128)(2,1)S(1)} async-done(((bf16[32,2,1024]{2,1,0:T(2,128)(2,1)}), bf16[32,2,1024]{2,1,0:T(2,128)(2,1)S(1)}, u32[]{:S(2)}, u32[]{:S(2)}) %all-to-all-start.1) | async-done | bytes 131104 | tf_op jit(solution)/shard_map/all_to_all | solution.py:189
  329.5 7.5 %collective-permute-done = bf16[16,4096]{1,0:T(8,128)(2,1)S(1)} collective-permute-done((bf16[16,4096]{1,0:T(8,128)(2,1)S(1)}, bf16[16,4096]{1,0:T(8,128)(2,1)S(1)}, u32[]{:S(2)}, u32[]{:S(2)}) %collective-permute-start) | collective-permute-done | bytes 131104 | tf_op jit(solution)/shard_map/ppermute | solution.py:119
  339.1 11.6 %collective-permute-done.1 = bf16[32,4096]{1,0:T(8,128)(2,1)S(1)} collective-permute-done((bf16[32,4096]{1,0:T(8,128)(2,1)S(1)}, bf16[32,4096]{1,0:T(8,128)(2,1)S(1)}, u32[]{:S(2)}, u32[]{:S(2)}) %collective-permute-start.1) | collective-permute-done | bytes 262176 | tf_op jit(solution)/shard_map/ppermute | solution.py:119
  353.6 13.0 %collective-permute-done.2 = bf16[64,4096]{1,0:T(8,128)(2,1)S(1)} collective-permute-done((bf16[64,4096]{1,0:T(8,128)(2,1)S(1)}, bf16[64,4096]{1,0:T(8,128)(2,1)S(1)}, u32[]{:S(2)}, u32[]{:S(2)}) %collective-permute-start.2) | collective-permute-done | bytes 524320 | tf_op jit(solution)/shard_map/ppermute | solution.py:119
  371.4 10.8 %collective-permute-done.3 = bf16[128,4096]{1,0:T(8,128)(2,1)S(1)} collective-permute-done((bf16[128,4096]{1,0:T(8,128)(2,1)S(1)}, bf16[128,4096]{1,0:T(8,128)(2,1)S(1)}, u32[]{:S(2)}, u32[]{:S(2)}) %collective-permute-start.3) | collective-permute-done | bytes 1048608 | tf_op jit(solution)/shard_map/ppermute | solution.py:119
  386.2 32.9 %collective-permute-done.4 = bf16[256,4096]{1,0:T(8,128)(2,1)} collective-permute-done((bf16[256,4096]{1,0:T(8,128)(2,1)}, bf16[256,4096]{1,0:T(8,128)(2,1)}, u32[]{:S(2)}, u32[]{:S(2)}) %collective-permute-start.4) | collective-permute-done | bytes 2097184 | tf_op jit(solution)/shard_map/ppermute | solution.py:119
  419.1 3.1 constant_dynamic-update-slice_fusion.5
  422.3 3.5 fusion.327
  426.6 16.8 %collective-permute-start.5 = (f32[264,256]{1,0:T(8,128)S(1)}, f32[264,256]{1,0:T(8,128)S(1)}, u32[]{:S(2)}, u32[]{:S(2)}) collective-permute-start(f32[264,256]{1,0:T(8,128)S(1)} %slice_select_fusion), channel_id=1, source_target_pairs={{0,32},{32,0},{64,96},{96,64},{128,160},{160,128},{192,224},{224,1... | collective-permute-start | bytes 811016 | tf_op jit(solution)/shard_map/ppermute | solution.py:157
  447.5 4.0 collective-permute-done.6
  451.5 3.3 collective-permute-start.7
  455.7 2.6 collective-permute-done.7
  458.3 10.8 %collective-permute-start.8 = (f32[33,256]{1,0:T(8,128)S(1)}, f32[33,256]{1,0:T(8,128)S(1)}, u32[]{:S(2)}, u32[]{:S(2)}) collective-permute-start(f32[33,256]{1,0:T(8,128)S(1)} %slice_select_fusion.3), channel_id=1, source_target_pairs={{0,64},{32,96},{64,0},{96,32},{128,192},{160,224},{192,128},{224,1... | collective-permute-start | bytes 101384 | tf_op jit(solution)/shard_map/ppermute | solution.py:157
  470.5 7.3 %collective-permute-start.9 = (f32[33,256]{1,0:T(8,128)S(1)}, f32[33,256]{1,0:T(8,128)S(1)}, u32[]{:S(2)}, u32[]{:S(2)}) collective-permute-start(f32[33,256]{1,0:T(8,128)S(1)} %select_add_fusion.3), channel_id=1, source_target_pairs={{0,64},{32,96},{64,0},{96,32},{128,192},{160,224},{192,128},{224,1... | collective-permute-start | bytes 101384 | tf_op jit(solution)/shard_map/ppermute | solution.py:159
  479.2 4.8 collective-permute-start.10
  485.8 2.5 collective-permute-start.11
  489.4 3.0 collective-permute-done.11
  492.4 7.7 %collective-permute-start.12 = (f32[264,256]{1,0:T(8,128)S(1)}, f32[264,256]{1,0:T(8,128)S(1)}, u32[]{:S(2)}, u32[]{:S(2)}) collective-permute-start(f32[264,256]{1,0:T(8,128)S(1)} %maximum_select_fusion.1), channel_id=1, source_target_pairs={{0,32},{32,0},{64,96},{96,64},{128,160},{160,128},{192,224},{224,1... | collective-permute-start | bytes 811016 | tf_op jit(solution)/shard_map/ppermute | solution.py:159
  (158 shorter events, 76.1 us)
Async XLA Ops:
  7.2 48.3 %copy-start.7 = (bf16[1,128,8192]{2,1,0:T(8,128)(2,1)S(1)}, bf16[1,128,8192]{2,1,0:T(8,128)(2,1)}, u32[]{:S(2)}) copy-start(bf16[1,128,8192]{2,1,0:T(8,128)(2,1)} %param.10) | copy-start | bytes 6291460
  7.2 262.5 %all-gather.2.cloned.1.call-start = ((), (), s32[]{:S(2)}) async-start(), calls=%async_computation.5 | async-start | bytes 8650752 | tf_op jit(solution)/shard_map/all_gather | solution.py:173
  11.6 24.2 %all-to-all-start.4 = ((bf16[32,2,1024]{2,1,0:T(2,128)(2,1)}), bf16[32,2,1024]{2,1,0:T(2,128)(2,1)S(1)}, u32[]{:S(2)}, u32[]{:S(2)}) async-start(bf16[32,2,1024]{2,1,0:T(2,128)(2,1)} %reshape.260), calls=%async_computation.4 | async-start | bytes 262144 | tf_op jit(solution)/shard_map/all_to_all | solution.py:186
  35.8 15.8 %all-to-all-start.2 = ((bf16[32,2,1024]{2,1,0:T(2,128)(2,1)}), bf16[32,2,1024]{2,1,0:T(2,128)(2,1)S(1)}, u32[]{:S(2)}, u32[]{:S(2)}) async-start(bf16[32,2,1024]{2,1,0:T(2,128)(2,1)} %reshape.258), calls=%async_computation.2 | async-start | bytes 262144 | tf_op jit(solution)/shard_map/all_to_all | solution.py:187
  51.6 15.4 %all-to-all-start.3 = ((bf16[32,2,1024]{2,1,0:T(2,128)(2,1)}), bf16[32,2,1024]{2,1,0:T(2,128)(2,1)S(1)}, u32[]{:S(2)}, u32[]{:S(2)}) async-start(bf16[32,2,1024]{2,1,0:T(2,128)(2,1)} %reshape.256), calls=%async_computation.3 | async-start | bytes 262144 | tf_op jit(solution)/shard_map/all_to_all | solution.py:188
  55.5 16.5 %copy-start.11 = (f32[16,16]{1,0:T(8,128)S(1)}, f32[16,16]{1,0:T(8,128)}, u32[]{:S(2)}) copy-start(f32[16,16]{1,0:T(8,128)} %param.13) | copy-start | bytes 3076
  67.1 91.9 %all-to-all-start = ((bf16[32,128,256]{1,2,0:T(8,128)(2,1)}), bf16[32,128,256]{1,2,0:T(8,128)(2,1)S(1)}, u32[]{:S(2)}, u32[]{:S(2)}) async-start(bf16[32,128,256]{1,2,0:T(8,128)(2,1)} %bitcast.1), calls=%async_computation | async-start | bytes 4194304 | tf_op jit(solution)/shard_map/all_to_all | solution.py:100
  72.8 0.7 copy-start.3
  73.1 0.7 copy-start.5
  278.0 14.7 %copy-start.9 = (f32[16,64,128]{2,1,0:T(8,128)S(1)}, f32[16,64,128]{2,1,0:T(8,128)}, u32[]{:S(2)}) copy-start(f32[16,64,128]{2,1,0:T(8,128)} %fusion.52) | copy-start | bytes 1572868
  283.2 19.4 %all-to-all-start.1 = ((bf16[32,2,1024]{2,1,0:T(2,128)(2,1)}), bf16[32,2,1024]{2,1,0:T(2,128)(2,1)S(1)}, u32[]{:S(2)}, u32[]{:S(2)}) async-start(bf16[32,2,1024]{2,1,0:T(2,128)(2,1)} %reshape.262), calls=%async_computation.1 | async-start | bytes 262144 | tf_op jit(solution)/shard_map/all_to_all | solution.py:189
  293.6 13.7 %copy-start.1 = (f32[16,64,128]{2,1,0:T(8,128)}, f32[16,64,128]{2,1,0:T(8,128)S(1)}, u32[]{:S(2)}) copy-start(f32[16,64,128]{2,1,0:T(8,128)S(1)} %convolution_subtract_fusion.5) | copy-start | bytes 1572868
  303.1 4.1 copy-start
  309.9 3.6 copy-start.10
  316.0 4.1 copy-start.2
  327.2 9.8 %collective-permute-start = (bf16[16,4096]{1,0:T(8,128)(2,1)S(1)}, bf16[16,4096]{1,0:T(8,128)(2,1)S(1)}, u32[]{:S(2)}, u32[]{:S(2)}) collective-permute-start(bf16[16,4096]{1,0:T(8,128)(2,1)S(1)} %get-tuple-element.16), channel_id=1, source_target_pairs={{0,16},{1,17},{2,18},{3,19},{4,20},{5,21},{6,22},{7,23},{8,24},{9,... | collective-permute-start | bytes 393224 | tf_op jit(solution)/shard_map/ppermute | solution.py:119
  337.1 13.6 %collective-permute-start.1 = (bf16[32,4096]{1,0:T(8,128)(2,1)S(1)}, bf16[32,4096]{1,0:T(8,128)(2,1)S(1)}, u32[]{:S(2)}, u32[]{:S(2)}) collective-permute-start(bf16[32,4096]{1,0:T(8,128)(2,1)S(1)} %pad_maximum_fusion.4), channel_id=1, source_target_pairs={{0,8},{1,9},{2,10},{3,11},{4,12},{5,13},{6,14},{7,15},{8,0},{9,1},... | collective-permute-start | bytes 786440 | tf_op jit(solution)/shard_map/ppermute | solution.py:119
  350.8 15.8 %collective-permute-start.2 = (bf16[64,4096]{1,0:T(8,128)(2,1)S(1)}, bf16[64,4096]{1,0:T(8,128)(2,1)S(1)}, u32[]{:S(2)}, u32[]{:S(2)}) collective-permute-start(bf16[64,4096]{1,0:T(8,128)(2,1)S(1)} %pad_maximum_fusion.1), channel_id=1, source_target_pairs={{0,2},{1,3},{2,0},{3,1},{4,6},{5,7},{6,4},{7,5},{8,10},{9,11},{10,... | collective-permute-start | bytes 1572872 | tf_op jit(solution)/shard_map/ppermute | solution.py:119
  366.7 15.5 %collective-permute-start.3 = (bf16[128,4096]{1,0:T(8,128)(2,1)S(1)}, bf16[128,4096]{1,0:T(8,128)(2,1)S(1)}, u32[]{:S(2)}, u32[]{:S(2)}) collective-permute-start(bf16[128,4096]{1,0:T(8,128)(2,1)S(1)} %pad_maximum_fusion), channel_id=1, source_target_pairs={{0,4},{1,5},{2,6},{3,7},{4,0},{5,1},{6,2},{7,3},{8,12},{9,13},{10,... | collective-permute-start | bytes 3145736 | tf_op jit(solution)/shard_map/ppermute | solution.py:119
  383.8 35.3 %collective-permute-start.4 = (bf16[256,4096]{1,0:T(8,128)(2,1)}, bf16[256,4096]{1,0:T(8,128)(2,1)}, u32[]{:S(2)}, u32[]{:S(2)}) collective-permute-start(bf16[256,4096]{1,0:T(8,128)(2,1)} %get-tuple-element.23), channel_id=1, source_target_pairs={{0,1},{1,0},{2,3},{3,2},{4,5},{5,4},{6,7},{7,6},{8,9},{9,8},{10,11... | collective-permute-start | bytes 6291464 | tf_op jit(solution)/shard_map/ppermute | solution.py:119
  386.2 36.1 %copy-start.8 = (bf16[32,128,256]{2,1,0:T(8,128)(2,1)S(1)}, bf16[32,128,256]{2,1,0:T(8,128)(2,1)}, u32[]{:S(2)}) copy-start(bf16[32,128,256]{2,1,0:T(8,128)(2,1)} %copy.82) | copy-start | bytes 6291460
  426.6 18.0 %collective-permute-start.5 = (f32[264,256]{1,0:T(8,128)S(1)}, f32[264,256]{1,0:T(8,128)S(1)}, u32[]{:S(2)}, u32[]{:S(2)}) collective-permute-start(f32[264,256]{1,0:T(8,128)S(1)} %slice_select_fusion), channel_id=1, source_target_pairs={{0,32},{32,0},{64,96},{96,64},{128,160},{160,128},{192,224},{224,1... | collective-permute-start | bytes 811016 | tf_op jit(solution)/shard_map/ppermute | solution.py:157
  444.7 6.8 %collective-permute-start.6 = (f32[132,256]{1,0:T(8,128)S(1)}, f32[132,256]{1,0:T(8,128)S(1)}, u32[]{:S(2)}, u32[]{:S(2)}) collective-permute-start(f32[132,256]{1,0:T(8,128)S(1)} %slice_select_fusion.1), channel_id=1, source_target_pairs={{0,128},{32,160},{64,192},{96,224},{128,0},{160,32},{192,64},{224,... | collective-permute-start | bytes 405512 | tf_op jit(solution)/shard_map/ppermute | solution.py:157
  451.5 36.8 %copy-start.4 = (f32[1,32,128,16]{2,1,3,0:T(8,128)S(1)}, f32[1,32,128,16]{2,1,3,0:T(8,128)}, u32[]{:S(2)}) copy-start(f32[1,32,128,16]{2,1,3,0:T(8,128)} %copy-done.3) | copy-start | bytes 786436
  451.5 36.8 %copy-start.6 = (f32[1,32,128,16]{2,1,3,0:T(8,128)S(1)}, f32[1,32,128,16]{2,1,3,0:T(8,128)}, u32[]{:S(2)}) copy-start(f32[1,32,128,16]{2,1,3,0:T(8,128)} %copy-done.5) | copy-start | bytes 786436
  451.5 6.7 %collective-permute-start.7 = (f32[66,256]{1,0:T(8,128)S(1)}, f32[66,256]{1,0:T(8,128)S(1)}, u32[]{:S(2)}, u32[]{:S(2)}) collective-permute-start(f32[66,256]{1,0:T(8,128)S(1)} %slice_select_fusion.2), channel_id=1, source_target_pairs={{0,256},{32,288},{64,320},{96,352},{128,384},{160,416},{192,448},{... | collective-permute-start | bytes 202760 | tf_op jit(solution)/shard_map/ppermute | solution.py:157
  458.3 12.1 %collective-permute-start.8 = (f32[33,256]{1,0:T(8,128)S(1)}, f32[33,256]{1,0:T(8,128)S(1)}, u32[]{:S(2)}, u32[]{:S(2)}) collective-permute-start(f32[33,256]{1,0:T(8,128)S(1)} %slice_select_fusion.3), channel_id=1, source_target_pairs={{0,64},{32,96},{64,0},{96,32},{128,192},{160,224},{192,128},{224,1... | collective-permute-start | bytes 101384 | tf_op jit(solution)/shard_map/ppermute | solution.py:157
  470.5 8.7 %collective-permute-start.9 = (f32[33,256]{1,0:T(8,128)S(1)}, f32[33,256]{1,0:T(8,128)S(1)}, u32[]{:S(2)}, u32[]{:S(2)}) collective-permute-start(f32[33,256]{1,0:T(8,128)S(1)} %select_add_fusion.3), channel_id=1, source_target_pairs={{0,64},{32,96},{64,0},{96,32},{128,192},{160,224},{192,128},{224,1... | collective-permute-start | bytes 101384 | tf_op jit(solution)/shard_map/ppermute | solution.py:159
  479.2 6.6 %collective-permute-start.10 = (f32[66,256]{1,0:T(8,128)S(1)}, f32[66,256]{1,0:T(8,128)S(1)}, u32[]{:S(2)}, u32[]{:S(2)}) collective-permute-start(f32[66,256]{1,0:T(8,128)S(1)} %maximum_select_fusion.3), channel_id=1, source_target_pairs={{0,256},{32,288},{64,320},{96,352},{128,384},{160,416},{192,448},{... | collective-permute-start | bytes 202760 | tf_op jit(solution)/shard_map/ppermute | solution.py:159
  485.8 6.6 %collective-permute-start.11 = (f32[132,256]{1,0:T(8,128)S(1)}, f32[132,256]{1,0:T(8,128)S(1)}, u32[]{:S(2)}, u32[]{:S(2)}) collective-permute-start(f32[132,256]{1,0:T(8,128)S(1)} %maximum_select_fusion.2), channel_id=1, source_target_pairs={{0,128},{32,160},{64,192},{96,224},{128,0},{160,32},{192,64},{224,... | collective-permute-start | bytes 405512 | tf_op jit(solution)/shard_map/ppermute | solution.py:159
  492.4 8.8 %collective-permute-start.12 = (f32[264,256]{1,0:T(8,128)S(1)}, f32[264,256]{1,0:T(8,128)S(1)}, u32[]{:S(2)}, u32[]{:S(2)}) collective-permute-start(f32[264,256]{1,0:T(8,128)S(1)} %maximum_select_fusion.1), channel_id=1, source_target_pairs={{0,32},{32,0},{64,96},{96,64},{128,160},{160,128},{192,224},{224,1... | collective-permute-start | bytes 811016 | tf_op jit(solution)/shard_map/ppermute | solution.py:159
Sparse Core Ops, SparseCore 0:
  10.0 259.6 all-gather.1

commit v3 on v2

--- a/solution.py
+++ b/solution.py
@@ -99,6 +99,32 @@
     pieces = jnp.transpose(rows.reshape(tok_rows, blocks, block_width), (1, 0, 2))
     moved = lax.all_to_all(pieces, "ctx", split_axis=0, concat_axis=0, tiled=True)
     return moved.reshape(blocks * tok_rows, block_width)
+
+
+def shared_weight(out_weight, masks):
+    channels, width = out_weight.shape
+    half = width // 2
+    core = lax.axis_index("dp") % 2
+    piece = lax.dynamic_slice_in_dim(out_weight, core * half, half, axis=1)
+    held = doubling_gather(piece, "ctx", masks)
+    held = held.reshape(-1, channels, half)
+    other = lax.ppermute(held, "dp", axis_pairs(lax.axis_size("dp"), 1))
+    return jnp.concatenate([held, other], axis=2)
+
+
+def matching_columns(rows, blocks, masks):
+    tok_rows = rows.shape[0]
+    half = rows.shape[1] // (2 * blocks)
+    me = lax.axis_index("ctx")
+    core = lax.axis_index("dp") % 2
+    place = jnp.arange(blocks, dtype=jnp.int32)
+    source = jnp.zeros_like(place)
+    for step, mask in enumerate(masks):
+        source = source | jnp.where(((place >> step) & 1) != 0, mask, 0)
+    source = me ^ source
+    index = (source[:, None] * 2 + (jnp.arange(2, dtype=jnp.int32)[None, :] ^ core)).reshape(-1)
+    halves = jnp.take(rows.reshape(tok_rows, 2 * blocks, half), index, axis=1)
+    return halves.reshape(tok_rows, blocks, 2 * half)
 
 
 def axis_pairs(size, mask):
@@ -170,15 +196,15 @@
     channels = out_weight.shape[0]
     block_width = out_weight.shape[1]
     tok_rows = grad_out.shape[1]
-    shard_piece = lax.all_gather(out_weight, "ctx", axis=1, tiled=True)
+    ctx_size = lax.axis_size("ctx")
+    gather_masks = ctx_masks(ctx_size)
+    weight_part = shared_weight(out_weight, gather_masks)
     grad_cols = columns_by_position(grad_out[0], block_width)
-    shard_piece, grad_cols = lax.optimization_barrier((shard_piece, grad_cols))
-    blocks = shard_piece.shape[1] // block_width
-    partial_value = grad_out[0]
-    partial_value = partial_value.reshape(tok_rows, blocks, block_width)
-    weight_part = shard_piece.reshape(channels, blocks, block_width)
+    weight_part, grad_cols = lax.optimization_barrier((weight_part, grad_cols))
+    blocks = weight_part.shape[0]
+    partial_value = matching_columns(grad_out[0], blocks, gather_masks)
     terms = jnp.einsum(
-        "tks,cks->ktc", partial_value, weight_part, preferred_element_type=jnp.float32
+        "tks,kcs->ktc", partial_value, weight_part, preferred_element_type=jnp.float32
     )
     gated_sum = rounded_sum(terms)
     grad_gated = gated_sum.astype(jnp.bfloat16)[None]
@@ -216,8 +242,6 @@
     grad_queries = (grad_gated_full * conv_out).T.astype(jnp.bfloat16)[None]
     grad_keys = (grad_product * value_full).T.astype(jnp.bfloat16)[None]
     grad_values = (grad_product * key_full).T.astype(jnp.bfloat16)[None]
-    ctx_size = lax.axis_size("ctx")
-    gather_masks = ctx_masks(ctx_size)
     gathered = doubling_gather(gated_t, "ctx", gather_masks)
     partial_value = lax.dot_general(
         gathered,

time: 519 us -> 517 us (level)
  waiting for transfers between devices: 310 us -> 266 us
  starting transfers between devices: 102 us -> 126 us
  local copies, waits for them, and re-layouts: 25.8 us -> 46.4 us
  between operations: 15.2 us -> 2.05 us
  other arithmetic: 15.3 us -> 27 us
    all_gather x1 -> x0, waiting for transfers between devices: 108 us -> none  [body(): shard_piece = lax.all_gather(out_weight, 'ctx', axis=1, tiled=True)]
    ppermute x5 -> x10, waiting for transfers between devices: 75.9 us -> 170 us  [doubling_gather(): lax.ppermute(held, axis, axis_pairs(size, mask))]
    all_to_all x1, waiting for transfers between devices: 79.6 us -> 31.2 us  [columns_by_position(): lax.all_to_all(pieces, 'ctx', split_axis=0, concat_axis=0, tiled=True)]
    all_to_all x1, waiting for transfers between devices: 6.74 us -> 39.3 us  [body(): lax.all_to_all(queries, 'ctx', split_axis=2, concat_axis=1, tiled=True)]
    ppermute x5 -> x10, starting transfers between devices: 10.5 us -> 40.3 us  [doubling_gather(): lax.ppermute(held, axis, axis_pairs(size, mask))]
    ppermute x4, starting transfers between devices: 32.8 us -> 23.2 us  [summed_over_dp(): held = keep + lax.ppermute(send, 'dp', axis_pairs(size, mask))]
    all_to_all x1, waiting for transfers between devices: 9.06 us -> 0.01 us  [body(): lax.all_to_all(values, 'ctx', split_axis=2, concat_axis=1, tiled=True)]
    concatenate x0 -> x1, other arithmetic: none -> 7.81 us  [shared_weight(): return jnp.concatenate([held, other], axis=2)]
  transfers between devices with their start and end apart: 19 -> 24, of which waited for: 19 -> 21; matrix products, arithmetic and copies ran while one was open for 7% -> 10% of each run, Pallas kernels for 0% -> 0%
where the time goes in v3:
time: 517 us; the launch traced here: 510 us
  waiting for transfers between devices  266 us (51%)
  starting transfers between devices  126 us (24%)
  local copies, waits for them, and re-layouts  46.4 us (9%)
  matrix products  42.4 us (8%)
  other arithmetic  27 us (5%)
    ppermute x10, waiting for transfers between devices, doubling_gather(): lax.ppermute(held, axis, axis_pairs(size, mask))  170 us
    ppermute x10, starting transfers between devices, doubling_gather(): lax.ppermute(held, axis, axis_pairs(size, mask))  40.3 us
    all_to_all x1, waiting for transfers between devices, body(): lax.all_to_all(queries, 'ctx', split_axis=2, concat_axis=1, tiled=True)  39.3 us
    all_to_all x1, waiting for transfers between devices, columns_by_position(): lax.all_to_all(pieces, 'ctx', split_axis=0, concat_axis=0, tiled=True)  31.2 us
    ppermute x4, starting transfers between devices, summed_over_dp(): held = keep + lax.ppermute(send, 'dp', axis_pairs(size, mask))  23.2 us
    ppermute x4, starting transfers between devices, summed_over_dp(): other = lax.ppermute(held, 'dp', axis_pairs(size, mask))  23.1 us
    dot_general x24, matrix products, single(): return jnp.einsum('ckm,mj->ckj', data, table, precision=HIGHEST)  21.6 us
    unnamed x70, local copies, waits for them, and re-layouts  19.2 us
  transfers between devices with their start and end apart: 24, of which 21 were waited for; matrix products, arithmetic and copies ran while one was open for 10% of the time, Pallas kernels for 0%

profile of v3, /device:TPU:1, one launch (start us, length us, event | category | flops | bytes accessed | tf_op | source)
XLA Modules:
  0.0 510.0 jit_solution(7493790573678561820)
XLA Ops:
  2.2 11.4 %collective-permute-start = (bf16[512,128]{1,0:T(8,128)(2,1)S(1)}, bf16[512,128]{1,0:T(8,128)(2,1)S(1)}, u32[]{:S(2)}, u32[]{:S(2)}) collective-permute-start(bf16[512,128]{1,0:T(8,128)(2,1)S(1)} %get-tuple-element.18), channel_id=1, source_target_pairs={{0,16},{1,17},{2,18},{3,19},{4,20},{5,21},{6,22},{7,23},{8,24},{9,... | collective-permute-start | bytes 393224 | tf_op jit(solution)/shard_map/ppermute | solution.py:145
  13.7 3.9 collective-permute-done
  17.6 6.9 %collective-permute-start.1 = (bf16[1024,128]{1,0:T(8,128)(2,1)S(1)}, bf16[1024,128]{1,0:T(8,128)(2,1)S(1)}, u32[]{:S(2)}, u32[]{:S(2)}) collective-permute-start(bf16[1024,128]{1,0:T(8,128)(2,1)S(1)} %pad_maximum_fusion.7), channel_id=1, source_target_pairs={{0,8},{1,9},{2,10},{3,11},{4,12},{5,13},{6,14},{7,15},{8,0},{9,1},... | collective-permute-start | bytes 786440 | tf_op jit(solution)/shard_map/ppermute | solution.py:145
  24.5 12.0 %collective-permute-done.1 = bf16[1024,128]{1,0:T(8,128)(2,1)S(1)} collective-permute-done((bf16[1024,128]{1,0:T(8,128)(2,1)S(1)}, bf16[1024,128]{1,0:T(8,128)(2,1)S(1)}, u32[]{:S(2)}, u32[]{:S(2)}) %collective-permute-start.1) | collective-permute-done | bytes 262176 | tf_op jit(solution)/shard_map/ppermute | solution.py:145
  36.5 4.2 collective-permute-start.2
  40.7 22.6 %collective-permute-done.2 = bf16[2048,128]{1,0:T(8,128)(2,1)S(1)} collective-permute-done((bf16[2048,128]{1,0:T(8,128)(2,1)S(1)}, bf16[2048,128]{1,0:T(8,128)(2,1)S(1)}, u32[]{:S(2)}, u32[]{:S(2)}) %collective-permute-start.2) | collective-permute-done | bytes 524320 | tf_op jit(solution)/shard_map/ppermute | solution.py:145
  68.7 19.8 %collective-permute-done.3 = bf16[4096,128]{1,0:T(8,128)(2,1)S(1)} collective-permute-done((bf16[4096,128]{1,0:T(8,128)(2,1)S(1)}, bf16[4096,128]{1,0:T(8,128)(2,1)S(1)}, u32[]{:S(2)}, u32[]{:S(2)}) %collective-permute-start.3) | collective-permute-done | bytes 1048608 | tf_op jit(solution)/shard_map/ppermute | solution.py:145
  90.0 4.4 collective-permute-start.4
  97.3 6.6 %all-to-all-start.4 = ((bf16[32,2,1024]{2,1,0:T(2,128)(2,1)}), bf16[32,2,1024]{2,1,0:T(2,128)(2,1)S(1)}, u32[]{:S(2)}, u32[]{:S(2)}) async-start(bf16[32,2,1024]{2,1,0:T(2,128)(2,1)} %reshape.350), calls=%async_computation.4 | async-start | bytes 262144 | tf_op jit(solution)/shard_map/all_to_all | solution.py:212
  106.2 39.3 %all-to-all-done.4 = bf16[32,2,1024]{2,1,0:T(2,128)(2,1)S(1)} async-done(((bf16[32,2,1024]{2,1,0:T(2,128)(2,1)}), bf16[32,2,1024]{2,1,0:T(2,128)(2,1)S(1)}, u32[]{:S(2)}, u32[]{:S(2)}) %all-to-all-start.4) | async-done | bytes 131104 | tf_op jit(solution)/shard_map/all_to_all | solution.py:212
  145.5 5.7 %all-to-all-start.2 = ((bf16[32,2,1024]{2,1,0:T(2,128)(2,1)}), bf16[32,2,1024]{2,1,0:T(2,128)(2,1)S(1)}, u32[]{:S(2)}, u32[]{:S(2)}) async-start(bf16[32,2,1024]{2,1,0:T(2,128)(2,1)} %reshape.348), calls=%async_computation.2 | async-start | bytes 262144 | tf_op jit(solution)/shard_map/all_to_all | solution.py:213
  153.8 7.3 %all-to-all-done.2 = bf16[32,2,1024]{2,1,0:T(2,128)(2,1)S(1)} async-done(((bf16[32,2,1024]{2,1,0:T(2,128)(2,1)}), bf16[32,2,1024]{2,1,0:T(2,128)(2,1)S(1)}, u32[]{:S(2)}, u32[]{:S(2)}) %all-to-all-start.2) | async-done | bytes 131104 | tf_op jit(solution)/shard_map/all_to_all | solution.py:213
  169.5 6.0 %collective-permute-start.5 = (bf16[32,512,128]{2,1,0:T(8,128)(2,1)}, bf16[32,512,128]{2,1,0:T(8,128)(2,1)}, u32[]{:S(2)}, u32[]{:S(2)}) collective-permute-start(bf16[32,512,128]{2,1,0:T(8,128)(2,1)} %bitcast.4), channel_id=1, source_target_pairs={{0,32},{32,0},{64,96},{96,64},{128,160},{160,128},{192,224},{224,1... | collective-permute-start | bytes 12582920 | tf_op jit(solution)/shard_map/ppermute | solution.py:111
  178.0 10.1 %all-to-all-start = ((bf16[32,128,256]{1,2,0:T(8,128)(2,1)}), bf16[32,128,256]{1,2,0:T(8,128)(2,1)}, u32[]{:S(2)}, u32[]{:S(2)}) async-start(bf16[32,128,256]{1,2,0:T(8,128)(2,1)} %bitcast.6), calls=%async_computation | async-start | bytes 4194304 | tf_op jit(solution)/shard_map/all_to_all | solution.py:100
  194.2 4.1 copy.74
  209.2 31.2 %all-to-all-done = bf16[32,128,256]{1,2,0:T(8,128)(2,1)} async-done(((bf16[32,128,256]{1,2,0:T(8,128)(2,1)}), bf16[32,128,256]{1,2,0:T(8,128)(2,1)}, u32[]{:S(2)}, u32[]{:S(2)}) %all-to-all-start) | async-done | bytes 2097184 | tf_op jit(solution)/shard_map/all_to_all | solution.py:100
  240.4 4.1 copy.76
  244.5 7.8 %pad_maximum_fusion = bf16[32,512,256]{2,1,0:T(8,128)(2,1)} fusion(bf16[32,512,128]{2,1,0:T(8,128)(2,1)} %collective-permute-done.5, bf16[32,512,128]{2,1,0:T(8,128)(2,1)} %bitcast.4), kind=kLoop, calls=%fused_computation.2 | loop fusion | flops 16777216 | bytes 16777216 | tf_op jit(solution)/shard_map/concatenate | solution.py:112
  252.3 8.2 %convolution_convert_fusion = bf16[32,128,512]{2,1,0:T(8,128)(2,1)} fusion(bf16[128,32,256]{0,2,1:T(8,128)(2,1)S(1)} %bitcast_select_fusion, bf16[32,512,256]{2,1,0:T(8,128)(2,1)} %pad_maximum_fusion), kind=kOutput, calls=%fused_computation.7 | convolution fusion | flops 1075838976 | bytes 14680064 | tf_op jit(solution)/shard_map/tks,kcs->ktc/dot_general | solution.py:206
  265.6 7.5 %all-to-all-start.1 = ((bf16[32,2,1024]{2,1,0:T(2,128)(2,1)}), bf16[32,2,1024]{2,1,0:T(2,128)(2,1)S(1)}, u32[]{:S(2)}, u32[]{:S(2)}) async-start(bf16[32,2,1024]{2,1,0:T(2,128)(2,1)} %reshape.352), calls=%async_computation.1 | async-start | bytes 262144 | tf_op jit(solution)/shard_map/all_to_all | solution.py:215
  274.0 9.0 %all-to-all-done.1 = bf16[32,2,1024]{2,1,0:T(2,128)(2,1)S(1)} async-done(((bf16[32,2,1024]{2,1,0:T(2,128)(2,1)}), bf16[32,2,1024]{2,1,0:T(2,128)(2,1)S(1)}, u32[]{:S(2)}, u32[]{:S(2)}) %all-to-all-start.1) | async-done | bytes 131104 | tf_op jit(solution)/shard_map/all_to_all | solution.py:215
  310.3 7.4 %collective-permute-done.6 = bf16[16,4096]{1,0:T(8,128)(2,1)S(1)} collective-permute-done((bf16[16,4096]{1,0:T(8,128)(2,1)S(1)}, bf16[16,4096]{1,0:T(8,128)(2,1)S(1)}, u32[]{:S(2)}, u32[]{:S(2)}) %collective-permute-start.6) | collective-permute-done | bytes 131104 | tf_op jit(solution)/shard_map/ppermute | solution.py:145
  320.0 12.3 %collective-permute-done.7 = bf16[32,4096]{1,0:T(8,128)(2,1)S(1)} collective-permute-done((bf16[32,4096]{1,0:T(8,128)(2,1)S(1)}, bf16[32,4096]{1,0:T(8,128)(2,1)S(1)}, u32[]{:S(2)}, u32[]{:S(2)}) %collective-permute-start.7) | collective-permute-done | bytes 262176 | tf_op jit(solution)/shard_map/ppermute | solution.py:145
  335.0 24.6 %collective-permute-done.8 = bf16[64,4096]{1,0:T(8,128)(2,1)S(1)} collective-permute-done((bf16[64,4096]{1,0:T(8,128)(2,1)S(1)}, bf16[64,4096]{1,0:T(8,128)(2,1)S(1)}, u32[]{:S(2)}, u32[]{:S(2)}) %collective-permute-start.8) | collective-permute-done | bytes 524320 | tf_op jit(solution)/shard_map/ppermute | solution.py:145
  364.0 21.7 %collective-permute-done.9 = bf16[128,4096]{1,0:T(8,128)(2,1)S(1)} collective-permute-done((bf16[128,4096]{1,0:T(8,128)(2,1)S(1)}, bf16[128,4096]{1,0:T(8,128)(2,1)S(1)}, u32[]{:S(2)}, u32[]{:S(2)}) %collective-permute-start.9) | collective-permute-done | bytes 1048608 | tf_op jit(solution)/shard_map/ppermute | solution.py:145
  391.3 45.7 %collective-permute-done.10 = bf16[256,4096]{1,0:T(8,128)(2,1)} collective-permute-done((bf16[256,4096]{1,0:T(8,128)(2,1)}, bf16[256,4096]{1,0:T(8,128)(2,1)}, u32[]{:S(2)}, u32[]{:S(2)}) %collective-permute-start.10) | collective-permute-done | bytes 2097184 | tf_op jit(solution)/shard_map/ppermute | solution.py:145
  444.8 4.1 collective-permute-start.11
  457.0 4.6 collective-permute-start.13
  463.6 11.3 %collective-permute-start.14 = (f32[33,256]{1,0:T(8,128)S(1)}, f32[33,256]{1,0:T(8,128)S(1)}, u32[]{:S(2)}, u32[]{:S(2)}) collective-permute-start(f32[33,256]{1,0:T(8,128)S(1)} %slice_select_fusion.3), channel_id=1, source_target_pairs={{0,64},{32,96},{64,0},{96,32},{128,192},{160,224},{192,128},{224,1... | collective-permute-start | bytes 101384 | tf_op jit(solution)/shard_map/ppermute | solution.py:183
  476.5 7.2 %collective-permute-start.15 = (f32[33,256]{1,0:T(8,128)S(1)}, f32[33,256]{1,0:T(8,128)S(1)}, u32[]{:S(2)}, u32[]{:S(2)}) collective-permute-start(f32[33,256]{1,0:T(8,128)S(1)} %select_add_fusion.3), channel_id=1, source_target_pairs={{0,64},{32,96},{64,0},{96,32},{128,192},{160,224},{192,128},{224,1... | collective-permute-start | bytes 101384 | tf_op jit(solution)/shard_map/ppermute | solution.py:185
  485.2 4.8 collective-permute-start.16
  498.4 8.0 %collective-permute-start.18 = (f32[264,256]{1,0:T(8,128)S(1)}, f32[264,256]{1,0:T(8,128)S(1)}, u32[]{:S(2)}, u32[]{:S(2)}) collective-permute-start(f32[264,256]{1,0:T(8,128)S(1)} %maximum_select_fusion.1), channel_id=1, source_target_pairs={{0,32},{32,0},{64,96},{96,64},{128,160},{160,128},{192,224},{224,1... | collective-permute-start | bytes 811016 | tf_op jit(solution)/shard_map/ppermute | solution.py:185
  (206 shorter events, 123.8 us)
Async XLA Ops:
  2.2 15.3 %collective-permute-start = (bf16[512,128]{1,0:T(8,128)(2,1)S(1)}, bf16[512,128]{1,0:T(8,128)(2,1)S(1)}, u32[]{:S(2)}, u32[]{:S(2)}) collective-permute-start(bf16[512,128]{1,0:T(8,128)(2,1)S(1)} %get-tuple-element.18), channel_id=1, source_target_pairs={{0,16},{1,17},{2,18},{3,19},{4,20},{5,21},{6,22},{7,23},{8,24},{9,... | collective-permute-start | bytes 393224 | tf_op jit(solution)/shard_map/ppermute | solution.py:145
  17.6 18.8 %collective-permute-start.1 = (bf16[1024,128]{1,0:T(8,128)(2,1)S(1)}, bf16[1024,128]{1,0:T(8,128)(2,1)S(1)}, u32[]{:S(2)}, u32[]{:S(2)}) collective-permute-start(bf16[1024,128]{1,0:T(8,128)(2,1)S(1)} %pad_maximum_fusion.7), channel_id=1, source_target_pairs={{0,8},{1,9},{2,10},{3,11},{4,12},{5,13},{6,14},{7,15},{8,0},{9,1},... | collective-permute-start | bytes 786440 | tf_op jit(solution)/shard_map/ppermute | solution.py:145
  36.5 26.9 %collective-permute-start.2 = (bf16[2048,128]{1,0:T(8,128)(2,1)S(1)}, bf16[2048,128]{1,0:T(8,128)(2,1)S(1)}, u32[]{:S(2)}, u32[]{:S(2)}) collective-permute-start(bf16[2048,128]{1,0:T(8,128)(2,1)S(1)} %pad_maximum_fusion.3), channel_id=1, source_target_pairs={{0,2},{1,3},{2,0},{3,1},{4,6},{5,7},{6,4},{7,5},{8,10},{9,11},{10,... | collective-permute-start | bytes 1572872 | tf_op jit(solution)/shard_map/ppermute | solution.py:145
  63.4 25.1 %collective-permute-start.3 = (bf16[4096,128]{1,0:T(8,128)(2,1)S(1)}, bf16[4096,128]{1,0:T(8,128)(2,1)S(1)}, u32[]{:S(2)}, u32[]{:S(2)}) collective-permute-start(bf16[4096,128]{1,0:T(8,128)(2,1)S(1)} %pad_maximum_fusion.1), channel_id=1, source_target_pairs={{0,4},{1,5},{2,6},{3,7},{4,0},{5,1},{6,2},{7,3},{8,12},{9,13},{10,... | collective-permute-start | bytes 3145736 | tf_op jit(solution)/shard_map/ppermute | solution.py:145
  67.6 26.9 %copy-start.13 = (bf16[1,128,512]{2,1,0:T(8,128)(2,1)S(1)}, bf16[1,128,512]{2,1,0:T(8,128)(2,1)}, u32[]{:S(2)}) copy-start(bf16[1,128,512]{2,1,0:T(8,128)(2,1)} %param.7) | copy-start | bytes 393220
  88.5 15.4 %copy-start.14 = (bf16[1,128,512]{2,1,0:T(8,128)(2,1)S(1)}, bf16[1,128,512]{2,1,0:T(8,128)(2,1)}, u32[]{:S(2)}) copy-start(bf16[1,128,512]{2,1,0:T(8,128)(2,1)} %param.8) | copy-start | bytes 393220
  90.0 61.5 %copy-start.15 = (bf16[1,128,512]{2,1,0:T(8,128)(2,1)S(1)}, bf16[1,128,512]{2,1,0:T(8,128)(2,1)}, u32[]{:S(2)}) copy-start(bf16[1,128,512]{2,1,0:T(8,128)(2,1)} %param.9) | copy-start | bytes 393220
  90.0 74.9 %collective-permute-start.4 = (bf16[8192,128]{1,0:T(8,128)(2,1)}, bf16[8192,128]{1,0:T(8,128)(2,1)S(1)}, u32[]{:S(2)}, u32[]{:S(2)}) collective-permute-start(bf16[8192,128]{1,0:T(8,128)(2,1)} %get-tuple-element.29), channel_id=1, source_target_pairs={{0,1},{1,0},{2,3},{3,2},{4,5},{5,4},{6,7},{7,6},{8,9},{9,8},{10,11... | collective-permute-start | bytes 6291464 | tf_op jit(solution)/shard_map/ppermute | solution.py:145
  97.3 48.2 %all-to-all-start.4 = ((bf16[32,2,1024]{2,1,0:T(2,128)(2,1)}), bf16[32,2,1024]{2,1,0:T(2,128)(2,1)S(1)}, u32[]{:S(2)}, u32[]{:S(2)}) async-start(bf16[32,2,1024]{2,1,0:T(2,128)(2,1)} %reshape.350), calls=%async_computation.4 | async-start | bytes 262144 | tf_op jit(solution)/shard_map/all_to_all | solution.py:212
  145.5 15.5 %all-to-all-start.2 = ((bf16[32,2,1024]{2,1,0:T(2,128)(2,1)}), bf16[32,2,1024]{2,1,0:T(2,128)(2,1)S(1)}, u32[]{:S(2)}, u32[]{:S(2)}) async-start(bf16[32,2,1024]{2,1,0:T(2,128)(2,1)} %reshape.348), calls=%async_computation.2 | async-start | bytes 262144 | tf_op jit(solution)/shard_map/all_to_all | solution.py:213
  161.1 16.9 %all-to-all-start.3 = ((bf16[32,2,1024]{2,1,0:T(2,128)(2,1)}), bf16[32,2,1024]{2,1,0:T(2,128)(2,1)S(1)}, u32[]{:S(2)}, u32[]{:S(2)}) async-start(bf16[32,2,1024]{2,1,0:T(2,128)(2,1)} %reshape.346), calls=%async_computation.3 | async-start | bytes 262144 | tf_op jit(solution)/shard_map/all_to_all | solution.py:214
  169.5 75.0 %collective-permute-start.5 = (bf16[32,512,128]{2,1,0:T(8,128)(2,1)}, bf16[32,512,128]{2,1,0:T(8,128)(2,1)}, u32[]{:S(2)}, u32[]{:S(2)}) collective-permute-start(bf16[32,512,128]{2,1,0:T(8,128)(2,1)} %bitcast.4), channel_id=1, source_target_pairs={{0,32},{32,0},{64,96},{96,64},{128,160},{160,128},{192,224},{224,1... | collective-permute-start | bytes 12582920 | tf_op jit(solution)/shard_map/ppermute | solution.py:111
  178.0 62.4 %all-to-all-start = ((bf16[32,128,256]{1,2,0:T(8,128)(2,1)}), bf16[32,128,256]{1,2,0:T(8,128)(2,1)}, u32[]{:S(2)}, u32[]{:S(2)}) async-start(bf16[32,128,256]{1,2,0:T(8,128)(2,1)} %bitcast.6), calls=%async_computation | async-start | bytes 4194304 | tf_op jit(solution)/shard_map/all_to_all | solution.py:100
  260.5 12.7 %copy-start.12 = (f32[16,64,128]{2,1,0:T(8,128)S(1)}, f32[16,64,128]{2,1,0:T(8,128)}, u32[]{:S(2)}) copy-start(f32[16,64,128]{2,1,0:T(8,128)} %fusion.47) | copy-start | bytes 1572868
  265.6 17.4 %all-to-all-start.1 = ((bf16[32,2,1024]{2,1,0:T(2,128)(2,1)}), bf16[32,2,1024]{2,1,0:T(2,128)(2,1)S(1)}, u32[]{:S(2)}, u32[]{:S(2)}) async-start(bf16[32,2,1024]{2,1,0:T(2,128)(2,1)} %reshape.352), calls=%async_computation.1 | async-start | bytes 262144 | tf_op jit(solution)/shard_map/all_to_all | solution.py:215
  274.0 14.1 %copy-start.1 = (f32[16,64,128]{2,1,0:T(8,128)}, f32[16,64,128]{2,1,0:T(8,128)S(1)}, u32[]{:S(2)}) copy-start(f32[16,64,128]{2,1,0:T(8,128)S(1)} %convolution_subtract_fusion.5) | copy-start | bytes 1572868
  307.8 10.0 %collective-permute-start.6 = (bf16[16,4096]{1,0:T(8,128)(2,1)S(1)}, bf16[16,4096]{1,0:T(8,128)(2,1)S(1)}, u32[]{:S(2)}, u32[]{:S(2)}) collective-permute-start(bf16[16,4096]{1,0:T(8,128)(2,1)S(1)} %get-tuple-element.16), channel_id=1, source_target_pairs={{0,16},{1,17},{2,18},{3,19},{4,20},{5,21},{6,22},{7,23},{8,24},{9,... | collective-permute-start | bytes 393224 | tf_op jit(solution)/shard_map/ppermute | solution.py:145
  317.8 14.5 %collective-permute-start.7 = (bf16[32,4096]{1,0:T(8,128)(2,1)S(1)}, bf16[32,4096]{1,0:T(8,128)(2,1)S(1)}, u32[]{:S(2)}, u32[]{:S(2)}) collective-permute-start(bf16[32,4096]{1,0:T(8,128)(2,1)S(1)} %pad_maximum_fusion.8), channel_id=1, source_target_pairs={{0,8},{1,9},{2,10},{3,11},{4,12},{5,13},{6,14},{7,15},{8,0},{9,1},... | collective-permute-start | bytes 786440 | tf_op jit(solution)/shard_map/ppermute | solution.py:145
  332.3 27.2 %collective-permute-start.8 = (bf16[64,4096]{1,0:T(8,128)(2,1)S(1)}, bf16[64,4096]{1,0:T(8,128)(2,1)S(1)}, u32[]{:S(2)}, u32[]{:S(2)}) collective-permute-start(bf16[64,4096]{1,0:T(8,128)(2,1)S(1)} %pad_maximum_fusion.4), channel_id=1, source_target_pairs={{0,2},{1,3},{2,0},{3,1},{4,6},{5,7},{6,4},{7,5},{8,10},{9,11},{10,... | collective-permute-start | bytes 1572872 | tf_op jit(solution)/shard_map/ppermute | solution.py:145
  359.6 26.1 %collective-permute-start.9 = (bf16[128,4096]{1,0:T(8,128)(2,1)S(1)}, bf16[128,4096]{1,0:T(8,128)(2,1)S(1)}, u32[]{:S(2)}, u32[]{:S(2)}) collective-permute-start(bf16[128,4096]{1,0:T(8,128)(2,1)S(1)} %pad_maximum_fusion.2), channel_id=1, source_target_pairs={{0,4},{1,5},{2,6},{3,7},{4,0},{5,1},{6,2},{7,3},{8,12},{9,13},{10,... | collective-permute-start | bytes 3145736 | tf_op jit(solution)/shard_map/ppermute | solution.py:145
  389.0 48.0 %collective-permute-start.10 = (bf16[256,4096]{1,0:T(8,128)(2,1)}, bf16[256,4096]{1,0:T(8,128)(2,1)}, u32[]{:S(2)}, u32[]{:S(2)}) collective-permute-start(bf16[256,4096]{1,0:T(8,128)(2,1)} %get-tuple-element.25), channel_id=1, source_target_pairs={{0,1},{1,0},{2,3},{3,2},{4,5},{5,4},{6,7},{7,6},{8,9},{9,8},{10,11... | collective-permute-start | bytes 6291464 | tf_op jit(solution)/shard_map/ppermute | solution.py:145
  444.8 5.3 %collective-permute-start.11 = (f32[264,256]{1,0:T(8,128)S(1)}, f32[264,256]{1,0:T(8,128)S(1)}, u32[]{:S(2)}, u32[]{:S(2)}) collective-permute-start(f32[264,256]{1,0:T(8,128)S(1)} %slice_select_fusion), channel_id=1, source_target_pairs={{0,32},{32,0},{64,96},{96,64},{128,160},{160,128},{192,224},{224,1... | collective-permute-start | bytes 811016 | tf_op jit(solution)/shard_map/ppermute | solution.py:183
  450.2 6.8 %collective-permute-start.12 = (f32[132,256]{1,0:T(8,128)S(1)}, f32[132,256]{1,0:T(8,128)S(1)}, u32[]{:S(2)}, u32[]{:S(2)}) collective-permute-start(f32[132,256]{1,0:T(8,128)S(1)} %slice_select_fusion.1), channel_id=1, source_target_pairs={{0,128},{32,160},{64,192},{96,224},{128,0},{160,32},{192,64},{224,... | collective-permute-start | bytes 405512 | tf_op jit(solution)/shard_map/ppermute | solution.py:183
  457.0 6.6 %collective-permute-start.13 = (f32[66,256]{1,0:T(8,128)S(1)}, f32[66,256]{1,0:T(8,128)S(1)}, u32[]{:S(2)}, u32[]{:S(2)}) collective-permute-start(f32[66,256]{1,0:T(8,128)S(1)} %slice_select_fusion.2), channel_id=1, source_target_pairs={{0,256},{32,288},{64,320},{96,352},{128,384},{160,416},{192,448},{... | collective-permute-start | bytes 202760 | tf_op jit(solution)/shard_map/ppermute | solution.py:183
  463.6 12.8 %collective-permute-start.14 = (f32[33,256]{1,0:T(8,128)S(1)}, f32[33,256]{1,0:T(8,128)S(1)}, u32[]{:S(2)}, u32[]{:S(2)}) collective-permute-start(f32[33,256]{1,0:T(8,128)S(1)} %slice_select_fusion.3), channel_id=1, source_target_pairs={{0,64},{32,96},{64,0},{96,32},{128,192},{160,224},{192,128},{224,1... | collective-permute-start | bytes 101384 | tf_op jit(solution)/shard_map/ppermute | solution.py:183
  476.5 8.7 %collective-permute-start.15 = (f32[33,256]{1,0:T(8,128)S(1)}, f32[33,256]{1,0:T(8,128)S(1)}, u32[]{:S(2)}, u32[]{:S(2)}) collective-permute-start(f32[33,256]{1,0:T(8,128)S(1)} %select_add_fusion.3), channel_id=1, source_target_pairs={{0,64},{32,96},{64,0},{96,32},{128,192},{160,224},{192,128},{224,1... | collective-permute-start | bytes 101384 | tf_op jit(solution)/shard_map/ppermute | solution.py:185
  484.5 10.5 %copy-start.6 = (f32[1,32,128,16]{2,1,3,0:T(8,128)S(1)}, f32[1,32,128,16]{2,1,3,0:T(8,128)}, u32[]{:S(2)}) copy-start(f32[1,32,128,16]{2,1,3,0:T(8,128)} %copy-done.5) | copy-start | bytes 786436
  484.5 10.5 %copy-start.8 = (f32[1,32,128,16]{2,1,3,0:T(8,128)S(1)}, f32[1,32,128,16]{2,1,3,0:T(8,128)}, u32[]{:S(2)}) copy-start(f32[1,32,128,16]{2,1,3,0:T(8,128)} %copy-done.7) | copy-start | bytes 786436
  485.2 21.3 %copy-start.4 = (f32[1,32,128,16]{2,1,3,0:T(8,128)S(1)}, f32[1,32,128,16]{2,1,3,0:T(8,128)}, u32[]{:S(2)}) copy-start(f32[1,32,128,16]{2,1,3,0:T(8,128)} %copy-done.3) | copy-start | bytes 786436
  485.2 6.7 %collective-permute-start.16 = (f32[66,256]{1,0:T(8,128)S(1)}, f32[66,256]{1,0:T(8,128)S(1)}, u32[]{:S(2)}, u32[]{:S(2)}) collective-permute-start(f32[66,256]{1,0:T(8,128)S(1)} %maximum_select_fusion.3), channel_id=1, source_target_pairs={{0,256},{32,288},{64,320},{96,352},{128,384},{160,416},{192,448},{... | collective-permute-start | bytes 202760 | tf_op jit(solution)/shard_map/ppermute | solution.py:185
  491.9 6.5 %collective-permute-start.17 = (f32[132,256]{1,0:T(8,128)S(1)}, f32[132,256]{1,0:T(8,128)S(1)}, u32[]{:S(2)}, u32[]{:S(2)}) collective-permute-start(f32[132,256]{1,0:T(8,128)S(1)} %maximum_select_fusion.2), channel_id=1, source_target_pairs={{0,128},{32,160},{64,192},{96,224},{128,0},{160,32},{192,64},{224,... | collective-permute-start | bytes 405512 | tf_op jit(solution)/shard_map/ppermute | solution.py:185
  498.4 9.2 %collective-permute-start.18 = (f32[264,256]{1,0:T(8,128)S(1)}, f32[264,256]{1,0:T(8,128)S(1)}, u32[]{:S(2)}, u32[]{:S(2)}) collective-permute-start(f32[264,256]{1,0:T(8,128)S(1)} %maximum_select_fusion.1), channel_id=1, source_target_pairs={{0,32},{32,0},{64,96},{96,64},{128,160},{160,128},{192,224},{224,1... | collective-permute-start | bytes 811016 | tf_op jit(solution)/shard_map/ppermute | solution.py:185
  (11 other events, 27.0 us)

commit v4 on v3

--- a/solution.py
+++ b/solution.py
@@ -101,15 +101,19 @@
     return moved.reshape(blocks * tok_rows, block_width)
 
 
-def shared_weight(out_weight, masks):
+def shared_weight(out_weight, masks, tie):
     channels, width = out_weight.shape
     half = width // 2
     core = lax.axis_index("dp") % 2
     piece = lax.dynamic_slice_in_dim(out_weight, core * half, half, axis=1)
-    held = doubling_gather(piece, "ctx", masks)
-    held = held.reshape(-1, channels, half)
+    piece, tie = lax.optimization_barrier((piece, tie))
+    split = channels // 2
+    first = doubling_gather(piece[:split], "ctx", masks).reshape(-1, split, half)
+    second = doubling_gather(piece[split:], "ctx", other_masks(masks)).reshape(-1, split, half)
+    held = jnp.concatenate([first, second], axis=1)
     other = lax.ppermute(held, "dp", axis_pairs(lax.axis_size("dp"), 1))
-    return jnp.concatenate([held, other], axis=2)
+    full = jnp.concatenate([held, other], axis=2)
+    return full[:, :split], full[:, split:], tie
 
 
 def matching_columns(rows, blocks, masks):
@@ -136,6 +140,10 @@
     low = [m for m in bits if m < 4]
     high = [m for m in bits if m >= 4]
     return tuple(reversed(high[1:])) + tuple(reversed(low[1:])) + tuple(high[:1]) + tuple(low[:1])
+
+
+def other_masks(masks):
+    return masks[:-2] + (masks[-1], masks[-2])
 
 
 def doubling_gather(block, axis, masks):
@@ -198,22 +206,32 @@
     tok_rows = grad_out.shape[1]
     ctx_size = lax.axis_size("ctx")
     gather_masks = ctx_masks(ctx_size)
-    weight_part = shared_weight(out_weight, gather_masks)
-    grad_cols = columns_by_position(grad_out[0], block_width)
-    weight_part, grad_cols = lax.optimization_barrier((weight_part, grad_cols))
-    blocks = weight_part.shape[0]
-    partial_value = matching_columns(grad_out[0], blocks, gather_masks)
-    terms = jnp.einsum(
-        "tks,kcs->ktc", partial_value, weight_part, preferred_element_type=jnp.float32
-    )
-    gated_sum = rounded_sum(terms)
-    grad_gated = gated_sum.astype(jnp.bfloat16)[None]
-    query_ch, key_ch, value_ch, gated_grad_ch = (
+    query_ch, key_ch, value_ch = (
         lax.all_to_all(queries, "ctx", split_axis=2, concat_axis=1, tiled=True),
         lax.all_to_all(keys, "ctx", split_axis=2, concat_axis=1, tiled=True),
         lax.all_to_all(values, "ctx", split_axis=2, concat_axis=1, tiled=True),
-        lax.all_to_all(grad_gated, "ctx", split_axis=2, concat_axis=1, tiled=True),
-    )
+    )
+    weight_first, weight_second, (query_ch, key_ch, value_ch) = shared_weight(
+        out_weight, gather_masks, (query_ch, key_ch, value_ch)
+    )
+    blocks = weight_first.shape[0]
+    terms = jnp.concatenate(
+        [
+            jnp.einsum(
+                "tks,kcs->ktc",
+                matching_columns(grad_out[0], blocks, order),
+                part,
+                preferred_element_type=jnp.float32,
+            )
+            for order, part in ((gather_masks, weight_first), (other_masks(gather_masks), weight_second))
+        ],
+        axis=2,
+    )
+    gated_sum = rounded_sum(terms)
+    grad_gated = gated_sum.astype(jnp.bfloat16)[None]
+    gated_grad_ch = lax.all_to_all(grad_gated, "ctx", split_axis=2, concat_axis=1, tiled=True)
+    grad_in, _ = lax.optimization_barrier((grad_out[0], weight_first))
+    grad_cols = columns_by_position(grad_in, block_width)
     grad_gated_full = channels_first(gated_grad_ch)
     seq_len = query_ch.shape[1]
     fft_rows = 2 * seq_len // FFT_COLS
@@ -242,14 +260,21 @@
     grad_queries = (grad_gated_full * conv_out).T.astype(jnp.bfloat16)[None]
     grad_keys = (grad_product * value_full).T.astype(jnp.bfloat16)[None]
     grad_values = (grad_product * key_full).T.astype(jnp.bfloat16)[None]
-    gathered = doubling_gather(gated_t, "ctx", gather_masks)
-    partial_value = lax.dot_general(
-        gathered,
-        grad_cols,
-        (((1,), (0,)), ((), ())),
-        preferred_element_type=jnp.float32,
-    )
-    grad_weight = unpermute_blocks(partial_value, "ctx", gather_masks)
+    gated_t, grad_cols = lax.optimization_barrier((gated_t, grad_cols))
+    split = gated_t.shape[0] // 2
+    pieces = []
+    for rows, order in ((gated_t[:split], gather_masks), (gated_t[split:], other_masks(gather_masks))):
+        partial_value = lax.dot_general(
+            doubling_gather(rows, "ctx", order),
+            grad_cols,
+            (((1,), (0,)), ((), ())),
+            preferred_element_type=jnp.float32,
+        )
+        pieces.append(unpermute_blocks(partial_value, "ctx", order))
+    width = grad_cols.shape[1]
+    grad_weight = jnp.stack(
+        [piece.reshape(ctx_size, split, width) for piece in pieces], axis=1
+    ).reshape(-1, width)
     grad_residues = jnp.sum(grad_taps[:, None, :] * decay_terms, axis=2)
     grad_decays = -residues * jnp.sum(
         (grad_taps * positions[None, :])[:, None, :] * decay_terms, axis=2

time: 517 us -> 444 us (0.86)
  the two profiles are of different devices: /device:TPU:1 before, /device:TPU:189 now
where the time goes in v4:
time: 444 us; the launch traced here: 436 us
  starting transfers between devices  168 us (38%)
  waiting for transfers between devices  136 us (31%)
  local copies, waits for them, and re-layouts  61.5 us (14%)
  matrix products  38.1 us (9%)
  other arithmetic  30.3 us (7%)
    ppermute x20, waiting for transfers between devices, doubling_gather(): lax.ppermute(held, axis, axis_pairs(size, mask))  98.7 us
    ppermute x20, starting transfers between devices, doubling_gather(): lax.ppermute(held, axis, axis_pairs(size, mask))  84.4 us
    unnamed x73, local copies, waits for them, and re-layouts  22.9 us
    dot_general x24, matrix products, single(): return jnp.einsum('ckm,mj->ckj', data, table, precision=HIGHEST)  20 us
    ppermute x4, starting transfers between devices, summed_over_dp(): other = lax.ppermute(held, 'dp', axis_pairs(size, mask))  16.6 us
    concatenate x8, local copies, waits for them, and re-layouts, doubling_gather(): jnp.concatenate([held, lax.ppermute(held, axis, axis_pairs(size, mask))],...  13.5 us
    ppermute x4, waiting for transfers between devices, summed_over_dp(): held = keep + lax.ppermute(send, 'dp', axis_pairs(size, mask))  13.5 us
    ppermute x4, waiting for transfers between devices, summed_over_dp(): other = lax.ppermute(held, 'dp', axis_pairs(size, mask))  11.7 us
  transfers between devices with their start and end apart: 34, of which 25 were waited for; matrix products, arithmetic and copies ran while one was open for 20% of the time, Pallas kernels for 0%

profile of v4, /device:TPU:189, one launch (start us, length us, event | category | flops | bytes accessed | tf_op | source)
XLA Modules:
  0.0 436.3 jit_solution(13111066779169733465)
XLA Ops:
  4.5 11.4 %all-to-all-start.1 = ((bf16[32,2,1024]{2,1,0:T(2,128)(2,1)}), bf16[32,2,1024]{2,1,0:T(2,128)(2,1)S(1)}, u32[]{:S(2)}, u32[]{:S(2)}) async-start(bf16[32,2,1024]{2,1,0:T(2,128)(2,1)} %reshape.276), calls=%async_computation.1 | async-start | bytes 262144 | tf_op jit(solution)/shard_map/all_to_all | solution.py:211
  21.9 7.7 %all-to-all-start.2 = ((bf16[32,2,1024]{2,1,0:T(2,128)(2,1)}), bf16[32,2,1024]{2,1,0:T(2,128)(2,1)S(1)}, u32[]{:S(2)}, u32[]{:S(2)}) async-start(bf16[32,2,1024]{2,1,0:T(2,128)(2,1)} %reshape.278), calls=%async_computation.2 | async-start | bytes 262144 | tf_op jit(solution)/shard_map/all_to_all | solution.py:212
  31.9 3.7 all-to-all-done.2
  35.7 7.7 %all-to-all-start = ((bf16[32,2,1024]{2,1,0:T(2,128)(2,1)}), bf16[32,2,1024]{2,1,0:T(2,128)(2,1)S(1)}, u32[]{:S(2)}, u32[]{:S(2)}) async-start(bf16[32,2,1024]{2,1,0:T(2,128)(2,1)} %reshape.274), calls=%async_computation | async-start | bytes 262144 | tf_op jit(solution)/shard_map/all_to_all | solution.py:210
  49.2 8.8 %all-to-all-start.4 = ((bf16[32,128,256]{1,2,0:T(8,128)(2,1)}), bf16[32,128,256]{1,2,0:T(8,128)(2,1)}, u32[]{:S(2)}, u32[]{:S(2)}) async-start(bf16[32,128,256]{1,2,0:T(8,128)(2,1)} %bitcast.44), calls=%async_computation.4 | async-start | bytes 4194304 | tf_op jit(solution)/shard_map/all_to_all | solution.py:100
  59.0 5.3 %collective-permute-start = (bf16[256,128]{1,0:T(8,128)(2,1)S(1)}, bf16[256,128]{1,0:T(8,128)(2,1)S(1)}, u32[]{:S(2)}, u32[]{:S(2)}) collective-permute-start(bf16[256,128]{1,0:T(8,128)(2,1)S(1)} %get-tuple-element.74), channel_id=1, source_target_pairs={{0,16},{1,17},{2,18},{3,19},{4,20},{5,21},{6,22},{7,23},{8,24},{9,... | collective-permute-start | bytes 196616 | tf_op jit(solution)/shard_map/ppermute | solution.py:153
  64.3 3.9 collective-permute-start.5
  68.2 42.5 %collective-permute-done = bf16[256,128]{1,0:T(8,128)(2,1)S(1)} collective-permute-done((bf16[256,128]{1,0:T(8,128)(2,1)S(1)}, bf16[256,128]{1,0:T(8,128)(2,1)S(1)}, u32[]{:S(2)}, u32[]{:S(2)}) %collective-permute-start) | collective-permute-done | bytes 65568 | tf_op jit(solution)/shard_map/ppermute | solution.py:153
  117.4 3.7 collective-permute-start.2
  126.3 3.3 collective-permute-start.3
  130.3 12.1 %collective-permute-done.7 = bf16[1024,128]{1,0:T(8,128)(2,1)S(1)} collective-permute-done((bf16[1024,128]{1,0:T(8,128)(2,1)S(1)}, bf16[1024,128]{1,0:T(8,128)(2,1)S(1)}, u32[]{:S(2)}, u32[]{:S(2)}) %collective-permute-start.7) | collective-permute-done | bytes 262176 | tf_op jit(solution)/shard_map/ppermute | solution.py:153
  153.8 6.0 %collective-permute-start.9 = (bf16[4096,128]{1,0:T(8,128)(2,1)}, bf16[4096,128]{1,0:T(8,128)(2,1)}, u32[]{:S(2)}, u32[]{:S(2)}) collective-permute-start(bf16[4096,128]{1,0:T(8,128)(2,1)} %get-tuple-element.47), channel_id=1, source_target_pairs={{0,4},{1,5},{2,6},{3,7},{4,0},{5,1},{6,2},{7,3},{8,12},{9,13},{10,... | collective-permute-start | bytes 3145736 | tf_op jit(solution)/shard_map/ppermute | solution.py:153
  165.3 9.0 %collective-permute-done.4 = bf16[4096,128]{1,0:T(8,128)(2,1)} collective-permute-done((bf16[4096,128]{1,0:T(8,128)(2,1)}, bf16[4096,128]{1,0:T(8,128)(2,1)}, u32[]{:S(2)}, u32[]{:S(2)}) %collective-permute-start.4) | collective-permute-done | bytes 1048608 | tf_op jit(solution)/shard_map/ppermute | solution.py:153
  178.8 4.8 %pad_maximum_fusion.1 = bf16[32,512,128]{2,1,0:T(8,128)(2,1)} fusion(bf16[32,256,128]{2,1,0:T(8,128)(2,1)} %bitcast.7, bf16[32,256,128]{2,1,0:T(8,128)(2,1)} %bitcast.6), kind=kLoop, calls=%fused_computation.7 | loop fusion | flops 8388608 | bytes 8388608 | tf_op jit(solution)/shard_map/concatenate | solution.py:113
  183.7 9.7 %collective-permute-start.10 = (bf16[32,512,128]{2,1,0:T(8,128)(2,1)}, bf16[32,512,128]{2,1,0:T(8,128)(2,1)}, u32[]{:S(2)}, u32[]{:S(2)}) collective-permute-start(bf16[32,512,128]{2,1,0:T(8,128)(2,1)} %pad_maximum_fusion.1), channel_id=1, source_target_pairs={{0,32},{32,0},{64,96},{96,64},{128,160},{160,128},{192,224},{224,1... | collective-permute-start | bytes 12582920 | tf_op jit(solution)/shard_map/ppermute | solution.py:114
  195.0 4.1 copy.63
  211.2 4.6 %pad_maximum_fusion = bf16[32,512,256]{2,1,0:T(8,128)(2,1)S(1)} fusion(bf16[32,512,128]{2,1,0:T(8,128)(2,1)} %collective-permute-done.10, bf16[32,256,128]{2,1,0:T(8,128)(2,1)} %bitcast.7, bf16[32,256,128]{2,1,0:T(8,128)(2,1)} %bitcast.6), kind=kLoop, calls=%fused_computation.4 | loop fusion | flops 25165824 | bytes 16777216 | tf_op jit(solution)/shard_map/concatenate | solution.py:115
  226.4 10.1 %all-to-all-start.3 = ((bf16[32,2,1024]{2,1,0:T(2,128)(2,1)}), bf16[32,2,1024]{2,1,0:T(2,128)(2,1)}, u32[]{:S(2)}, u32[]{:S(2)}) async-start(bf16[32,2,1024]{2,1,0:T(2,128)(2,1)} %reshape.280), calls=%async_computation.3 | async-start | bytes 262144 | tf_op jit(solution)/shard_map/all_to_all | solution.py:232
  237.4 3.5 copy.78
  272.5 3.9 collective-permute-start.11
  276.6 5.2 %collective-permute-start.16 = (bf16[8,4096]{1,0:T(8,128)(2,1)S(1)}, bf16[8,4096]{1,0:T(8,128)(2,1)S(1)}, u32[]{:S(2)}, u32[]{:S(2)}) collective-permute-start(bf16[8,4096]{1,0:T(8,128)(2,1)S(1)} %get-tuple-element.63), channel_id=1, source_target_pairs={{0,16},{1,17},{2,18},{3,19},{4,20},{5,21},{6,22},{7,23},{8,24},{9,... | collective-permute-start | bytes 196616 | tf_op jit(solution)/shard_map/ppermute | solution.py:153
  281.8 3.7 collective-permute-start.12
  300.5 21.1 %collective-permute-start.14 = (bf16[64,4096]{1,0:T(8,128)(2,1)S(1)}, bf16[64,4096]{1,0:T(8,128)(2,1)S(1)}, u32[]{:S(2)}, u32[]{:S(2)}) collective-permute-start(bf16[64,4096]{1,0:T(8,128)(2,1)S(1)} %pad_maximum_fusion.5), channel_id=1, source_target_pairs={{0,4},{1,5},{2,6},{3,7},{4,0},{5,1},{6,2},{7,3},{8,12},{9,13},{10,... | collective-permute-start | bytes 1572872 | tf_op jit(solution)/shard_map/ppermute | solution.py:153
  324.5 8.8 %collective-permute-done.14 = bf16[64,4096]{1,0:T(8,128)(2,1)S(1)} collective-permute-done((bf16[64,4096]{1,0:T(8,128)(2,1)S(1)}, bf16[64,4096]{1,0:T(8,128)(2,1)S(1)}, u32[]{:S(2)}, u32[]{:S(2)}) %collective-permute-start.14) | collective-permute-done | bytes 524320 | tf_op jit(solution)/shard_map/ppermute | solution.py:153
  338.3 5.1 %collective-permute-start.20 = (bf16[128,4096]{1,0:T(8,128)(2,1)}, bf16[128,4096]{1,0:T(8,128)(2,1)}, u32[]{:S(2)}, u32[]{:S(2)}) collective-permute-start(bf16[128,4096]{1,0:T(8,128)(2,1)} %get-tuple-element.37), channel_id=1, source_target_pairs={{0,4},{1,5},{2,6},{3,7},{4,0},{5,1},{6,2},{7,3},{8,12},{9,13},{10,... | collective-permute-start | bytes 3145736 | tf_op jit(solution)/shard_map/ppermute | solution.py:153
  343.6 16.5 %collective-permute-done.15 = bf16[128,4096]{1,0:T(8,128)(2,1)} collective-permute-done((bf16[128,4096]{1,0:T(8,128)(2,1)}, bf16[128,4096]{1,0:T(8,128)(2,1)}, u32[]{:S(2)}, u32[]{:S(2)}) %collective-permute-start.15) | collective-permute-done | bytes 1048608 | tf_op jit(solution)/shard_map/ppermute | solution.py:153
  374.3 4.1 collective-permute-start.21
  389.4 3.7 collective-permute-done.23
  396.4 5.5 %collective-permute-done.24 = f32[33,256]{1,0:T(8,128)S(1)} collective-permute-done((f32[33,256]{1,0:T(8,128)S(1)}, f32[33,256]{1,0:T(8,128)S(1)}, u32[]{:S(2)}, u32[]{:S(2)}) %collective-permute-start.24) | collective-permute-done | bytes 33824 | tf_op jit(solution)/shard_map/ppermute | solution.py:191
  405.1 5.4 %collective-permute-done.25 = f32[33,256]{1,0:T(8,128)S(1)} collective-permute-done((f32[33,256]{1,0:T(8,128)S(1)}, f32[33,256]{1,0:T(8,128)S(1)}, u32[]{:S(2)}, u32[]{:S(2)}) %collective-permute-start.25) | collective-permute-done | bytes 33824 | tf_op jit(solution)/shard_map/ppermute | solution.py:193
  413.4 3.7 collective-permute-done.26
  423.3 9.3 %collective-permute-start.28 = (f32[264,256]{1,0:T(8,128)S(1)}, f32[264,256]{1,0:T(8,128)S(1)}, u32[]{:S(2)}, u32[]{:S(2)}) collective-permute-start(f32[264,256]{1,0:T(8,128)S(1)} %maximum_select_fusion.1), channel_id=1, source_target_pairs={{0,32},{32,0},{64,96},{96,64},{128,160},{160,128},{192,224},{224,1... | collective-permute-start | bytes 811016 | tf_op jit(solution)/shard_map/ppermute | solution.py:193
  (245 shorter events, 176.1 us)
Async XLA Ops:
  4.5 17.4 %all-to-all-start.1 = ((bf16[32,2,1024]{2,1,0:T(2,128)(2,1)}), bf16[32,2,1024]{2,1,0:T(2,128)(2,1)S(1)}, u32[]{:S(2)}, u32[]{:S(2)}) async-start(bf16[32,2,1024]{2,1,0:T(2,128)(2,1)} %reshape.276), calls=%async_computation.1 | async-start | bytes 262144 | tf_op jit(solution)/shard_map/all_to_all | solution.py:211
  21.9 13.8 %all-to-all-start.2 = ((bf16[32,2,1024]{2,1,0:T(2,128)(2,1)}), bf16[32,2,1024]{2,1,0:T(2,128)(2,1)S(1)}, u32[]{:S(2)}, u32[]{:S(2)}) async-start(bf16[32,2,1024]{2,1,0:T(2,128)(2,1)} %reshape.278), calls=%async_computation.2 | async-start | bytes 262144 | tf_op jit(solution)/shard_map/all_to_all | solution.py:212
  35.7 13.5 %all-to-all-start = ((bf16[32,2,1024]{2,1,0:T(2,128)(2,1)}), bf16[32,2,1024]{2,1,0:T(2,128)(2,1)S(1)}, u32[]{:S(2)}, u32[]{:S(2)}) async-start(bf16[32,2,1024]{2,1,0:T(2,128)(2,1)} %reshape.274), calls=%async_computation | async-start | bytes 262144 | tf_op jit(solution)/shard_map/all_to_all | solution.py:210
  49.2 177.2 %all-to-all-start.4 = ((bf16[32,128,256]{1,2,0:T(8,128)(2,1)}), bf16[32,128,256]{1,2,0:T(8,128)(2,1)}, u32[]{:S(2)}, u32[]{:S(2)}) async-start(bf16[32,128,256]{1,2,0:T(8,128)(2,1)} %bitcast.44), calls=%async_computation.4 | async-start | bytes 4194304 | tf_op jit(solution)/shard_map/all_to_all | solution.py:100
  59.0 51.7 %collective-permute-start = (bf16[256,128]{1,0:T(8,128)(2,1)S(1)}, bf16[256,128]{1,0:T(8,128)(2,1)S(1)}, u32[]{:S(2)}, u32[]{:S(2)}) collective-permute-start(bf16[256,128]{1,0:T(8,128)(2,1)S(1)} %get-tuple-element.74), channel_id=1, source_target_pairs={{0,16},{1,17},{2,18},{3,19},{4,20},{5,21},{6,22},{7,23},{8,24},{9,... | collective-permute-start | bytes 196616 | tf_op jit(solution)/shard_map/ppermute | solution.py:153
  64.3 49.4 %collective-permute-start.5 = (bf16[256,128]{1,0:T(8,128)(2,1)S(1)}, bf16[256,128]{1,0:T(8,128)(2,1)S(1)}, u32[]{:S(2)}, u32[]{:S(2)}) collective-permute-start(bf16[256,128]{1,0:T(8,128)(2,1)S(1)} %get-tuple-element.73), channel_id=1, source_target_pairs={{0,16},{1,17},{2,18},{3,19},{4,20},{5,21},{6,22},{7,23},{8,24},{9,... | collective-permute-start | bytes 196616 | tf_op jit(solution)/shard_map/ppermute | solution.py:153
  110.7 6.7 %collective-permute-start.1 = (bf16[512,128]{1,0:T(8,128)(2,1)S(1)}, bf16[512,128]{1,0:T(8,128)(2,1)S(1)}, u32[]{:S(2)}, u32[]{:S(2)}) collective-permute-start(bf16[512,128]{1,0:T(8,128)(2,1)S(1)} %pad_maximum_fusion.14), channel_id=1, source_target_pairs={{0,8},{1,9},{2,10},{3,11},{4,12},{5,13},{6,14},{7,15},{8,0},{9,1},... | collective-permute-start | bytes 393224 | tf_op jit(solution)/shard_map/ppermute | solution.py:153
  113.7 9.9 %collective-permute-start.6 = (bf16[512,128]{1,0:T(8,128)(2,1)S(1)}, bf16[512,128]{1,0:T(8,128)(2,1)S(1)}, u32[]{:S(2)}, u32[]{:S(2)}) collective-permute-start(bf16[512,128]{1,0:T(8,128)(2,1)S(1)} %pad_maximum_fusion.15), channel_id=1, source_target_pairs={{0,8},{1,9},{2,10},{3,11},{4,12},{5,13},{6,14},{7,15},{8,0},{9,1},... | collective-permute-start | bytes 393224 | tf_op jit(solution)/shard_map/ppermute | solution.py:153
  117.4 8.8 %collective-permute-start.2 = (bf16[1024,128]{1,0:T(8,128)(2,1)S(1)}, bf16[1024,128]{1,0:T(8,128)(2,1)S(1)}, u32[]{:S(2)}, u32[]{:S(2)}) collective-permute-start(bf16[1024,128]{1,0:T(8,128)(2,1)S(1)} %pad_maximum_fusion.10), channel_id=1, source_target_pairs={{0,2},{1,3},{2,0},{3,1},{4,6},{5,7},{6,4},{7,5},{8,10},{9,11},{10,... | collective-permute-start | bytes 786440 | tf_op jit(solution)/shard_map/ppermute | solution.py:153
  123.7 18.8 %collective-permute-start.7 = (bf16[1024,128]{1,0:T(8,128)(2,1)S(1)}, bf16[1024,128]{1,0:T(8,128)(2,1)S(1)}, u32[]{:S(2)}, u32[]{:S(2)}) collective-permute-start(bf16[1024,128]{1,0:T(8,128)(2,1)S(1)} %pad_maximum_fusion.11), channel_id=1, source_target_pairs={{0,2},{1,3},{2,0},{3,1},{4,6},{5,7},{6,4},{7,5},{8,10},{9,11},{10,... | collective-permute-start | bytes 786440 | tf_op jit(solution)/shard_map/ppermute | solution.py:153
  126.3 20.1 %collective-permute-start.3 = (bf16[2048,128]{1,0:T(8,128)(2,1)S(1)}, bf16[2048,128]{1,0:T(8,128)(2,1)S(1)}, u32[]{:S(2)}, u32[]{:S(2)}) collective-permute-start(bf16[2048,128]{1,0:T(8,128)(2,1)S(1)} %pad_maximum_fusion.3), channel_id=1, source_target_pairs={{0,4},{1,5},{2,6},{3,7},{4,0},{5,1},{6,2},{7,3},{8,12},{9,13},{10,... | collective-permute-start | bytes 1572872 | tf_op jit(solution)/shard_map/ppermute | solution.py:153
  142.5 10.2 %collective-permute-start.8 = (bf16[2048,128]{1,0:T(8,128)(2,1)S(1)}, bf16[2048,128]{1,0:T(8,128)(2,1)S(1)}, u32[]{:S(2)}, u32[]{:S(2)}) collective-permute-start(bf16[2048,128]{1,0:T(8,128)(2,1)S(1)} %pad_maximum_fusion.4), channel_id=1, source_target_pairs={{0,1},{1,0},{2,3},{3,2},{4,5},{5,4},{6,7},{7,6},{8,9},{9,8},{10,11... | collective-permute-start | bytes 1572872 | tf_op jit(solution)/shard_map/ppermute | solution.py:153
  147.4 26.9 %collective-permute-start.4 = (bf16[4096,128]{1,0:T(8,128)(2,1)}, bf16[4096,128]{1,0:T(8,128)(2,1)}, u32[]{:S(2)}, u32[]{:S(2)}) collective-permute-start(bf16[4096,128]{1,0:T(8,128)(2,1)} %get-tuple-element.45), channel_id=1, source_target_pairs={{0,1},{1,0},{2,3},{3,2},{4,5},{5,4},{6,7},{7,6},{8,9},{9,8},{10,11... | collective-permute-start | bytes 3145736 | tf_op jit(solution)/shard_map/ppermute | solution.py:153
  153.8 22.8 %collective-permute-start.9 = (bf16[4096,128]{1,0:T(8,128)(2,1)}, bf16[4096,128]{1,0:T(8,128)(2,1)}, u32[]{:S(2)}, u32[]{:S(2)}) collective-permute-start(bf16[4096,128]{1,0:T(8,128)(2,1)} %get-tuple-element.47), channel_id=1, source_target_pairs={{0,4},{1,5},{2,6},{3,7},{4,0},{5,1},{6,2},{7,3},{8,12},{9,13},{10,... | collective-permute-start | bytes 3145736 | tf_op jit(solution)/shard_map/ppermute | solution.py:153
  183.7 27.6 %collective-permute-start.10 = (bf16[32,512,128]{2,1,0:T(8,128)(2,1)}, bf16[32,512,128]{2,1,0:T(8,128)(2,1)}, u32[]{:S(2)}, u32[]{:S(2)}) collective-permute-start(bf16[32,512,128]{2,1,0:T(8,128)(2,1)} %pad_maximum_fusion.1), channel_id=1, source_target_pairs={{0,32},{32,0},{64,96},{96,64},{128,160},{160,128},{192,224},{224,1... | collective-permute-start | bytes 12582920 | tf_op jit(solution)/shard_map/ppermute | solution.py:114
  226.4 17.3 %all-to-all-start.3 = ((bf16[32,2,1024]{2,1,0:T(2,128)(2,1)}), bf16[32,2,1024]{2,1,0:T(2,128)(2,1)}, u32[]{:S(2)}, u32[]{:S(2)}) async-start(bf16[32,2,1024]{2,1,0:T(2,128)(2,1)} %reshape.280), calls=%async_computation.3 | async-start | bytes 262144 | tf_op jit(solution)/shard_map/all_to_all | solution.py:232
  272.5 9.3 %collective-permute-start.11 = (bf16[8,4096]{1,0:T(8,128)(2,1)S(1)}, bf16[8,4096]{1,0:T(8,128)(2,1)S(1)}, u32[]{:S(2)}, u32[]{:S(2)}) collective-permute-start(bf16[8,4096]{1,0:T(8,128)(2,1)S(1)} %get-tuple-element.64), channel_id=1, source_target_pairs={{0,16},{1,17},{2,18},{3,19},{4,20},{5,21},{6,22},{7,23},{8,24},{9,... | collective-permute-start | bytes 196616 | tf_op jit(solution)/shard_map/ppermute | solution.py:153
  276.6 9.6 %collective-permute-start.16 = (bf16[8,4096]{1,0:T(8,128)(2,1)S(1)}, bf16[8,4096]{1,0:T(8,128)(2,1)S(1)}, u32[]{:S(2)}, u32[]{:S(2)}) collective-permute-start(bf16[8,4096]{1,0:T(8,128)(2,1)S(1)} %get-tuple-element.63), channel_id=1, source_target_pairs={{0,16},{1,17},{2,18},{3,19},{4,20},{5,21},{6,22},{7,23},{8,24},{9,... | collective-permute-start | bytes 196616 | tf_op jit(solution)/shard_map/ppermute | solution.py:153
  281.8 10.2 %collective-permute-start.12 = (bf16[16,4096]{1,0:T(8,128)(2,1)S(1)}, bf16[16,4096]{1,0:T(8,128)(2,1)S(1)}, u32[]{:S(2)}, u32[]{:S(2)}) collective-permute-start(bf16[16,4096]{1,0:T(8,128)(2,1)S(1)} %pad_maximum_fusion.16), channel_id=1, source_target_pairs={{0,8},{1,9},{2,10},{3,11},{4,12},{5,13},{6,14},{7,15},{8,0},{9,1},... | collective-permute-start | bytes 393224 | tf_op jit(solution)/shard_map/ppermute | solution.py:153
  286.2 10.2 %collective-permute-start.17 = (bf16[16,4096]{1,0:T(8,128)(2,1)S(1)}, bf16[16,4096]{1,0:T(8,128)(2,1)S(1)}, u32[]{:S(2)}, u32[]{:S(2)}) collective-permute-start(bf16[16,4096]{1,0:T(8,128)(2,1)S(1)} %pad_maximum_fusion.17), channel_id=1, source_target_pairs={{0,8},{1,9},{2,10},{3,11},{4,12},{5,13},{6,14},{7,15},{8,0},{9,1},... | collective-permute-start | bytes 393224 | tf_op jit(solution)/shard_map/ppermute | solution.py:153
  292.0 8.5 %collective-permute-start.13 = (bf16[32,4096]{1,0:T(8,128)(2,1)S(1)}, bf16[32,4096]{1,0:T(8,128)(2,1)S(1)}, u32[]{:S(2)}, u32[]{:S(2)}) collective-permute-start(bf16[32,4096]{1,0:T(8,128)(2,1)S(1)} %pad_maximum_fusion.12), channel_id=1, source_target_pairs={{0,2},{1,3},{2,0},{3,1},{4,6},{5,7},{6,4},{7,5},{8,10},{9,11},{10,... | collective-permute-start | bytes 786440 | tf_op jit(solution)/shard_map/ppermute | solution.py:153
  296.4 25.2 %collective-permute-start.18 = (bf16[32,4096]{1,0:T(8,128)(2,1)S(1)}, bf16[32,4096]{1,0:T(8,128)(2,1)S(1)}, u32[]{:S(2)}, u32[]{:S(2)}) collective-permute-start(bf16[32,4096]{1,0:T(8,128)(2,1)S(1)} %pad_maximum_fusion.13), channel_id=1, source_target_pairs={{0,2},{1,3},{2,0},{3,1},{4,6},{5,7},{6,4},{7,5},{8,10},{9,11},{10,... | collective-permute-start | bytes 786440 | tf_op jit(solution)/shard_map/ppermute | solution.py:153
  300.5 32.7 %collective-permute-start.14 = (bf16[64,4096]{1,0:T(8,128)(2,1)S(1)}, bf16[64,4096]{1,0:T(8,128)(2,1)S(1)}, u32[]{:S(2)}, u32[]{:S(2)}) collective-permute-start(bf16[64,4096]{1,0:T(8,128)(2,1)S(1)} %pad_maximum_fusion.5), channel_id=1, source_target_pairs={{0,4},{1,5},{2,6},{3,7},{4,0},{5,1},{6,2},{7,3},{8,12},{9,13},{10,... | collective-permute-start | bytes 1572872 | tf_op jit(solution)/shard_map/ppermute | solution.py:153
  321.7 15.5 %collective-permute-start.19 = (bf16[64,4096]{1,0:T(8,128)(2,1)S(1)}, bf16[64,4096]{1,0:T(8,128)(2,1)S(1)}, u32[]{:S(2)}, u32[]{:S(2)}) collective-permute-start(bf16[64,4096]{1,0:T(8,128)(2,1)S(1)} %pad_maximum_fusion.6), channel_id=1, source_target_pairs={{0,1},{1,0},{2,3},{3,2},{4,5},{5,4},{6,7},{7,6},{8,9},{9,8},{10,11... | collective-permute-start | bytes 1572872 | tf_op jit(solution)/shard_map/ppermute | solution.py:153
  334.4 25.7 %collective-permute-start.15 = (bf16[128,4096]{1,0:T(8,128)(2,1)}, bf16[128,4096]{1,0:T(8,128)(2,1)}, u32[]{:S(2)}, u32[]{:S(2)}) collective-permute-start(bf16[128,4096]{1,0:T(8,128)(2,1)} %get-tuple-element.35), channel_id=1, source_target_pairs={{0,1},{1,0},{2,3},{3,2},{4,5},{5,4},{6,7},{7,6},{8,9},{9,8},{10,11... | collective-permute-start | bytes 3145736 | tf_op jit(solution)/shard_map/ppermute | solution.py:153
  338.3 27.1 %collective-permute-start.20 = (bf16[128,4096]{1,0:T(8,128)(2,1)}, bf16[128,4096]{1,0:T(8,128)(2,1)}, u32[]{:S(2)}, u32[]{:S(2)}) collective-permute-start(bf16[128,4096]{1,0:T(8,128)(2,1)} %get-tuple-element.37), channel_id=1, source_target_pairs={{0,4},{1,5},{2,6},{3,7},{4,0},{5,1},{6,2},{7,3},{8,12},{9,13},{10,... | collective-permute-start | bytes 3145736 | tf_op jit(solution)/shard_map/ppermute | solution.py:153
  379.7 6.8 %collective-permute-start.22 = (f32[132,256]{1,0:T(8,128)S(1)}, f32[132,256]{1,0:T(8,128)S(1)}, u32[]{:S(2)}, u32[]{:S(2)}) collective-permute-start(f32[132,256]{1,0:T(8,128)S(1)} %slice_select_fusion.1), channel_id=1, source_target_pairs={{0,128},{32,160},{64,192},{96,224},{128,0},{160,32},{192,64},{224,... | collective-permute-start | bytes 405512 | tf_op jit(solution)/shard_map/ppermute | solution.py:191
  386.5 6.6 %collective-permute-start.23 = (f32[66,256]{1,0:T(8,128)S(1)}, f32[66,256]{1,0:T(8,128)S(1)}, u32[]{:S(2)}, u32[]{:S(2)}) collective-permute-start(f32[66,256]{1,0:T(8,128)S(1)} %slice_select_fusion.2), channel_id=1, source_target_pairs={{0,256},{32,288},{64,320},{96,352},{128,384},{160,416},{192,448},{... | collective-permute-start | bytes 202760 | tf_op jit(solution)/shard_map/ppermute | solution.py:191
  393.2 8.7 %collective-permute-start.24 = (f32[33,256]{1,0:T(8,128)S(1)}, f32[33,256]{1,0:T(8,128)S(1)}, u32[]{:S(2)}, u32[]{:S(2)}) collective-permute-start(f32[33,256]{1,0:T(8,128)S(1)} %slice_select_fusion.3), channel_id=1, source_target_pairs={{0,64},{32,96},{64,0},{96,32},{128,192},{160,224},{192,128},{224,1... | collective-permute-start | bytes 101384 | tf_op jit(solution)/shard_map/ppermute | solution.py:191
  401.9 8.7 %collective-permute-start.25 = (f32[33,256]{1,0:T(8,128)S(1)}, f32[33,256]{1,0:T(8,128)S(1)}, u32[]{:S(2)}, u32[]{:S(2)}) collective-permute-start(f32[33,256]{1,0:T(8,128)S(1)} %select_add_fusion.3), channel_id=1, source_target_pairs={{0,64},{32,96},{64,0},{96,32},{128,192},{160,224},{192,128},{224,1... | collective-permute-start | bytes 101384 | tf_op jit(solution)/shard_map/ppermute | solution.py:193
  410.6 6.6 %collective-permute-start.26 = (f32[66,256]{1,0:T(8,128)S(1)}, f32[66,256]{1,0:T(8,128)S(1)}, u32[]{:S(2)}, u32[]{:S(2)}) collective-permute-start(f32[66,256]{1,0:T(8,128)S(1)} %maximum_select_fusion.3), channel_id=1, source_target_pairs={{0,256},{32,288},{64,320},{96,352},{128,384},{160,416},{192,448},{... | collective-permute-start | bytes 202760 | tf_op jit(solution)/shard_map/ppermute | solution.py:193
  423.3 10.5 %collective-permute-start.28 = (f32[264,256]{1,0:T(8,128)S(1)}, f32[264,256]{1,0:T(8,128)S(1)}, u32[]{:S(2)}, u32[]{:S(2)}) collective-permute-start(f32[264,256]{1,0:T(8,128)S(1)} %maximum_select_fusion.1), channel_id=1, source_target_pairs={{0,32},{32,0},{64,96},{96,64},{128,160},{160,128},{192,224},{224,1... | collective-permute-start | bytes 811016 | tf_op jit(solution)/shard_map/ppermute | solution.py:193
  (19 other events, 432.5 us)

commit v5 on v4

--- a/solution.py
+++ b/solution.py
@@ -206,10 +206,8 @@
     tok_rows = grad_out.shape[1]
     ctx_size = lax.axis_size("ctx")
     gather_masks = ctx_masks(ctx_size)
-    query_ch, key_ch, value_ch = (
-        lax.all_to_all(queries, "ctx", split_axis=2, concat_axis=1, tiled=True),
-        lax.all_to_all(keys, "ctx", split_axis=2, concat_axis=1, tiled=True),
-        lax.all_to_all(values, "ctx", split_axis=2, concat_axis=1, tiled=True),
+    query_ch, key_ch, value_ch = lax.all_to_all(
+        jnp.stack([queries, keys, values]), "ctx", split_axis=3, concat_axis=2, tiled=True
     )
     weight_first, weight_second, (query_ch, key_ch, value_ch) = shared_weight(
         out_weight, gather_masks, (query_ch, key_ch, value_ch)
@@ -230,8 +228,7 @@
     gated_sum = rounded_sum(terms)
     grad_gated = gated_sum.astype(jnp.bfloat16)[None]
     gated_grad_ch = lax.all_to_all(grad_gated, "ctx", split_axis=2, concat_axis=1, tiled=True)
-    grad_in, _ = lax.optimization_barrier((grad_out[0], weight_first))
-    grad_cols = columns_by_position(grad_in, block_width)
+    grad_cols = columns_by_position(grad_out[0], block_width)
     grad_gated_full = channels_first(gated_grad_ch)
     seq_len = query_ch.shape[1]
     fft_rows = 2 * seq_len // FFT_COLS

time: 444 us -> 428 us (0.964)
  the two profiles are of different devices: /device:TPU:189 before, /device:TPU:1 now
where the time goes in v5:
time: 428 us; the launch traced here: 422 us
  starting transfers between devices  170 us (40%)
  waiting for transfers between devices  126 us (29%)
  local copies, waits for them, and re-layouts  58.1 us (14%)
  matrix products  38.1 us (9%)
  other arithmetic  27.3 us (6%)
    ppermute x20, waiting for transfers between devices, doubling_gather(): lax.ppermute(held, axis, axis_pairs(size, mask))  97.3 us
    ppermute x20, starting transfers between devices, doubling_gather(): lax.ppermute(held, axis, axis_pairs(size, mask))  87 us
    ppermute x4, starting transfers between devices, summed_over_dp(): other = lax.ppermute(held, 'dp', axis_pairs(size, mask))  22.9 us
    dot_general x24, matrix products, single(): return jnp.einsum('ckm,mj->ckj', data, table, precision=HIGHEST)  20 us
    ppermute x4, starting transfers between devices, summed_over_dp(): held = keep + lax.ppermute(send, 'dp', axis_pairs(size, mask))  19.4 us
    unnamed x59, local copies, waits for them, and re-layouts  18.1 us
    all_to_all x1, starting transfers between devices, body(): lax.all_to_all(jnp.stack([queries, keys, values]), 'ctx', split_axis=3, c...  14.3 us
    concatenate x8, local copies, waits for them, and re-layouts, doubling_gather(): jnp.concatenate([held, lax.ppermute(held, axis, axis_pairs(size, mask))],...  13.6 us
  transfers between devices with their start and end apart: 32, of which 22 were waited for; matrix products, arithmetic and copies ran while one was open for 19% of the time, Pallas kernels for 0%

profile of v5, /device:TPU:1, one launch (start us, length us, event | category | flops | bytes accessed | tf_op | source)
XLA Modules:
  0.0 421.7 jit_solution(3742544066074946048)
XLA Ops:
  3.0 14.3 %all-to-all-start = ((bf16[3,1,128,512]{2,0,1,3:T(4,128)(2,1)}), bf16[3,1,128,512]{2,0,1,3:T(4,128)(2,1)S(1)}, u32[]{:S(2)}, u32[]{:S(2)}) async-start(bf16[3,1,128,512]{2,0,1,3:T(4,128)(2,1)} %copy.81), calls=%async_computation | async-start | bytes 1048576 | tf_op jit(solution)/shard_map/all_to_all | solution.py:209
  19.8 12.5 %all-to-all-done = bf16[3,1,128,512]{2,0,1,3:T(4,128)(2,1)S(1)} async-done(((bf16[3,1,128,512]{2,0,1,3:T(4,128)(2,1)}), bf16[3,1,128,512]{2,0,1,3:T(4,128)(2,1)S(1)}, u32[]{:S(2)}, u32[]{:S(2)}) %all-to-all-start) | async-done | bytes 393248 | tf_op jit(solution)/shard_map/all_to_all | solution.py:209
  32.3 6.9 %all-to-all-start.2 = ((bf16[32,128,256]{1,2,0:T(8,128)(2,1)}), bf16[32,128,256]{1,2,0:T(8,128)(2,1)}, u32[]{:S(2)}, u32[]{:S(2)}) async-start(bf16[32,128,256]{1,2,0:T(8,128)(2,1)} %bitcast.46), calls=%async_computation.2 | async-start | bytes 4194304 | tf_op jit(solution)/shard_map/all_to_all | solution.py:100
  40.4 7.0 %collective-permute-start = (bf16[256,128]{1,0:T(8,128)(2,1)S(1)}, bf16[256,128]{1,0:T(8,128)(2,1)S(1)}, u32[]{:S(2)}, u32[]{:S(2)}) collective-permute-start(bf16[256,128]{1,0:T(8,128)(2,1)S(1)} %get-tuple-element.75), channel_id=1, source_target_pairs={{0,16},{1,17},{2,18},{3,19},{4,20},{5,21},{6,22},{7,23},{8,24},{9,... | collective-permute-start | bytes 196616 | tf_op jit(solution)/shard_map/ppermute | solution.py:153
  49.7 42.7 %collective-permute-done = bf16[256,128]{1,0:T(8,128)(2,1)S(1)} collective-permute-done((bf16[256,128]{1,0:T(8,128)(2,1)S(1)}, bf16[256,128]{1,0:T(8,128)(2,1)S(1)}, u32[]{:S(2)}, u32[]{:S(2)}) %collective-permute-start) | collective-permute-done | bytes 65568 | tf_op jit(solution)/shard_map/ppermute | solution.py:153
  95.3 3.3 collective-permute-start.6
  99.2 6.8 %collective-permute-start.2 = (bf16[1024,128]{1,0:T(8,128)(2,1)S(1)}, bf16[1024,128]{1,0:T(8,128)(2,1)S(1)}, u32[]{:S(2)}, u32[]{:S(2)}) collective-permute-start(bf16[1024,128]{1,0:T(8,128)(2,1)S(1)} %pad_maximum_fusion.11), channel_id=1, source_target_pairs={{0,2},{1,3},{2,0},{3,1},{4,6},{5,7},{6,4},{7,5},{8,10},{9,11},{10,... | collective-permute-start | bytes 786440 | tf_op jit(solution)/shard_map/ppermute | solution.py:153
  107.5 4.2 %collective-permute-start.7 = (bf16[1024,128]{1,0:T(8,128)(2,1)S(1)}, bf16[1024,128]{1,0:T(8,128)(2,1)S(1)}, u32[]{:S(2)}, u32[]{:S(2)}) collective-permute-start(bf16[1024,128]{1,0:T(8,128)(2,1)S(1)} %pad_maximum_fusion.12), channel_id=1, source_target_pairs={{0,2},{1,3},{2,0},{3,1},{4,6},{5,7},{6,4},{7,5},{8,10},{9,11},{10,... | collective-permute-start | bytes 786440 | tf_op jit(solution)/shard_map/ppermute | solution.py:153
  114.4 12.5 %collective-permute-done.7 = bf16[1024,128]{1,0:T(8,128)(2,1)S(1)} collective-permute-done((bf16[1024,128]{1,0:T(8,128)(2,1)S(1)}, bf16[1024,128]{1,0:T(8,128)(2,1)S(1)}, u32[]{:S(2)}, u32[]{:S(2)}) %collective-permute-start.7) | collective-permute-done | bytes 262176 | tf_op jit(solution)/shard_map/ppermute | solution.py:153
  131.9 5.9 %collective-permute-start.4 = (bf16[4096,128]{1,0:T(8,128)(2,1)}, bf16[4096,128]{1,0:T(8,128)(2,1)}, u32[]{:S(2)}, u32[]{:S(2)}) collective-permute-start(bf16[4096,128]{1,0:T(8,128)(2,1)} %get-tuple-element.43), channel_id=1, source_target_pairs={{0,1},{1,0},{2,3},{3,2},{4,5},{5,4},{6,7},{7,6},{8,9},{9,8},{10,11... | collective-permute-start | bytes 3145736 | tf_op jit(solution)/shard_map/ppermute | solution.py:153
  140.2 4.2 collective-permute-start.9
  149.9 11.9 %collective-permute-done.4 = bf16[4096,128]{1,0:T(8,128)(2,1)} collective-permute-done((bf16[4096,128]{1,0:T(8,128)(2,1)}, bf16[4096,128]{1,0:T(8,128)(2,1)}, u32[]{:S(2)}, u32[]{:S(2)}) %collective-permute-start.4) | collective-permute-done | bytes 1048608 | tf_op jit(solution)/shard_map/ppermute | solution.py:153
  166.4 4.8 %pad_maximum_fusion.1 = bf16[32,512,128]{2,1,0:T(8,128)(2,1)} fusion(bf16[32,256,128]{2,1,0:T(8,128)(2,1)} %bitcast.10, bf16[32,256,128]{2,1,0:T(8,128)(2,1)} %bitcast.9), kind=kLoop, calls=%fused_computation.9 | loop fusion | flops 8388608 | bytes 8388608 | tf_op jit(solution)/shard_map/concatenate | solution.py:113
  171.2 6.8 %collective-permute-start.10 = (bf16[32,512,128]{2,1,0:T(8,128)(2,1)}, bf16[32,512,128]{2,1,0:T(8,128)(2,1)}, u32[]{:S(2)}, u32[]{:S(2)}) collective-permute-start(bf16[32,512,128]{2,1,0:T(8,128)(2,1)} %pad_maximum_fusion.1), channel_id=1, source_target_pairs={{0,32},{32,0},{64,96},{96,64},{128,160},{160,128},{192,224},{224,1... | collective-permute-start | bytes 12582920 | tf_op jit(solution)/shard_map/ppermute | solution.py:114
  179.5 4.1 copy.80
  195.8 4.6 %pad_maximum_fusion = bf16[32,512,256]{2,1,0:T(8,128)(2,1)S(1)} fusion(bf16[32,512,128]{2,1,0:T(8,128)(2,1)} %collective-permute-done.10, bf16[32,256,128]{2,1,0:T(8,128)(2,1)} %bitcast.10, bf16[32,256,128]{2,1,0:T(8,128)(2,1)} %bitcast.9), kind=kLoop, calls=%fused_computation.4 | loop fusion | flops 25165824 | bytes 16777216 | tf_op jit(solution)/shard_map/concatenate | solution.py:115
  211.5 12.4 %all-to-all-start.1 = ((bf16[32,2,1024]{2,1,0:T(2,128)(2,1)}), bf16[32,2,1024]{2,1,0:T(2,128)(2,1)}, u32[]{:S(2)}, u32[]{:S(2)}) async-start(bf16[32,2,1024]{2,1,0:T(2,128)(2,1)} %reshape.276), calls=%async_computation.1 | async-start | bytes 262144 | tf_op jit(solution)/shard_map/all_to_all | solution.py:230
  224.7 3.5 copy.94
  228.2 5.7 %all-to-all-done.1 = bf16[32,2,1024]{2,1,0:T(2,128)(2,1)} async-done(((bf16[32,2,1024]{2,1,0:T(2,128)(2,1)}), bf16[32,2,1024]{2,1,0:T(2,128)(2,1)}, u32[]{:S(2)}, u32[]{:S(2)}) %all-to-all-start.1) | async-done | bytes 131104 | tf_op jit(solution)/shard_map/all_to_all | solution.py:230
  265.4 6.5 %collective-permute-start.16 = (bf16[8,4096]{1,0:T(8,128)(2,1)S(1)}, bf16[8,4096]{1,0:T(8,128)(2,1)S(1)}, u32[]{:S(2)}, u32[]{:S(2)}) collective-permute-start(bf16[8,4096]{1,0:T(8,128)(2,1)S(1)} %get-tuple-element.64), channel_id=1, source_target_pairs={{0,16},{1,17},{2,18},{3,19},{4,20},{5,21},{6,22},{7,23},{8,24},{9,... | collective-permute-start | bytes 196616 | tf_op jit(solution)/shard_map/ppermute | solution.py:153
  275.0 4.2 collective-permute-start.17
  282.8 4.5 %collective-permute-done.17 = bf16[16,4096]{1,0:T(8,128)(2,1)S(1)} collective-permute-done((bf16[16,4096]{1,0:T(8,128)(2,1)S(1)}, bf16[16,4096]{1,0:T(8,128)(2,1)S(1)}, u32[]{:S(2)}, u32[]{:S(2)}) %collective-permute-start.17) | collective-permute-done | bytes 131104 | tf_op jit(solution)/shard_map/ppermute | solution.py:153
  292.0 15.5 %collective-permute-start.14 = (bf16[64,4096]{1,0:T(8,128)(2,1)S(1)}, bf16[64,4096]{1,0:T(8,128)(2,1)S(1)}, u32[]{:S(2)}, u32[]{:S(2)}) collective-permute-start(bf16[64,4096]{1,0:T(8,128)(2,1)S(1)} %pad_maximum_fusion.5), channel_id=1, source_target_pairs={{0,4},{1,5},{2,6},{3,7},{4,0},{5,1},{6,2},{7,3},{8,12},{9,13},{10,... | collective-permute-start | bytes 1572872 | tf_op jit(solution)/shard_map/ppermute | solution.py:153
  310.4 7.0 %collective-permute-done.14 = bf16[64,4096]{1,0:T(8,128)(2,1)S(1)} collective-permute-done((bf16[64,4096]{1,0:T(8,128)(2,1)S(1)}, bf16[64,4096]{1,0:T(8,128)(2,1)S(1)}, u32[]{:S(2)}, u32[]{:S(2)}) %collective-permute-start.14) | collective-permute-done | bytes 524320 | tf_op jit(solution)/shard_map/ppermute | solution.py:153
  322.5 6.9 %collective-permute-start.20 = (bf16[128,4096]{1,0:T(8,128)(2,1)}, bf16[128,4096]{1,0:T(8,128)(2,1)}, u32[]{:S(2)}, u32[]{:S(2)}) collective-permute-start(bf16[128,4096]{1,0:T(8,128)(2,1)} %get-tuple-element.35), channel_id=1, source_target_pairs={{0,4},{1,5},{2,6},{3,7},{4,0},{5,1},{6,2},{7,3},{8,12},{9,13},{10,... | collective-permute-start | bytes 3145736 | tf_op jit(solution)/shard_map/ppermute | solution.py:153
  329.6 13.0 %collective-permute-done.15 = bf16[128,4096]{1,0:T(8,128)(2,1)} collective-permute-done((bf16[128,4096]{1,0:T(8,128)(2,1)}, bf16[128,4096]{1,0:T(8,128)(2,1)}, u32[]{:S(2)}, u32[]{:S(2)}) %collective-permute-start.15) | collective-permute-done | bytes 1048608 | tf_op jit(solution)/shard_map/ppermute | solution.py:153
  359.6 4.8 %collective-permute-start.21 = (f32[264,256]{1,0:T(8,128)S(1)}, f32[264,256]{1,0:T(8,128)S(1)}, u32[]{:S(2)}, u32[]{:S(2)}) collective-permute-start(f32[264,256]{1,0:T(8,128)S(1)} %slice_select_fusion), channel_id=1, source_target_pairs={{0,32},{32,0},{64,96},{96,64},{128,160},{160,128},{192,224},{224,1... | collective-permute-start | bytes 811016 | tf_op jit(solution)/shard_map/ppermute | solution.py:191
  372.5 4.7 %collective-permute-start.23 = (f32[66,256]{1,0:T(8,128)S(1)}, f32[66,256]{1,0:T(8,128)S(1)}, u32[]{:S(2)}, u32[]{:S(2)}) collective-permute-start(f32[66,256]{1,0:T(8,128)S(1)} %slice_select_fusion.2), channel_id=1, source_target_pairs={{0,256},{32,288},{64,320},{96,352},{128,384},{160,416},{192,448},{... | collective-permute-start | bytes 202760 | tf_op jit(solution)/shard_map/ppermute | solution.py:191
  379.2 6.7 %collective-permute-start.24 = (f32[33,256]{1,0:T(8,128)S(1)}, f32[33,256]{1,0:T(8,128)S(1)}, u32[]{:S(2)}, u32[]{:S(2)}) collective-permute-start(f32[33,256]{1,0:T(8,128)S(1)} %slice_select_fusion.3), channel_id=1, source_target_pairs={{0,64},{32,96},{64,0},{96,32},{128,192},{160,224},{192,128},{224,1... | collective-permute-start | bytes 101384 | tf_op jit(solution)/shard_map/ppermute | solution.py:191
  387.8 6.7 %collective-permute-start.25 = (f32[33,256]{1,0:T(8,128)S(1)}, f32[33,256]{1,0:T(8,128)S(1)}, u32[]{:S(2)}, u32[]{:S(2)}) collective-permute-start(f32[33,256]{1,0:T(8,128)S(1)} %select_add_fusion.3), channel_id=1, source_target_pairs={{0,64},{32,96},{64,0},{96,32},{128,192},{160,224},{192,128},{224,1... | collective-permute-start | bytes 101384 | tf_op jit(solution)/shard_map/ppermute | solution.py:193
  396.5 4.7 %collective-permute-start.26 = (f32[66,256]{1,0:T(8,128)S(1)}, f32[66,256]{1,0:T(8,128)S(1)}, u32[]{:S(2)}, u32[]{:S(2)}) collective-permute-start(f32[66,256]{1,0:T(8,128)S(1)} %maximum_select_fusion.3), channel_id=1, source_target_pairs={{0,256},{32,288},{64,320},{96,352},{128,384},{160,416},{192,448},{... | collective-permute-start | bytes 202760 | tf_op jit(solution)/shard_map/ppermute | solution.py:193
  409.8 8.3 %collective-permute-start.28 = (f32[264,256]{1,0:T(8,128)S(1)}, f32[264,256]{1,0:T(8,128)S(1)}, u32[]{:S(2)}, u32[]{:S(2)}) collective-permute-start(f32[264,256]{1,0:T(8,128)S(1)} %maximum_select_fusion.1), channel_id=1, source_target_pairs={{0,32},{32,0},{64,96},{96,64},{128,160},{160,128},{192,224},{224,1... | collective-permute-start | bytes 811016 | tf_op jit(solution)/shard_map/ppermute | solution.py:193
  (232 shorter events, 152.0 us)
Async XLA Ops:
  3.0 29.3 %all-to-all-start = ((bf16[3,1,128,512]{2,0,1,3:T(4,128)(2,1)}), bf16[3,1,128,512]{2,0,1,3:T(4,128)(2,1)S(1)}, u32[]{:S(2)}, u32[]{:S(2)}) async-start(bf16[3,1,128,512]{2,0,1,3:T(4,128)(2,1)} %copy.81), calls=%async_computation | async-start | bytes 1048576 | tf_op jit(solution)/shard_map/all_to_all | solution.py:209
  32.3 179.2 %all-to-all-start.2 = ((bf16[32,128,256]{1,2,0:T(8,128)(2,1)}), bf16[32,128,256]{1,2,0:T(8,128)(2,1)}, u32[]{:S(2)}, u32[]{:S(2)}) async-start(bf16[32,128,256]{1,2,0:T(8,128)(2,1)} %bitcast.46), calls=%async_computation.2 | async-start | bytes 4194304 | tf_op jit(solution)/shard_map/all_to_all | solution.py:100
  40.4 51.9 %collective-permute-start = (bf16[256,128]{1,0:T(8,128)(2,1)S(1)}, bf16[256,128]{1,0:T(8,128)(2,1)S(1)}, u32[]{:S(2)}, u32[]{:S(2)}) collective-permute-start(bf16[256,128]{1,0:T(8,128)(2,1)S(1)} %get-tuple-element.75), channel_id=1, source_target_pairs={{0,16},{1,17},{2,18},{3,19},{4,20},{5,21},{6,22},{7,23},{8,24},{9,... | collective-permute-start | bytes 196616 | tf_op jit(solution)/shard_map/ppermute | solution.py:153
  47.4 47.9 %collective-permute-start.5 = (bf16[256,128]{1,0:T(8,128)(2,1)S(1)}, bf16[256,128]{1,0:T(8,128)(2,1)S(1)}, u32[]{:S(2)}, u32[]{:S(2)}) collective-permute-start(bf16[256,128]{1,0:T(8,128)(2,1)S(1)} %get-tuple-element.74), channel_id=1, source_target_pairs={{0,16},{1,17},{2,18},{3,19},{4,20},{5,21},{6,22},{7,23},{8,24},{9,... | collective-permute-start | bytes 196616 | tf_op jit(solution)/shard_map/ppermute | solution.py:153
  92.4 6.9 %collective-permute-start.1 = (bf16[512,128]{1,0:T(8,128)(2,1)S(1)}, bf16[512,128]{1,0:T(8,128)(2,1)S(1)}, u32[]{:S(2)}, u32[]{:S(2)}) collective-permute-start(bf16[512,128]{1,0:T(8,128)(2,1)S(1)} %pad_maximum_fusion.15), channel_id=1, source_target_pairs={{0,8},{1,9},{2,10},{3,11},{4,12},{5,13},{6,14},{7,15},{8,0},{9,1},... | collective-permute-start | bytes 393224 | tf_op jit(solution)/shard_map/ppermute | solution.py:153
  95.3 12.1 %collective-permute-start.6 = (bf16[512,128]{1,0:T(8,128)(2,1)S(1)}, bf16[512,128]{1,0:T(8,128)(2,1)S(1)}, u32[]{:S(2)}, u32[]{:S(2)}) collective-permute-start(bf16[512,128]{1,0:T(8,128)(2,1)S(1)} %pad_maximum_fusion.16), channel_id=1, source_target_pairs={{0,8},{1,9},{2,10},{3,11},{4,12},{5,13},{6,14},{7,15},{8,0},{9,1},... | collective-permute-start | bytes 393224 | tf_op jit(solution)/shard_map/ppermute | solution.py:153
  99.2 12.4 %collective-permute-start.2 = (bf16[1024,128]{1,0:T(8,128)(2,1)S(1)}, bf16[1024,128]{1,0:T(8,128)(2,1)S(1)}, u32[]{:S(2)}, u32[]{:S(2)}) collective-permute-start(bf16[1024,128]{1,0:T(8,128)(2,1)S(1)} %pad_maximum_fusion.11), channel_id=1, source_target_pairs={{0,2},{1,3},{2,0},{3,1},{4,6},{5,7},{6,4},{7,5},{8,10},{9,11},{10,... | collective-permute-start | bytes 786440 | tf_op jit(solution)/shard_map/ppermute | solution.py:153
  107.5 19.5 %collective-permute-start.7 = (bf16[1024,128]{1,0:T(8,128)(2,1)S(1)}, bf16[1024,128]{1,0:T(8,128)(2,1)S(1)}, u32[]{:S(2)}, u32[]{:S(2)}) collective-permute-start(bf16[1024,128]{1,0:T(8,128)(2,1)S(1)} %pad_maximum_fusion.12), channel_id=1, source_target_pairs={{0,2},{1,3},{2,0},{3,1},{4,6},{5,7},{6,4},{7,5},{8,10},{9,11},{10,... | collective-permute-start | bytes 786440 | tf_op jit(solution)/shard_map/ppermute | solution.py:153
  111.7 19.1 %collective-permute-start.3 = (bf16[2048,128]{1,0:T(8,128)(2,1)S(1)}, bf16[2048,128]{1,0:T(8,128)(2,1)S(1)}, u32[]{:S(2)}, u32[]{:S(2)}) collective-permute-start(bf16[2048,128]{1,0:T(8,128)(2,1)S(1)} %pad_maximum_fusion.3), channel_id=1, source_target_pairs={{0,4},{1,5},{2,6},{3,7},{4,0},{5,1},{6,2},{7,3},{8,12},{9,13},{10,... | collective-permute-start | bytes 1572872 | tf_op jit(solution)/shard_map/ppermute | solution.py:153
  127.0 12.1 %collective-permute-start.8 = (bf16[2048,128]{1,0:T(8,128)(2,1)S(1)}, bf16[2048,128]{1,0:T(8,128)(2,1)S(1)}, u32[]{:S(2)}, u32[]{:S(2)}) collective-permute-start(bf16[2048,128]{1,0:T(8,128)(2,1)S(1)} %pad_maximum_fusion.4), channel_id=1, source_target_pairs={{0,1},{1,0},{2,3},{3,2},{4,5},{5,4},{6,7},{7,6},{8,9},{9,8},{10,11... | collective-permute-start | bytes 1572872 | tf_op jit(solution)/shard_map/ppermute | solution.py:153
  131.9 29.9 %collective-permute-start.4 = (bf16[4096,128]{1,0:T(8,128)(2,1)}, bf16[4096,128]{1,0:T(8,128)(2,1)}, u32[]{:S(2)}, u32[]{:S(2)}) collective-permute-start(bf16[4096,128]{1,0:T(8,128)(2,1)} %get-tuple-element.43), channel_id=1, source_target_pairs={{0,1},{1,0},{2,3},{3,2},{4,5},{5,4},{6,7},{7,6},{8,9},{9,8},{10,11... | collective-permute-start | bytes 3145736 | tf_op jit(solution)/shard_map/ppermute | solution.py:153
  140.2 23.9 %collective-permute-start.9 = (bf16[4096,128]{1,0:T(8,128)(2,1)}, bf16[4096,128]{1,0:T(8,128)(2,1)}, u32[]{:S(2)}, u32[]{:S(2)}) collective-permute-start(bf16[4096,128]{1,0:T(8,128)(2,1)} %get-tuple-element.45), channel_id=1, source_target_pairs={{0,4},{1,5},{2,6},{3,7},{4,0},{5,1},{6,2},{7,3},{8,12},{9,13},{10,... | collective-permute-start | bytes 3145736 | tf_op jit(solution)/shard_map/ppermute | solution.py:153
  171.2 24.6 %collective-permute-start.10 = (bf16[32,512,128]{2,1,0:T(8,128)(2,1)}, bf16[32,512,128]{2,1,0:T(8,128)(2,1)}, u32[]{:S(2)}, u32[]{:S(2)}) collective-permute-start(bf16[32,512,128]{2,1,0:T(8,128)(2,1)} %pad_maximum_fusion.1), channel_id=1, source_target_pairs={{0,32},{32,0},{64,96},{96,64},{128,160},{160,128},{192,224},{224,1... | collective-permute-start | bytes 12582920 | tf_op jit(solution)/shard_map/ppermute | solution.py:114
  211.5 22.3 %all-to-all-start.1 = ((bf16[32,2,1024]{2,1,0:T(2,128)(2,1)}), bf16[32,2,1024]{2,1,0:T(2,128)(2,1)}, u32[]{:S(2)}, u32[]{:S(2)}) async-start(bf16[32,2,1024]{2,1,0:T(2,128)(2,1)} %reshape.276), calls=%async_computation.1 | async-start | bytes 262144 | tf_op jit(solution)/shard_map/all_to_all | solution.py:230
  262.6 9.6 %collective-permute-start.11 = (bf16[8,4096]{1,0:T(8,128)(2,1)S(1)}, bf16[8,4096]{1,0:T(8,128)(2,1)S(1)}, u32[]{:S(2)}, u32[]{:S(2)}) collective-permute-start(bf16[8,4096]{1,0:T(8,128)(2,1)S(1)} %get-tuple-element.65), channel_id=1, source_target_pairs={{0,16},{1,17},{2,18},{3,19},{4,20},{5,21},{6,22},{7,23},{8,24},{9,... | collective-permute-start | bytes 196616 | tf_op jit(solution)/shard_map/ppermute | solution.py:153
  265.4 9.6 %collective-permute-start.16 = (bf16[8,4096]{1,0:T(8,128)(2,1)S(1)}, bf16[8,4096]{1,0:T(8,128)(2,1)S(1)}, u32[]{:S(2)}, u32[]{:S(2)}) collective-permute-start(bf16[8,4096]{1,0:T(8,128)(2,1)S(1)} %get-tuple-element.64), channel_id=1, source_target_pairs={{0,16},{1,17},{2,18},{3,19},{4,20},{5,21},{6,22},{7,23},{8,24},{9,... | collective-permute-start | bytes 196616 | tf_op jit(solution)/shard_map/ppermute | solution.py:153
  272.3 8.3 %collective-permute-start.12 = (bf16[16,4096]{1,0:T(8,128)(2,1)S(1)}, bf16[16,4096]{1,0:T(8,128)(2,1)S(1)}, u32[]{:S(2)}, u32[]{:S(2)}) collective-permute-start(bf16[16,4096]{1,0:T(8,128)(2,1)S(1)} %pad_maximum_fusion.17), channel_id=1, source_target_pairs={{0,8},{1,9},{2,10},{3,11},{4,12},{5,13},{6,14},{7,15},{8,0},{9,1},... | collective-permute-start | bytes 393224 | tf_op jit(solution)/shard_map/ppermute | solution.py:153
  275.0 12.3 %collective-permute-start.17 = (bf16[16,4096]{1,0:T(8,128)(2,1)S(1)}, bf16[16,4096]{1,0:T(8,128)(2,1)S(1)}, u32[]{:S(2)}, u32[]{:S(2)}) collective-permute-start(bf16[16,4096]{1,0:T(8,128)(2,1)S(1)} %pad_maximum_fusion.18), channel_id=1, source_target_pairs={{0,8},{1,9},{2,10},{3,11},{4,12},{5,13},{6,14},{7,15},{8,0},{9,1},... | collective-permute-start | bytes 393224 | tf_op jit(solution)/shard_map/ppermute | solution.py:153
  280.6 11.4 %collective-permute-start.13 = (bf16[32,4096]{1,0:T(8,128)(2,1)S(1)}, bf16[32,4096]{1,0:T(8,128)(2,1)S(1)}, u32[]{:S(2)}, u32[]{:S(2)}) collective-permute-start(bf16[32,4096]{1,0:T(8,128)(2,1)S(1)} %pad_maximum_fusion.13), channel_id=1, source_target_pairs={{0,2},{1,3},{2,0},{3,1},{4,6},{5,7},{6,4},{7,5},{8,10},{9,11},{10,... | collective-permute-start | bytes 786440 | tf_op jit(solution)/shard_map/ppermute | solution.py:153
  287.4 20.2 %collective-permute-start.18 = (bf16[32,4096]{1,0:T(8,128)(2,1)S(1)}, bf16[32,4096]{1,0:T(8,128)(2,1)S(1)}, u32[]{:S(2)}, u32[]{:S(2)}) collective-permute-start(bf16[32,4096]{1,0:T(8,128)(2,1)S(1)} %pad_maximum_fusion.14), channel_id=1, source_target_pairs={{0,2},{1,3},{2,0},{3,1},{4,6},{5,7},{6,4},{7,5},{8,10},{9,11},{10,... | collective-permute-start | bytes 786440 | tf_op jit(solution)/shard_map/ppermute | solution.py:153
  292.0 25.4 %collective-permute-start.14 = (bf16[64,4096]{1,0:T(8,128)(2,1)S(1)}, bf16[64,4096]{1,0:T(8,128)(2,1)S(1)}, u32[]{:S(2)}, u32[]{:S(2)}) collective-permute-start(bf16[64,4096]{1,0:T(8,128)(2,1)S(1)} %pad_maximum_fusion.5), channel_id=1, source_target_pairs={{0,4},{1,5},{2,6},{3,7},{4,0},{5,1},{6,2},{7,3},{8,12},{9,13},{10,... | collective-permute-start | bytes 1572872 | tf_op jit(solution)/shard_map/ppermute | solution.py:153
  307.6 13.7 %collective-permute-start.19 = (bf16[64,4096]{1,0:T(8,128)(2,1)S(1)}, bf16[64,4096]{1,0:T(8,128)(2,1)S(1)}, u32[]{:S(2)}, u32[]{:S(2)}) collective-permute-start(bf16[64,4096]{1,0:T(8,128)(2,1)S(1)} %pad_maximum_fusion.6), channel_id=1, source_target_pairs={{0,1},{1,0},{2,3},{3,2},{4,5},{5,4},{6,7},{7,6},{8,9},{9,8},{10,11... | collective-permute-start | bytes 1572872 | tf_op jit(solution)/shard_map/ppermute | solution.py:153
  318.6 24.1 %collective-permute-start.15 = (bf16[128,4096]{1,0:T(8,128)(2,1)}, bf16[128,4096]{1,0:T(8,128)(2,1)}, u32[]{:S(2)}, u32[]{:S(2)}) collective-permute-start(bf16[128,4096]{1,0:T(8,128)(2,1)} %get-tuple-element.33), channel_id=1, source_target_pairs={{0,1},{1,0},{2,3},{3,2},{4,5},{5,4},{6,7},{7,6},{8,9},{9,8},{10,11... | collective-permute-start | bytes 3145736 | tf_op jit(solution)/shard_map/ppermute | solution.py:153
  322.5 28.3 %collective-permute-start.20 = (bf16[128,4096]{1,0:T(8,128)(2,1)}, bf16[128,4096]{1,0:T(8,128)(2,1)}, u32[]{:S(2)}, u32[]{:S(2)}) collective-permute-start(bf16[128,4096]{1,0:T(8,128)(2,1)} %get-tuple-element.35), channel_id=1, source_target_pairs={{0,4},{1,5},{2,6},{3,7},{4,0},{5,1},{6,2},{7,3},{8,12},{9,13},{10,... | collective-permute-start | bytes 3145736 | tf_op jit(solution)/shard_map/ppermute | solution.py:153
  359.6 5.9 %collective-permute-start.21 = (f32[264,256]{1,0:T(8,128)S(1)}, f32[264,256]{1,0:T(8,128)S(1)}, u32[]{:S(2)}, u32[]{:S(2)}) collective-permute-start(f32[264,256]{1,0:T(8,128)S(1)} %slice_select_fusion), channel_id=1, source_target_pairs={{0,32},{32,0},{64,96},{96,64},{128,160},{160,128},{192,224},{224,1... | collective-permute-start | bytes 811016 | tf_op jit(solution)/shard_map/ppermute | solution.py:191
  365.7 6.8 %collective-permute-start.22 = (f32[132,256]{1,0:T(8,128)S(1)}, f32[132,256]{1,0:T(8,128)S(1)}, u32[]{:S(2)}, u32[]{:S(2)}) collective-permute-start(f32[132,256]{1,0:T(8,128)S(1)} %slice_select_fusion.1), channel_id=1, source_target_pairs={{0,128},{32,160},{64,192},{96,224},{128,0},{160,32},{192,64},{224,... | collective-permute-start | bytes 405512 | tf_op jit(solution)/shard_map/ppermute | solution.py:191
  372.5 6.6 %collective-permute-start.23 = (f32[66,256]{1,0:T(8,128)S(1)}, f32[66,256]{1,0:T(8,128)S(1)}, u32[]{:S(2)}, u32[]{:S(2)}) collective-permute-start(f32[66,256]{1,0:T(8,128)S(1)} %slice_select_fusion.2), channel_id=1, source_target_pairs={{0,256},{32,288},{64,320},{96,352},{128,384},{160,416},{192,448},{... | collective-permute-start | bytes 202760 | tf_op jit(solution)/shard_map/ppermute | solution.py:191
  379.2 8.7 %collective-permute-start.24 = (f32[33,256]{1,0:T(8,128)S(1)}, f32[33,256]{1,0:T(8,128)S(1)}, u32[]{:S(2)}, u32[]{:S(2)}) collective-permute-start(f32[33,256]{1,0:T(8,128)S(1)} %slice_select_fusion.3), channel_id=1, source_target_pairs={{0,64},{32,96},{64,0},{96,32},{128,192},{160,224},{192,128},{224,1... | collective-permute-start | bytes 101384 | tf_op jit(solution)/shard_map/ppermute | solution.py:191
  387.8 8.7 %collective-permute-start.25 = (f32[33,256]{1,0:T(8,128)S(1)}, f32[33,256]{1,0:T(8,128)S(1)}, u32[]{:S(2)}, u32[]{:S(2)}) collective-permute-start(f32[33,256]{1,0:T(8,128)S(1)} %select_add_fusion.3), channel_id=1, source_target_pairs={{0,64},{32,96},{64,0},{96,32},{128,192},{160,224},{192,128},{224,1... | collective-permute-start | bytes 101384 | tf_op jit(solution)/shard_map/ppermute | solution.py:193
  396.5 6.6 %collective-permute-start.26 = (f32[66,256]{1,0:T(8,128)S(1)}, f32[66,256]{1,0:T(8,128)S(1)}, u32[]{:S(2)}, u32[]{:S(2)}) collective-permute-start(f32[66,256]{1,0:T(8,128)S(1)} %maximum_select_fusion.3), channel_id=1, source_target_pairs={{0,256},{32,288},{64,320},{96,352},{128,384},{160,416},{192,448},{... | collective-permute-start | bytes 202760 | tf_op jit(solution)/shard_map/ppermute | solution.py:193
  403.1 6.6 %collective-permute-start.27 = (f32[132,256]{1,0:T(8,128)S(1)}, f32[132,256]{1,0:T(8,128)S(1)}, u32[]{:S(2)}, u32[]{:S(2)}) collective-permute-start(f32[132,256]{1,0:T(8,128)S(1)} %maximum_select_fusion.2), channel_id=1, source_target_pairs={{0,128},{32,160},{64,192},{96,224},{128,0},{160,32},{192,64},{224,... | collective-permute-start | bytes 405512 | tf_op jit(solution)/shard_map/ppermute | solution.py:193
  409.8 9.5 %collective-permute-start.28 = (f32[264,256]{1,0:T(8,128)S(1)}, f32[264,256]{1,0:T(8,128)S(1)}, u32[]{:S(2)}, u32[]{:S(2)}) collective-permute-start(f32[264,256]{1,0:T(8,128)S(1)} %maximum_select_fusion.1), channel_id=1, source_target_pairs={{0,32},{32,0},{64,96},{96,64},{128,160},{160,128},{192,224},{224,1... | collective-permute-start | bytes 811016 | tf_op jit(solution)/shard_map/ppermute | solution.py:193
  (16 other events, 344.4 us)

commit v6 on v5

--- a/solution.py
+++ b/solution.py
@@ -165,9 +165,13 @@
     return jnp.take(blocks, place, axis=0).reshape(rows.shape)
 
 
-def dp_masks(size):
+def dp_groups(size):
     bits = [1 << b for b in range(size.bit_length() - 1)]
-    return tuple(bits[:1]) + tuple(bits[2:]) + tuple(bits[1:2])
+    return ((bits[2], bits[3]), (bits[0], bits[1]))
+
+
+def group_partner(pair, offset):
+    return (pair[0] if offset & 1 else 0) | (pair[1] if offset & 2 else 0)
 
 
 def summed_over_dp(grad_weight, grad_residues, grad_decays):
@@ -181,18 +185,23 @@
         [grad_weight, extra, jnp.zeros((padded_rows - rows, width), jnp.float32)], axis=0
     )
     me = lax.axis_index("dp")
-    masks = dp_masks(size)
-    for mask in masks:
-        half = held.shape[0] // 2
-        low, high = held[:half], held[half:]
-        upper = (me & mask) != 0
-        keep = jnp.where(upper, high, low)
-        send = jnp.where(upper, low, high)
-        held = keep + lax.ppermute(send, "dp", axis_pairs(size, mask))
-    for mask in reversed(masks):
-        other = lax.ppermute(held, "dp", axis_pairs(size, mask))
-        upper = (me & mask) != 0
-        held = jnp.where(upper, jnp.concatenate([other, held]), jnp.concatenate([held, other]))
+    groups = dp_groups(size)
+    for pair in groups:
+        mine = ((me & pair[0]) != 0).astype(jnp.int32) + 2 * ((me & pair[1]) != 0).astype(jnp.int32)
+        quarters = held.reshape(4, held.shape[0] // 4, width)
+        total = jnp.take(quarters, mine, axis=0)
+        for offset in (1, 2, 3):
+            send = jnp.take(quarters, mine ^ offset, axis=0)
+            total = total + lax.ppermute(send, "dp", axis_pairs(size, group_partner(pair, offset)))
+        held = total
+    for pair in reversed(groups):
+        mine = ((me & pair[0]) != 0).astype(jnp.int32) + 2 * ((me & pair[1]) != 0).astype(jnp.int32)
+        arrived = [held] + [
+            lax.ppermute(held, "dp", axis_pairs(size, group_partner(pair, offset)))
+            for offset in (1, 2, 3)
+        ]
+        held = jnp.take(jnp.stack(arrived), jnp.arange(4, dtype=jnp.int32) ^ mine, axis=0)
+        held = held.reshape(-1, width)
     count = grad_residues.size
     weight = held[: grad_weight.shape[0]]
     residue_sum = held[grad_weight.shape[0], :count].reshape(grad_residues.shape)

time: 428 us -> 431 us (level)
  the two profiles are of different devices: /device:TPU:1 before, /device:TPU:43 now
where the time goes in v6:
time: 431 us; the launch traced here: 424 us
  starting transfers between devices  165 us (38%)
  waiting for transfers between devices  130 us (30%)
  local copies, waits for them, and re-layouts  55.8 us (13%)
  matrix products  37.5 us (9%)
  other arithmetic  34.1 us (8%)
    ppermute x20, waiting for transfers between devices, doubling_gather(): lax.ppermute(held, axis, axis_pairs(size, mask))  97.1 us
    ppermute x20, starting transfers between devices, doubling_gather(): lax.ppermute(held, axis, axis_pairs(size, mask))  83.3 us
    ppermute x6, starting transfers between devices, summed_over_dp(): lax.ppermute(send, 'dp', axis_pairs(size, group_partner(pair, offset)))  24.8 us
    dot_general x24, matrix products, single(): return jnp.einsum('ckm,mj->ckj', data, table, precision=HIGHEST)  23.9 us
    ppermute x6, starting transfers between devices, summed_over_dp(): lax.ppermute(held, 'dp', axis_pairs(size, group_partner(pair, offset)))  23.8 us
    unnamed x83, local copies, waits for them, and re-layouts  19.3 us
    all_to_all x1, waiting for transfers between devices, body(): lax.all_to_all(jnp.stack([queries, keys, values]), 'ctx', split_axis=3, c...  12.3 us
    ppermute x6, waiting for transfers between devices, summed_over_dp(): lax.ppermute(held, 'dp', axis_pairs(size, group_partner(pair, offset)))  11.8 us
  transfers between devices with their start and end apart: 36, of which 22 were waited for; matrix products, arithmetic and copies ran while one was open for 21% of the time, Pallas kernels for 0%

profile of v6, /device:TPU:43, one launch (start us, length us, event | category | flops | bytes accessed | tf_op | source)
XLA Modules:
  0.0 424.4 jit_solution(12654789439160593248)
XLA Ops:
  3.0 11.6 %all-to-all-start = ((bf16[3,1,128,512]{2,0,1,3:T(4,128)(2,1)}), bf16[3,1,128,512]{2,0,1,3:T(4,128)(2,1)S(1)}, u32[]{:S(2)}, u32[]{:S(2)}) async-start(bf16[3,1,128,512]{2,0,1,3:T(4,128)(2,1)} %copy.76), calls=%async_computation | async-start | bytes 1048576 | tf_op jit(solution)/shard_map/all_to_all | solution.py:218
  17.1 12.3 %all-to-all-done = bf16[3,1,128,512]{2,0,1,3:T(4,128)(2,1)S(1)} async-done(((bf16[3,1,128,512]{2,0,1,3:T(4,128)(2,1)}), bf16[3,1,128,512]{2,0,1,3:T(4,128)(2,1)S(1)}, u32[]{:S(2)}, u32[]{:S(2)}) %all-to-all-start) | async-done | bytes 393248 | tf_op jit(solution)/shard_map/all_to_all | solution.py:218
  29.4 7.0 %all-to-all-start.2 = ((bf16[32,128,256]{1,2,0:T(8,128)(2,1)}), bf16[32,128,256]{1,2,0:T(8,128)(2,1)}, u32[]{:S(2)}, u32[]{:S(2)}) async-start(bf16[32,128,256]{1,2,0:T(8,128)(2,1)} %bitcast.46), calls=%async_computation.2 | async-start | bytes 4194304 | tf_op jit(solution)/shard_map/all_to_all | solution.py:100
  37.6 7.0 %collective-permute-start = (bf16[256,128]{1,0:T(8,128)(2,1)S(1)}, bf16[256,128]{1,0:T(8,128)(2,1)S(1)}, u32[]{:S(2)}, u32[]{:S(2)}) collective-permute-start(bf16[256,128]{1,0:T(8,128)(2,1)S(1)} %get-tuple-element.105), channel_id=1, source_target_pairs={{0,16},{1,17},{2,18},{3,19},{4,20},{5,21},{6,22},{7,23},{8,24},{9,... | collective-permute-start | bytes 196616 | tf_op jit(solution)/shard_map/ppermute | solution.py:153
  47.1 43.6 %collective-permute-done = bf16[256,128]{1,0:T(8,128)(2,1)S(1)} collective-permute-done((bf16[256,128]{1,0:T(8,128)(2,1)S(1)}, bf16[256,128]{1,0:T(8,128)(2,1)S(1)}, u32[]{:S(2)}, u32[]{:S(2)}) %collective-permute-start) | collective-permute-done | bytes 65568 | tf_op jit(solution)/shard_map/ppermute | solution.py:153
  93.2 3.8 collective-permute-start.6
  98.1 9.1 %collective-permute-start.2 = (bf16[1024,128]{1,0:T(8,128)(2,1)}, bf16[1024,128]{1,0:T(8,128)(2,1)S(1)}, u32[]{:S(2)}, u32[]{:S(2)}) collective-permute-start(bf16[1024,128]{1,0:T(8,128)(2,1)} %pad_maximum_fusion.10), channel_id=1, source_target_pairs={{0,2},{1,3},{2,0},{3,1},{4,6},{5,7},{6,4},{7,5},{8,10},{9,11},{10,... | collective-permute-start | bytes 786440 | tf_op jit(solution)/shard_map/ppermute | solution.py:153
  119.0 7.4 %collective-permute-start.3 = (bf16[2048,128]{1,0:T(8,128)(2,1)S(1)}, bf16[2048,128]{1,0:T(8,128)(2,1)S(1)}, u32[]{:S(2)}, u32[]{:S(2)}) collective-permute-start(bf16[2048,128]{1,0:T(8,128)(2,1)S(1)} %pad_maximum_fusion.4), channel_id=1, source_target_pairs={{0,4},{1,5},{2,6},{3,7},{4,0},{5,1},{6,2},{7,3},{8,12},{9,13},{10,... | collective-permute-start | bytes 1572872 | tf_op jit(solution)/shard_map/ppermute | solution.py:153
  129.3 4.1 collective-permute-start.8
  139.7 4.6 %collective-permute-done.8 = bf16[2048,128]{1,0:T(8,128)(2,1)S(1)} collective-permute-done((bf16[2048,128]{1,0:T(8,128)(2,1)S(1)}, bf16[2048,128]{1,0:T(8,128)(2,1)S(1)}, u32[]{:S(2)}, u32[]{:S(2)}) %collective-permute-start.8) | collective-permute-done | bytes 524320 | tf_op jit(solution)/shard_map/ppermute | solution.py:153
  148.9 4.1 copy.75
  155.1 11.8 %collective-permute-done.4 = bf16[4096,128]{1,0:T(8,128)(2,1)} collective-permute-done((bf16[4096,128]{1,0:T(8,128)(2,1)}, bf16[4096,128]{1,0:T(8,128)(2,1)}, u32[]{:S(2)}, u32[]{:S(2)}) %collective-permute-start.4) | collective-permute-done | bytes 1048608 | tf_op jit(solution)/shard_map/ppermute | solution.py:153
  171.6 4.1 pad_maximum_fusion.1
  175.7 5.9 %collective-permute-start.10 = (bf16[32,512,128]{2,1,0:T(8,128)(2,1)}, bf16[32,512,128]{2,1,0:T(8,128)(2,1)}, u32[]{:S(2)}, u32[]{:S(2)}) collective-permute-start(bf16[32,512,128]{2,1,0:T(8,128)(2,1)} %pad_maximum_fusion.1), channel_id=1, source_target_pairs={{0,32},{32,0},{64,96},{96,64},{128,160},{160,128},{192,224},{224,1... | collective-permute-start | bytes 12582920 | tf_op jit(solution)/shard_map/ppermute | solution.py:114
  183.3 4.1 copy.83
  197.4 4.0 pad_maximum_fusion
  212.5 8.1 %all-to-all-start.1 = ((bf16[32,2,1024]{2,1,0:T(2,128)(2,1)}), bf16[32,2,1024]{2,1,0:T(2,128)(2,1)}, u32[]{:S(2)}, u32[]{:S(2)}) async-start(bf16[32,2,1024]{2,1,0:T(2,128)(2,1)} %reshape.532), calls=%async_computation.1 | async-start | bytes 262144 | tf_op jit(solution)/shard_map/all_to_all | solution.py:239
  259.2 5.8 %collective-permute-start.16 = (bf16[8,4096]{1,0:T(8,128)(2,1)}, bf16[8,4096]{1,0:T(8,128)(2,1)S(1)}, u32[]{:S(2)}, u32[]{:S(2)}) collective-permute-start(bf16[8,4096]{1,0:T(8,128)(2,1)} %get-tuple-element.94), channel_id=1, source_target_pairs={{0,16},{1,17},{2,18},{3,19},{4,20},{5,21},{6,22},{7,23},{8,24},{9,... | collective-permute-start | bytes 196616 | tf_op jit(solution)/shard_map/ppermute | solution.py:153
  281.1 5.2 %collective-permute-start.13 = (bf16[32,4096]{1,0:T(8,128)(2,1)S(1)}, bf16[32,4096]{1,0:T(8,128)(2,1)S(1)}, u32[]{:S(2)}, u32[]{:S(2)}) collective-permute-start(bf16[32,4096]{1,0:T(8,128)(2,1)S(1)} %pad_maximum_fusion.12), channel_id=1, source_target_pairs={{0,2},{1,3},{2,0},{3,1},{4,6},{5,7},{6,4},{7,5},{8,10},{9,11},{10,... | collective-permute-start | bytes 786440 | tf_op jit(solution)/shard_map/ppermute | solution.py:153
  291.9 8.8 %collective-permute-done.13 = bf16[32,4096]{1,0:T(8,128)(2,1)S(1)} collective-permute-done((bf16[32,4096]{1,0:T(8,128)(2,1)S(1)}, bf16[32,4096]{1,0:T(8,128)(2,1)S(1)}, u32[]{:S(2)}, u32[]{:S(2)}) %collective-permute-start.13) | collective-permute-done | bytes 262176 | tf_op jit(solution)/shard_map/ppermute | solution.py:153
  307.2 5.5 %collective-permute-start.19 = (bf16[64,4096]{1,0:T(8,128)(2,1)S(1)}, bf16[64,4096]{1,0:T(8,128)(2,1)S(1)}, u32[]{:S(2)}, u32[]{:S(2)}) collective-permute-start(bf16[64,4096]{1,0:T(8,128)(2,1)S(1)} %pad_maximum_fusion.7), channel_id=1, source_target_pairs={{0,1},{1,0},{2,3},{3,2},{4,5},{5,4},{6,7},{7,6},{8,9},{9,8},{10,11... | collective-permute-start | bytes 1572872 | tf_op jit(solution)/shard_map/ppermute | solution.py:153
  315.3 5.3 %collective-permute-start.15 = (bf16[128,4096]{1,0:T(8,128)(2,1)}, bf16[128,4096]{1,0:T(8,128)(2,1)S(1)}, u32[]{:S(2)}, u32[]{:S(2)}) collective-permute-start(bf16[128,4096]{1,0:T(8,128)(2,1)} %get-tuple-element.60), channel_id=1, source_target_pairs={{0,1},{1,0},{2,3},{3,2},{4,5},{5,4},{6,7},{7,6},{8,9},{9,8},{10,11... | collective-permute-start | bytes 3145736 | tf_op jit(solution)/shard_map/ppermute | solution.py:153
  324.3 3.7 collective-permute-start.20
  329.6 16.2 %collective-permute-done.15 = bf16[128,4096]{1,0:T(8,128)(2,1)S(1)} collective-permute-done((bf16[128,4096]{1,0:T(8,128)(2,1)}, bf16[128,4096]{1,0:T(8,128)(2,1)S(1)}, u32[]{:S(2)}, u32[]{:S(2)}) %collective-permute-start.15) | collective-permute-done | bytes 1048608 | tf_op jit(solution)/shard_map/ppermute | solution.py:153
  353.2 4.8 %collective-permute-start.22 = (f32[132,256]{1,0:T(8,128)S(1)}, f32[132,256]{1,0:T(8,128)S(1)}, u32[]{:S(2)}, u32[]{:S(2)}) collective-permute-start(f32[132,256]{1,0:T(8,128)S(1)} %get-tuple-element.59), channel_id=1, source_target_pairs={{0,256},{32,288},{64,320},{96,352},{128,384},{160,416},{192,448},{... | collective-permute-start | bytes 405512 | tf_op jit(solution)/shard_map/ppermute | solution.py:195
  364.2 6.5 %collective-permute-start.24 = (f32[33,256]{1,0:T(8,128)S(1)}, f32[33,256]{1,0:T(8,128)S(1)}, u32[]{:S(2)}, u32[]{:S(2)}) collective-permute-start(f32[33,256]{1,0:T(8,128)S(1)} %get-tuple-element.85), channel_id=1, source_target_pairs={{0,32},{32,0},{64,96},{96,64},{128,160},{160,128},{192,224},{224,1... | collective-permute-start | bytes 101384 | tf_op jit(solution)/shard_map/ppermute | solution.py:195
  373.4 6.8 %collective-permute-start.26 = (f32[33,256]{1,0:T(8,128)S(1)}, f32[33,256]{1,0:T(8,128)S(1)}, u32[]{:S(2)}, u32[]{:S(2)}) collective-permute-start(f32[33,256]{1,0:T(8,128)S(1)} %get-tuple-element.86), channel_id=1, source_target_pairs={{0,96},{32,64},{64,32},{96,0},{128,224},{160,192},{192,160},{224,1... | collective-permute-start | bytes 101384 | tf_op jit(solution)/shard_map/ppermute | solution.py:195
  385.5 6.0 %collective-permute-start.28 = (f32[33,256]{1,0:T(8,128)S(1)}, f32[33,256]{1,0:T(8,128)S(1)}, u32[]{:S(2)}, u32[]{:S(2)}) collective-permute-start(f32[33,256]{1,0:T(8,128)S(1)} %fusion.110), channel_id=1, source_target_pairs={{0,64},{32,96},{64,0},{96,32},{128,192},{160,224},{192,128},{224,1... | collective-permute-start | bytes 101384 | tf_op jit(solution)/shard_map/ppermute | solution.py:200
  391.5 3.9 collective-permute-start.29
  396.1 4.9 %collective-permute-done.29 = f32[33,256]{1,0:T(8,128)S(1)} collective-permute-done((f32[33,256]{1,0:T(8,128)S(1)}, f32[33,256]{1,0:T(8,128)S(1)}, u32[]{:S(2)}, u32[]{:S(2)}) %collective-permute-start.29) | collective-permute-done | bytes 33824 | tf_op jit(solution)/shard_map/ppermute | solution.py:200
  401.8 7.0 %collective-permute-start.30 = (f32[132,256]{1,0:T(8,128)S(1)}, f32[132,256]{1,0:T(8,128)S(1)}, u32[]{:S(2)}, u32[]{:S(2)}) collective-permute-start(f32[132,256]{1,0:T(8,128)S(1)} %broadcast_select_fusion.2), channel_id=1, source_target_pairs={{0,128},{32,160},{64,192},{96,224},{128,0},{160,32},{192,64},{224,... | collective-permute-start | bytes 405512 | tf_op jit(solution)/shard_map/ppermute | solution.py:200
  416.7 4.1 collective-permute-done.32
  (277 shorter events, 174.8 us)
Async XLA Ops:
  3.0 26.5 %all-to-all-start = ((bf16[3,1,128,512]{2,0,1,3:T(4,128)(2,1)}), bf16[3,1,128,512]{2,0,1,3:T(4,128)(2,1)S(1)}, u32[]{:S(2)}, u32[]{:S(2)}) async-start(bf16[3,1,128,512]{2,0,1,3:T(4,128)(2,1)} %copy.76), calls=%async_computation | async-start | bytes 1048576 | tf_op jit(solution)/shard_map/all_to_all | solution.py:218
  29.4 183.1 %all-to-all-start.2 = ((bf16[32,128,256]{1,2,0:T(8,128)(2,1)}), bf16[32,128,256]{1,2,0:T(8,128)(2,1)}, u32[]{:S(2)}, u32[]{:S(2)}) async-start(bf16[32,128,256]{1,2,0:T(8,128)(2,1)} %bitcast.46), calls=%async_computation.2 | async-start | bytes 4194304 | tf_op jit(solution)/shard_map/all_to_all | solution.py:100
  37.6 53.1 %collective-permute-start = (bf16[256,128]{1,0:T(8,128)(2,1)S(1)}, bf16[256,128]{1,0:T(8,128)(2,1)S(1)}, u32[]{:S(2)}, u32[]{:S(2)}) collective-permute-start(bf16[256,128]{1,0:T(8,128)(2,1)S(1)} %get-tuple-element.105), channel_id=1, source_target_pairs={{0,16},{1,17},{2,18},{3,19},{4,20},{5,21},{6,22},{7,23},{8,24},{9,... | collective-permute-start | bytes 196616 | tf_op jit(solution)/shard_map/ppermute | solution.py:153
  44.9 48.3 %collective-permute-start.5 = (bf16[256,128]{1,0:T(8,128)(2,1)S(1)}, bf16[256,128]{1,0:T(8,128)(2,1)S(1)}, u32[]{:S(2)}, u32[]{:S(2)}) collective-permute-start(bf16[256,128]{1,0:T(8,128)(2,1)S(1)} %get-tuple-element.104), channel_id=1, source_target_pairs={{0,16},{1,17},{2,18},{3,19},{4,20},{5,21},{6,22},{7,23},{8,24},{9,... | collective-permute-start | bytes 196616 | tf_op jit(solution)/shard_map/ppermute | solution.py:153
  93.2 20.1 %collective-permute-start.6 = (bf16[512,128]{1,0:T(8,128)(2,1)S(1)}, bf16[512,128]{1,0:T(8,128)(2,1)S(1)}, u32[]{:S(2)}, u32[]{:S(2)}) collective-permute-start(bf16[512,128]{1,0:T(8,128)(2,1)S(1)} %pad_maximum_fusion.16), channel_id=1, source_target_pairs={{0,8},{1,9},{2,10},{3,11},{4,12},{5,13},{6,14},{7,15},{8,0},{9,1},... | collective-permute-start | bytes 393224 | tf_op jit(solution)/shard_map/ppermute | solution.py:153
  98.1 20.0 %collective-permute-start.2 = (bf16[1024,128]{1,0:T(8,128)(2,1)}, bf16[1024,128]{1,0:T(8,128)(2,1)S(1)}, u32[]{:S(2)}, u32[]{:S(2)}) collective-permute-start(bf16[1024,128]{1,0:T(8,128)(2,1)} %pad_maximum_fusion.10), channel_id=1, source_target_pairs={{0,2},{1,3},{2,0},{3,1},{4,6},{5,7},{6,4},{7,5},{8,10},{9,11},{10,... | collective-permute-start | bytes 786440 | tf_op jit(solution)/shard_map/ppermute | solution.py:153
  113.4 15.9 %collective-permute-start.7 = (bf16[1024,128]{1,0:T(8,128)(2,1)S(1)}, bf16[1024,128]{1,0:T(8,128)(2,1)S(1)}, u32[]{:S(2)}, u32[]{:S(2)}) collective-permute-start(bf16[1024,128]{1,0:T(8,128)(2,1)S(1)} %pad_maximum_fusion.11), channel_id=1, source_target_pairs={{0,2},{1,3},{2,0},{3,1},{4,6},{5,7},{6,4},{7,5},{8,10},{9,11},{10,... | collective-permute-start | bytes 786440 | tf_op jit(solution)/shard_map/ppermute | solution.py:153
  119.0 16.1 %collective-permute-start.3 = (bf16[2048,128]{1,0:T(8,128)(2,1)S(1)}, bf16[2048,128]{1,0:T(8,128)(2,1)S(1)}, u32[]{:S(2)}, u32[]{:S(2)}) collective-permute-start(bf16[2048,128]{1,0:T(8,128)(2,1)S(1)} %pad_maximum_fusion.4), channel_id=1, source_target_pairs={{0,4},{1,5},{2,6},{3,7},{4,0},{5,1},{6,2},{7,3},{8,12},{9,13},{10,... | collective-permute-start | bytes 1572872 | tf_op jit(solution)/shard_map/ppermute | solution.py:153
  129.3 15.0 %collective-permute-start.8 = (bf16[2048,128]{1,0:T(8,128)(2,1)S(1)}, bf16[2048,128]{1,0:T(8,128)(2,1)S(1)}, u32[]{:S(2)}, u32[]{:S(2)}) collective-permute-start(bf16[2048,128]{1,0:T(8,128)(2,1)S(1)} %pad_maximum_fusion.5), channel_id=1, source_target_pairs={{0,1},{1,0},{2,3},{3,2},{4,5},{5,4},{6,7},{7,6},{8,9},{9,8},{10,11... | collective-permute-start | bytes 1572872 | tf_op jit(solution)/shard_map/ppermute | solution.py:153
  136.2 30.7 %collective-permute-start.4 = (bf16[4096,128]{1,0:T(8,128)(2,1)}, bf16[4096,128]{1,0:T(8,128)(2,1)}, u32[]{:S(2)}, u32[]{:S(2)}) collective-permute-start(bf16[4096,128]{1,0:T(8,128)(2,1)} %get-tuple-element.70), channel_id=1, source_target_pairs={{0,1},{1,0},{2,3},{3,2},{4,5},{5,4},{6,7},{7,6},{8,9},{9,8},{10,11... | collective-permute-start | bytes 3145736 | tf_op jit(solution)/shard_map/ppermute | solution.py:153
  145.4 23.8 %collective-permute-start.9 = (bf16[4096,128]{1,0:T(8,128)(2,1)}, bf16[4096,128]{1,0:T(8,128)(2,1)}, u32[]{:S(2)}, u32[]{:S(2)}) collective-permute-start(bf16[4096,128]{1,0:T(8,128)(2,1)} %get-tuple-element.72), channel_id=1, source_target_pairs={{0,4},{1,5},{2,6},{3,7},{4,0},{5,1},{6,2},{7,3},{8,12},{9,13},{10,... | collective-permute-start | bytes 3145736 | tf_op jit(solution)/shard_map/ppermute | solution.py:153
  175.7 21.7 %collective-permute-start.10 = (bf16[32,512,128]{2,1,0:T(8,128)(2,1)}, bf16[32,512,128]{2,1,0:T(8,128)(2,1)}, u32[]{:S(2)}, u32[]{:S(2)}) collective-permute-start(bf16[32,512,128]{2,1,0:T(8,128)(2,1)} %pad_maximum_fusion.1), channel_id=1, source_target_pairs={{0,32},{32,0},{64,96},{96,64},{128,160},{160,128},{192,224},{224,1... | collective-permute-start | bytes 12582920 | tf_op jit(solution)/shard_map/ppermute | solution.py:114
  212.5 16.5 %all-to-all-start.1 = ((bf16[32,2,1024]{2,1,0:T(2,128)(2,1)}), bf16[32,2,1024]{2,1,0:T(2,128)(2,1)}, u32[]{:S(2)}, u32[]{:S(2)}) async-start(bf16[32,2,1024]{2,1,0:T(2,128)(2,1)} %reshape.532), calls=%async_computation.1 | async-start | bytes 262144 | tf_op jit(solution)/shard_map/all_to_all | solution.py:239
  255.7 12.8 %collective-permute-start.11 = (bf16[8,4096]{1,0:T(8,128)(2,1)}, bf16[8,4096]{1,0:T(8,128)(2,1)S(1)}, u32[]{:S(2)}, u32[]{:S(2)}) collective-permute-start(bf16[8,4096]{1,0:T(8,128)(2,1)} %get-tuple-element.95), channel_id=1, source_target_pairs={{0,16},{1,17},{2,18},{3,19},{4,20},{5,21},{6,22},{7,23},{8,24},{9,... | collective-permute-start | bytes 196616 | tf_op jit(solution)/shard_map/ppermute | solution.py:153
  259.2 13.1 %collective-permute-start.16 = (bf16[8,4096]{1,0:T(8,128)(2,1)}, bf16[8,4096]{1,0:T(8,128)(2,1)S(1)}, u32[]{:S(2)}, u32[]{:S(2)}) collective-permute-start(bf16[8,4096]{1,0:T(8,128)(2,1)} %get-tuple-element.94), channel_id=1, source_target_pairs={{0,16},{1,17},{2,18},{3,19},{4,20},{5,21},{6,22},{7,23},{8,24},{9,... | collective-permute-start | bytes 196616 | tf_op jit(solution)/shard_map/ppermute | solution.py:153
  269.3 10.8 %collective-permute-start.12 = (bf16[16,4096]{1,0:T(8,128)(2,1)S(1)}, bf16[16,4096]{1,0:T(8,128)(2,1)S(1)}, u32[]{:S(2)}, u32[]{:S(2)}) collective-permute-start(bf16[16,4096]{1,0:T(8,128)(2,1)S(1)} %pad_maximum_fusion.17), channel_id=1, source_target_pairs={{0,8},{1,9},{2,10},{3,11},{4,12},{5,13},{6,14},{7,15},{8,0},{9,1},... | collective-permute-start | bytes 393224 | tf_op jit(solution)/shard_map/ppermute | solution.py:153
  273.8 12.4 %collective-permute-start.17 = (bf16[16,4096]{1,0:T(8,128)(2,1)S(1)}, bf16[16,4096]{1,0:T(8,128)(2,1)S(1)}, u32[]{:S(2)}, u32[]{:S(2)}) collective-permute-start(bf16[16,4096]{1,0:T(8,128)(2,1)S(1)} %pad_maximum_fusion.18), channel_id=1, source_target_pairs={{0,8},{1,9},{2,10},{3,11},{4,12},{5,13},{6,14},{7,15},{8,0},{9,1},... | collective-permute-start | bytes 393224 | tf_op jit(solution)/shard_map/ppermute | solution.py:153
  281.1 19.7 %collective-permute-start.13 = (bf16[32,4096]{1,0:T(8,128)(2,1)S(1)}, bf16[32,4096]{1,0:T(8,128)(2,1)S(1)}, u32[]{:S(2)}, u32[]{:S(2)}) collective-permute-start(bf16[32,4096]{1,0:T(8,128)(2,1)S(1)} %pad_maximum_fusion.12), channel_id=1, source_target_pairs={{0,2},{1,3},{2,0},{3,1},{4,6},{5,7},{6,4},{7,5},{8,10},{9,11},{10,... | collective-permute-start | bytes 786440 | tf_op jit(solution)/shard_map/ppermute | solution.py:153
  287.2 19.2 %collective-permute-start.18 = (bf16[32,4096]{1,0:T(8,128)(2,1)S(1)}, bf16[32,4096]{1,0:T(8,128)(2,1)S(1)}, u32[]{:S(2)}, u32[]{:S(2)}) collective-permute-start(bf16[32,4096]{1,0:T(8,128)(2,1)S(1)} %pad_maximum_fusion.13), channel_id=1, source_target_pairs={{0,2},{1,3},{2,0},{3,1},{4,6},{5,7},{6,4},{7,5},{8,10},{9,11},{10,... | collective-permute-start | bytes 786440 | tf_op jit(solution)/shard_map/ppermute | solution.py:153
  301.6 12.8 %collective-permute-start.14 = (bf16[64,4096]{1,0:T(8,128)(2,1)S(1)}, bf16[64,4096]{1,0:T(8,128)(2,1)S(1)}, u32[]{:S(2)}, u32[]{:S(2)}) collective-permute-start(bf16[64,4096]{1,0:T(8,128)(2,1)S(1)} %pad_maximum_fusion.6), channel_id=1, source_target_pairs={{0,4},{1,5},{2,6},{3,7},{4,0},{5,1},{6,2},{7,3},{8,12},{9,13},{10,... | collective-permute-start | bytes 1572872 | tf_op jit(solution)/shard_map/ppermute | solution.py:153
  307.2 16.1 %collective-permute-start.19 = (bf16[64,4096]{1,0:T(8,128)(2,1)S(1)}, bf16[64,4096]{1,0:T(8,128)(2,1)S(1)}, u32[]{:S(2)}, u32[]{:S(2)}) collective-permute-start(bf16[64,4096]{1,0:T(8,128)(2,1)S(1)} %pad_maximum_fusion.7), channel_id=1, source_target_pairs={{0,1},{1,0},{2,3},{3,2},{4,5},{5,4},{6,7},{7,6},{8,9},{9,8},{10,11... | collective-permute-start | bytes 1572872 | tf_op jit(solution)/shard_map/ppermute | solution.py:153
  315.3 30.6 %collective-permute-start.15 = (bf16[128,4096]{1,0:T(8,128)(2,1)}, bf16[128,4096]{1,0:T(8,128)(2,1)S(1)}, u32[]{:S(2)}, u32[]{:S(2)}) collective-permute-start(bf16[128,4096]{1,0:T(8,128)(2,1)} %get-tuple-element.60), channel_id=1, source_target_pairs={{0,1},{1,0},{2,3},{3,2},{4,5},{5,4},{6,7},{7,6},{8,9},{9,8},{10,11... | collective-permute-start | bytes 3145736 | tf_op jit(solution)/shard_map/ppermute | solution.py:153
  324.3 24.2 %collective-permute-start.20 = (bf16[128,4096]{1,0:T(8,128)(2,1)}, bf16[128,4096]{1,0:T(8,128)(2,1)S(1)}, u32[]{:S(2)}, u32[]{:S(2)}) collective-permute-start(bf16[128,4096]{1,0:T(8,128)(2,1)} %get-tuple-element.62), channel_id=1, source_target_pairs={{0,4},{1,5},{2,6},{3,7},{4,0},{5,1},{6,2},{7,3},{8,12},{9,13},{10,... | collective-permute-start | bytes 3145736 | tf_op jit(solution)/shard_map/ppermute | solution.py:153
  351.3 9.7 %collective-permute-start.21 = (f32[132,256]{1,0:T(8,128)S(1)}, f32[132,256]{1,0:T(8,128)S(1)}, u32[]{:S(2)}, u32[]{:S(2)}) collective-permute-start(f32[132,256]{1,0:T(8,128)S(1)} %get-tuple-element.57), channel_id=1, source_target_pairs={{0,128},{32,160},{64,192},{96,224},{128,0},{160,32},{192,64},{224,... | collective-permute-start | bytes 405512 | tf_op jit(solution)/shard_map/ppermute | solution.py:195
  364.2 17.0 %collective-permute-start.24 = (f32[33,256]{1,0:T(8,128)S(1)}, f32[33,256]{1,0:T(8,128)S(1)}, u32[]{:S(2)}, u32[]{:S(2)}) collective-permute-start(f32[33,256]{1,0:T(8,128)S(1)} %get-tuple-element.85), channel_id=1, source_target_pairs={{0,32},{32,0},{64,96},{96,64},{128,160},{160,128},{192,224},{224,1... | collective-permute-start | bytes 101384 | tf_op jit(solution)/shard_map/ppermute | solution.py:195
  370.8 10.5 %collective-permute-start.25 = (f32[33,256]{1,0:T(8,128)S(1)}, f32[33,256]{1,0:T(8,128)S(1)}, u32[]{:S(2)}, u32[]{:S(2)}) collective-permute-start(f32[33,256]{1,0:T(8,128)S(1)} %get-tuple-element.87), channel_id=1, source_target_pairs={{0,64},{32,96},{64,0},{96,32},{128,192},{160,224},{192,128},{224,1... | collective-permute-start | bytes 101384 | tf_op jit(solution)/shard_map/ppermute | solution.py:195
  373.4 10.1 %collective-permute-start.26 = (f32[33,256]{1,0:T(8,128)S(1)}, f32[33,256]{1,0:T(8,128)S(1)}, u32[]{:S(2)}, u32[]{:S(2)}) collective-permute-start(f32[33,256]{1,0:T(8,128)S(1)} %get-tuple-element.86), channel_id=1, source_target_pairs={{0,96},{32,64},{64,32},{96,0},{128,224},{160,192},{192,160},{224,1... | collective-permute-start | bytes 101384 | tf_op jit(solution)/shard_map/ppermute | solution.py:195
  383.6 12.6 %collective-permute-start.27 = (f32[33,256]{1,0:T(8,128)S(1)}, f32[33,256]{1,0:T(8,128)S(1)}, u32[]{:S(2)}, u32[]{:S(2)}) collective-permute-start(f32[33,256]{1,0:T(8,128)S(1)} %fusion.110), channel_id=1, source_target_pairs={{0,32},{32,0},{64,96},{96,64},{128,160},{160,128},{192,224},{224,1... | collective-permute-start | bytes 101384 | tf_op jit(solution)/shard_map/ppermute | solution.py:200
  385.5 10.6 %collective-permute-start.28 = (f32[33,256]{1,0:T(8,128)S(1)}, f32[33,256]{1,0:T(8,128)S(1)}, u32[]{:S(2)}, u32[]{:S(2)}) collective-permute-start(f32[33,256]{1,0:T(8,128)S(1)} %fusion.110), channel_id=1, source_target_pairs={{0,64},{32,96},{64,0},{96,32},{128,192},{160,224},{192,128},{224,1... | collective-permute-start | bytes 101384 | tf_op jit(solution)/shard_map/ppermute | solution.py:200
  391.5 9.6 %collective-permute-start.29 = (f32[33,256]{1,0:T(8,128)S(1)}, f32[33,256]{1,0:T(8,128)S(1)}, u32[]{:S(2)}, u32[]{:S(2)}) collective-permute-start(f32[33,256]{1,0:T(8,128)S(1)} %fusion.110), channel_id=1, source_target_pairs={{0,96},{32,64},{64,32},{96,0},{128,224},{160,192},{192,160},{224,1... | collective-permute-start | bytes 101384 | tf_op jit(solution)/shard_map/ppermute | solution.py:200
  401.8 12.2 %collective-permute-start.30 = (f32[132,256]{1,0:T(8,128)S(1)}, f32[132,256]{1,0:T(8,128)S(1)}, u32[]{:S(2)}, u32[]{:S(2)}) collective-permute-start(f32[132,256]{1,0:T(8,128)S(1)} %broadcast_select_fusion.2), channel_id=1, source_target_pairs={{0,128},{32,160},{64,192},{96,224},{128,0},{160,32},{192,64},{224,... | collective-permute-start | bytes 405512 | tf_op jit(solution)/shard_map/ppermute | solution.py:200
  410.8 10.0 %collective-permute-start.32 = (f32[132,256]{1,0:T(8,128)S(1)}, f32[132,256]{1,0:T(8,128)S(1)}, u32[]{:S(2)}, u32[]{:S(2)}) collective-permute-start(f32[132,256]{1,0:T(8,128)S(1)} %broadcast_select_fusion.2), channel_id=1, source_target_pairs={{0,384},{32,416},{64,448},{96,480},{128,256},{160,288},{192,320},{... | collective-permute-start | bytes 405512 | tf_op jit(solution)/shard_map/ppermute | solution.py:200
  (32 other events, 550.7 us)

commit v7 on v5

--- a/solution.py
+++ b/solution.py
@@ -108,8 +108,9 @@
     piece = lax.dynamic_slice_in_dim(out_weight, core * half, half, axis=1)
     piece, tie = lax.optimization_barrier((piece, tie))
     split = channels // 2
-    first = doubling_gather(piece[:split], "ctx", masks).reshape(-1, split, half)
-    second = doubling_gather(piece[split:], "ctx", other_masks(masks)).reshape(-1, split, half)
+    first, second = paired_gather(piece, "ctx", masks)
+    first = first.reshape(-1, split, half)
+    second = second.reshape(-1, split, half)
     held = jnp.concatenate([first, second], axis=1)
     other = lax.ppermute(held, "dp", axis_pairs(lax.axis_size("dp"), 1))
     full = jnp.concatenate([held, other], axis=2)
@@ -144,6 +145,21 @@
 
 def other_masks(masks):
     return masks[:-2] + (masks[-1], masks[-2])
+
+
+def paired_gather(block, axis, masks):
+    size = lax.axis_size(axis)
+    rows = block.shape[0]
+    held = block
+    for mask in masks[:-2]:
+        held = jnp.concatenate([held, lax.ppermute(held, axis, axis_pairs(size, mask))], axis=0)
+    held = held.reshape(-1, 2, rows // 2, *block.shape[1:])
+    first = held[:, 0].reshape(-1, *block.shape[1:])
+    second = held[:, 1].reshape(-1, *block.shape[1:])
+    for mask, other in zip(masks[-2:], other_masks(masks)[-2:]):
+        first = jnp.concatenate([first, lax.ppermute(first, axis, axis_pairs(size, mask))], axis=0)
+        second = jnp.concatenate([second, lax.ppermute(second, axis, axis_pairs(size, other))], axis=0)
+    return first, second
 
 
 def doubling_gather(block, axis, masks):
@@ -260,9 +276,10 @@
     gated_t, grad_cols = lax.optimization_barrier((gated_t, grad_cols))
     split = gated_t.shape[0] // 2
     pieces = []
-    for rows, order in ((gated_t[:split], gather_masks), (gated_t[split:], other_masks(gather_masks))):
+    halves = paired_gather(gated_t, "ctx", gather_masks)
+    for rows, order in zip(halves, (gather_masks, other_masks(gather_masks))):
         partial_value = lax.dot_general(
-            doubling_gather(rows, "ctx", order),
+            rows,
             grad_cols,
             (((1,), (0,)), ((), ())),
             preferred_element_type=jnp.float32,

time: 428 us -> 437 us (1.021)
  waiting for transfers between devices: 126 us -> 206 us
  starting transfers between devices: 170 us -> 121 us
  local copies, waits for them, and re-layouts: 58.1 us -> 31.1 us
  other arithmetic: 27.3 us -> 33.1 us
    ppermute x20 -> x14, waiting for transfers between devices: 97.3 us -> 173 us  [the longest x6 82 us: paired_gather(): lax.ppermute(held, axis, axis_pairs(size, mask))]
    ppermute x20 -> x14, starting transfers between devices: 87 us -> 44.5 us  [the longest x6 24.9 us: paired_gather(): lax.ppermute(held, axis, axis_pairs(size, mask))]
    concatenate x8 -> x0, local copies, waits for them, and re-layouts: 13.6 us -> none  [doubling_gather(): jnp.concatenate([held, lax.ppermute(held, axis, axis_pairs(size, mask))],...]
    unnamed x59 -> x49, local copies, waits for them, and re-layouts: 18.1 us -> 5.36 us
    concatenate x12, other arithmetic: 0.25 us -> 8.73 us  [the longest x3 4.79 us: paired_gather(): jnp.concatenate([second, lax.ppermute(second, axis, axis_pairs(size, othe...]
    all_to_all x1, starting transfers between devices: 12.4 us -> 7.48 us  [body(): lax.all_to_all(grad_gated, 'ctx', split_axis=2, concat_axis=1, tiled=True)]
  transfers between devices with their start and end apart: 32 -> 26, of which waited for: 22 -> 22; matrix products, arithmetic and copies ran while one was open for 19% -> 16% of each run, Pallas kernels for 0% -> 0%
where the time goes in v7:
time: 437 us; the launch traced here: 431 us
  waiting for transfers between devices  206 us (47%)
  starting transfers between devices  121 us (28%)
  matrix products  37.6 us (9%)
  other arithmetic  33.1 us (8%)
  local copies, waits for them, and re-layouts  31.1 us (7%)
    ppermute x6, waiting for transfers between devices, paired_gather(): lax.ppermute(held, axis, axis_pairs(size, mask))  82 us
    ppermute x4, waiting for transfers between devices, paired_gather(): lax.ppermute(second, axis, axis_pairs(size, other))  49.9 us
    ppermute x4, waiting for transfers between devices, paired_gather(): lax.ppermute(first, axis, axis_pairs(size, mask))  40.9 us
    ppermute x6, starting transfers between devices, paired_gather(): lax.ppermute(held, axis, axis_pairs(size, mask))  24.9 us
    ppermute x4, starting transfers between devices, summed_over_dp(): other = lax.ppermute(held, 'dp', axis_pairs(size, mask))  21.4 us
    dot_general x24, matrix products, single(): return jnp.einsum('ckm,mj->ckj', data, table, precision=HIGHEST)  20 us
    ppermute x4, starting transfers between devices, summed_over_dp(): held = keep + lax.ppermute(send, 'dp', axis_pairs(size, mask))  18.9 us
    all_to_all x1, waiting for transfers between devices, body(): lax.all_to_all(jnp.stack([queries, keys, values]), 'ctx', split_axis=3, c...  15 us
  transfers between devices with their start and end apart: 26, of which 22 were waited for; matrix products, arithmetic and copies ran while one was open for 16% of the time, Pallas kernels for 0%

profile of v7, /device:TPU:1, one launch (start us, length us, event | category | flops | bytes accessed | tf_op | source)
XLA Modules:
  0.0 431.2 jit_solution(4199580865443376000)
XLA Ops:
  2.8 14.3 %all-to-all-start = ((bf16[3,1,128,512]{2,0,1,3:T(4,128)(2,1)}), bf16[3,1,128,512]{2,0,1,3:T(4,128)(2,1)S(1)}, u32[]{:S(2)}, u32[]{:S(2)}) async-start(bf16[3,1,128,512]{2,0,1,3:T(4,128)(2,1)} %copy.81), calls=%async_computation | async-start | bytes 1048576 | tf_op jit(solution)/shard_map/all_to_all | solution.py:225
  17.2 15.0 %all-to-all-done = bf16[3,1,128,512]{2,0,1,3:T(4,128)(2,1)S(1)} async-done(((bf16[3,1,128,512]{2,0,1,3:T(4,128)(2,1)}), bf16[3,1,128,512]{2,0,1,3:T(4,128)(2,1)S(1)}, u32[]{:S(2)}, u32[]{:S(2)}) %all-to-all-start) | async-done | bytes 393248 | tf_op jit(solution)/shard_map/all_to_all | solution.py:225
  33.9 5.2 %collective-permute-start = (bf16[512,128]{1,0:T(8,128)(2,1)S(1)}, bf16[512,128]{1,0:T(8,128)(2,1)S(1)}, u32[]{:S(2)}, u32[]{:S(2)}) collective-permute-start(bf16[512,128]{1,0:T(8,128)(2,1)S(1)} %constant_dynamic-slice_fusion), channel_id=1, source_target_pairs={{0,16},{1,17},{2,18},{3,19},{4,20},{5,21},{6,22},{7,23},{8,24},{9,... | collective-permute-start | bytes 393224 | tf_op jit(solution)/shard_map/ppermute | solution.py:155
  39.1 4.5 %collective-permute-done = bf16[512,128]{1,0:T(8,128)(2,1)S(1)} collective-permute-done((bf16[512,128]{1,0:T(8,128)(2,1)S(1)}, bf16[512,128]{1,0:T(8,128)(2,1)S(1)}, u32[]{:S(2)}, u32[]{:S(2)}) %collective-permute-start) | collective-permute-done | bytes 131104 | tf_op jit(solution)/shard_map/ppermute | solution.py:155
  43.6 5.4 %collective-permute-start.1 = (bf16[1024,128]{1,0:T(8,128)(2,1)S(1)}, bf16[1024,128]{1,0:T(8,128)(2,1)S(1)}, u32[]{:S(2)}, u32[]{:S(2)}) collective-permute-start(bf16[1024,128]{1,0:T(8,128)(2,1)S(1)} %pad_maximum_fusion.17), channel_id=1, source_target_pairs={{0,8},{1,9},{2,10},{3,11},{4,12},{5,13},{6,14},{7,15},{8,0},{9,1},... | collective-permute-start | bytes 786440 | tf_op jit(solution)/shard_map/ppermute | solution.py:155
  49.0 10.9 %collective-permute-done.1 = bf16[1024,128]{1,0:T(8,128)(2,1)S(1)} collective-permute-done((bf16[1024,128]{1,0:T(8,128)(2,1)S(1)}, bf16[1024,128]{1,0:T(8,128)(2,1)S(1)}, u32[]{:S(2)}, u32[]{:S(2)}) %collective-permute-start.1) | collective-permute-done | bytes 262176 | tf_op jit(solution)/shard_map/ppermute | solution.py:155
  60.0 7.6 %collective-permute-start.2 = (bf16[2048,128]{1,0:T(8,128)(2,1)S(1)}, bf16[2048,128]{1,0:T(8,128)(2,1)S(1)}, u32[]{:S(2)}, u32[]{:S(2)}) collective-permute-start(bf16[2048,128]{1,0:T(8,128)(2,1)S(1)} %pad_maximum_fusion.11), channel_id=1, source_target_pairs={{0,2},{1,3},{2,0},{3,1},{4,6},{5,7},{6,4},{7,5},{8,10},{9,11},{10,... | collective-permute-start | bytes 1572872 | tf_op jit(solution)/shard_map/ppermute | solution.py:155
  67.6 21.1 %collective-permute-done.2 = bf16[2048,128]{1,0:T(8,128)(2,1)S(1)} collective-permute-done((bf16[2048,128]{1,0:T(8,128)(2,1)S(1)}, bf16[2048,128]{1,0:T(8,128)(2,1)S(1)}, u32[]{:S(2)}, u32[]{:S(2)}) %collective-permute-start.2) | collective-permute-done | bytes 524320 | tf_op jit(solution)/shard_map/ppermute | solution.py:155
  93.3 8.6 %all-to-all-start.2 = ((bf16[32,128,256]{1,2,0:T(8,128)(2,1)}), bf16[32,128,256]{1,2,0:T(8,128)(2,1)}, u32[]{:S(2)}, u32[]{:S(2)}) async-start(bf16[32,128,256]{1,2,0:T(8,128)(2,1)} %bitcast.49), calls=%async_computation.2 | async-start | bytes 4194304 | tf_op jit(solution)/shard_map/all_to_all | solution.py:100
  101.9 3.1 collective-permute-start.5
  109.6 46.8 %collective-permute-done.5 = bf16[2048,128]{1,0:T(8,128)(2,1)S(1)} collective-permute-done((bf16[2048,128]{1,0:T(8,128)(2,1)S(1)}, bf16[2048,128]{1,0:T(8,128)(2,1)S(1)}, u32[]{:S(2)}, u32[]{:S(2)}) %collective-permute-start.5) | collective-permute-done | bytes 524320 | tf_op jit(solution)/shard_map/ppermute | solution.py:161
  159.4 3.2 copy.79
  162.7 16.3 %collective-permute-done.4 = bf16[4096,128]{1,0:T(8,128)(2,1)} collective-permute-done((bf16[4096,128]{1,0:T(8,128)(2,1)}, bf16[4096,128]{1,0:T(8,128)(2,1)}, u32[]{:S(2)}, u32[]{:S(2)}) %collective-permute-start.4) | collective-permute-done | bytes 1048608 | tf_op jit(solution)/shard_map/ppermute | solution.py:160
  185.2 6.2 %collective-permute-start.7 = (bf16[32,512,128]{2,1,0:T(8,128)(2,1)}, bf16[32,512,128]{2,1,0:T(8,128)(2,1)}, u32[]{:S(2)}, u32[]{:S(2)}) collective-permute-start(bf16[32,512,128]{2,1,0:T(8,128)(2,1)} %pad_maximum_fusion.1), channel_id=1, source_target_pairs={{0,32},{32,0},{64,96},{96,64},{128,160},{160,128},{192,224},{224,1... | collective-permute-start | bytes 12582920 | tf_op jit(solution)/shard_map/ppermute | solution.py:115
  193.5 3.2 select_bitcast_fusion.1
  196.7 4.1 copy.80
  212.5 3.5 pad_maximum_fusion
  227.0 7.5 %all-to-all-start.1 = ((bf16[32,2,1024]{2,1,0:T(2,128)(2,1)}), bf16[32,2,1024]{2,1,0:T(2,128)(2,1)S(1)}, u32[]{:S(2)}, u32[]{:S(2)}) async-start(bf16[32,2,1024]{2,1,0:T(2,128)(2,1)} %reshape.284), calls=%async_computation.1 | async-start | bytes 262144 | tf_op jit(solution)/shard_map/all_to_all | solution.py:246
  235.4 4.1 copy.94
  239.4 5.1 %all-to-all-done.1 = bf16[32,2,1024]{2,1,0:T(2,128)(2,1)S(1)} async-done(((bf16[32,2,1024]{2,1,0:T(2,128)(2,1)}), bf16[32,2,1024]{2,1,0:T(2,128)(2,1)S(1)}, u32[]{:S(2)}, u32[]{:S(2)}) %all-to-all-start.1) | async-done | bytes 131104 | tf_op jit(solution)/shard_map/all_to_all | solution.py:246
  271.7 7.6 %collective-permute-done.8 = bf16[16,4096]{1,0:T(8,128)(2,1)S(1)} collective-permute-done((bf16[16,4096]{1,0:T(8,128)(2,1)S(1)}, bf16[16,4096]{1,0:T(8,128)(2,1)S(1)}, u32[]{:S(2)}, u32[]{:S(2)}) %collective-permute-start.8) | collective-permute-done | bytes 131104 | tf_op jit(solution)/shard_map/ppermute | solution.py:155
  281.4 13.4 %collective-permute-done.9 = bf16[32,4096]{1,0:T(8,128)(2,1)S(1)} collective-permute-done((bf16[32,4096]{1,0:T(8,128)(2,1)S(1)}, bf16[32,4096]{1,0:T(8,128)(2,1)S(1)}, u32[]{:S(2)}, u32[]{:S(2)}) %collective-permute-start.9) | collective-permute-done | bytes 262176 | tf_op jit(solution)/shard_map/ppermute | solution.py:155
  296.8 24.5 %collective-permute-done.10 = bf16[64,4096]{1,0:T(8,128)(2,1)S(1)} collective-permute-done((bf16[64,4096]{1,0:T(8,128)(2,1)S(1)}, bf16[64,4096]{1,0:T(8,128)(2,1)S(1)}, u32[]{:S(2)}, u32[]{:S(2)}) %collective-permute-start.10) | collective-permute-done | bytes 524320 | tf_op jit(solution)/shard_map/ppermute | solution.py:155
  326.3 8.8 %collective-permute-done.11 = bf16[64,4096]{1,0:T(8,128)(2,1)S(1)} collective-permute-done((bf16[64,4096]{1,0:T(8,128)(2,1)S(1)}, bf16[64,4096]{1,0:T(8,128)(2,1)S(1)}, u32[]{:S(2)}, u32[]{:S(2)}) %collective-permute-start.11) | collective-permute-done | bytes 524320 | tf_op jit(solution)/shard_map/ppermute | solution.py:160
  343.4 15.9 %collective-permute-done.12 = bf16[128,4096]{1,0:T(8,128)(2,1)} collective-permute-done((bf16[128,4096]{1,0:T(8,128)(2,1)S(1)}, bf16[128,4096]{1,0:T(8,128)(2,1)}, u32[]{:S(2)}, u32[]{:S(2)}) %collective-permute-start.12) | collective-permute-done | bytes 1048608 | tf_op jit(solution)/shard_map/ppermute | solution.py:160
  369.0 4.8 %collective-permute-start.15 = (f32[264,256]{1,0:T(8,128)S(1)}, f32[264,256]{1,0:T(8,128)S(1)}, u32[]{:S(2)}, u32[]{:S(2)}) collective-permute-start(f32[264,256]{1,0:T(8,128)S(1)} %slice_select_fusion), channel_id=1, source_target_pairs={{0,32},{32,0},{64,96},{96,64},{128,160},{160,128},{192,224},{224,1... | collective-permute-start | bytes 811016 | tf_op jit(solution)/shard_map/ppermute | solution.py:207
  375.1 3.0 collective-permute-start.16
  381.9 5.3 %collective-permute-start.17 = (f32[66,256]{1,0:T(8,128)S(1)}, f32[66,256]{1,0:T(8,128)S(1)}, u32[]{:S(2)}, u32[]{:S(2)}) collective-permute-start(f32[66,256]{1,0:T(8,128)S(1)} %slice_select_fusion.2), channel_id=1, source_target_pairs={{0,256},{32,288},{64,320},{96,352},{128,384},{160,416},{192,448},{... | collective-permute-start | bytes 202760 | tf_op jit(solution)/shard_map/ppermute | solution.py:207
  388.9 5.9 %collective-permute-start.18 = (f32[33,256]{1,0:T(8,128)S(1)}, f32[33,256]{1,0:T(8,128)S(1)}, u32[]{:S(2)}, u32[]{:S(2)}) collective-permute-start(f32[33,256]{1,0:T(8,128)S(1)} %slice_select_fusion.3), channel_id=1, source_target_pairs={{0,64},{32,96},{64,0},{96,32},{128,192},{160,224},{192,128},{224,1... | collective-permute-start | bytes 101384 | tf_op jit(solution)/shard_map/ppermute | solution.py:207
  397.6 5.9 %collective-permute-start.19 = (f32[33,256]{1,0:T(8,128)S(1)}, f32[33,256]{1,0:T(8,128)S(1)}, u32[]{:S(2)}, u32[]{:S(2)}) collective-permute-start(f32[33,256]{1,0:T(8,128)S(1)} %select_add_fusion.3), channel_id=1, source_target_pairs={{0,64},{32,96},{64,0},{96,32},{128,192},{160,224},{192,128},{224,1... | collective-permute-start | bytes 101384 | tf_op jit(solution)/shard_map/ppermute | solution.py:209
  406.2 4.9 %collective-permute-start.20 = (f32[66,256]{1,0:T(8,128)S(1)}, f32[66,256]{1,0:T(8,128)S(1)}, u32[]{:S(2)}, u32[]{:S(2)}) collective-permute-start(f32[66,256]{1,0:T(8,128)S(1)} %maximum_select_fusion.3), channel_id=1, source_target_pairs={{0,256},{32,288},{64,320},{96,352},{128,384},{160,416},{192,448},{... | collective-permute-start | bytes 202760 | tf_op jit(solution)/shard_map/ppermute | solution.py:209
  419.5 8.1 %collective-permute-start.22 = (f32[264,256]{1,0:T(8,128)S(1)}, f32[264,256]{1,0:T(8,128)S(1)}, u32[]{:S(2)}, u32[]{:S(2)}) collective-permute-start(f32[264,256]{1,0:T(8,128)S(1)} %maximum_select_fusion.1), channel_id=1, source_target_pairs={{0,32},{32,0},{64,96},{96,64},{128,160},{160,128},{192,224},{224,1... | collective-permute-start | bytes 811016 | tf_op jit(solution)/shard_map/ppermute | solution.py:209
  (204 shorter events, 125.7 us)
Async XLA Ops:
  0.6 16.5 %copy-start = (bf16[512,256]{1,0:T(8,128)(2,1)S(1)}, bf16[512,256]{1,0:T(8,128)(2,1)}, u32[]{:S(2)}) copy-start(bf16[512,256]{1,0:T(8,128)(2,1)} %param.15) | copy-start | bytes 786436
  2.8 29.3 %all-to-all-start = ((bf16[3,1,128,512]{2,0,1,3:T(4,128)(2,1)}), bf16[3,1,128,512]{2,0,1,3:T(4,128)(2,1)S(1)}, u32[]{:S(2)}, u32[]{:S(2)}) async-start(bf16[3,1,128,512]{2,0,1,3:T(4,128)(2,1)} %copy.81), calls=%async_computation | async-start | bytes 1048576 | tf_op jit(solution)/shard_map/all_to_all | solution.py:225
  33.9 9.7 %collective-permute-start = (bf16[512,128]{1,0:T(8,128)(2,1)S(1)}, bf16[512,128]{1,0:T(8,128)(2,1)S(1)}, u32[]{:S(2)}, u32[]{:S(2)}) collective-permute-start(bf16[512,128]{1,0:T(8,128)(2,1)S(1)} %constant_dynamic-slice_fusion), channel_id=1, source_target_pairs={{0,16},{1,17},{2,18},{3,19},{4,20},{5,21},{6,22},{7,23},{8,24},{9,... | collective-permute-start | bytes 393224 | tf_op jit(solution)/shard_map/ppermute | solution.py:155
  43.6 16.3 %collective-permute-start.1 = (bf16[1024,128]{1,0:T(8,128)(2,1)S(1)}, bf16[1024,128]{1,0:T(8,128)(2,1)S(1)}, u32[]{:S(2)}, u32[]{:S(2)}) collective-permute-start(bf16[1024,128]{1,0:T(8,128)(2,1)S(1)} %pad_maximum_fusion.17), channel_id=1, source_target_pairs={{0,8},{1,9},{2,10},{3,11},{4,12},{5,13},{6,14},{7,15},{8,0},{9,1},... | collective-permute-start | bytes 786440 | tf_op jit(solution)/shard_map/ppermute | solution.py:155
  60.0 30.8 %copy-start.8 = (bf16[1,128,8192]{2,1,0:T(8,128)(2,1)S(1)}, bf16[1,128,8192]{2,1,0:T(8,128)(2,1)}, u32[]{:S(2)}) copy-start(bf16[1,128,8192]{2,1,0:T(8,128)(2,1)} %param.14) | copy-start | bytes 6291460
  60.0 28.7 %collective-permute-start.2 = (bf16[2048,128]{1,0:T(8,128)(2,1)S(1)}, bf16[2048,128]{1,0:T(8,128)(2,1)S(1)}, u32[]{:S(2)}, u32[]{:S(2)}) collective-permute-start(bf16[2048,128]{1,0:T(8,128)(2,1)S(1)} %pad_maximum_fusion.11), channel_id=1, source_target_pairs={{0,2},{1,3},{2,0},{3,1},{4,6},{5,7},{6,4},{7,5},{8,10},{9,11},{10,... | collective-permute-start | bytes 1572872 | tf_op jit(solution)/shard_map/ppermute | solution.py:155
  88.9 16.1 %collective-permute-start.3 = (bf16[2048,128]{1,0:T(8,128)(2,1)S(1)}, bf16[2048,128]{1,0:T(8,128)(2,1)}, u32[]{:S(2)}, u32[]{:S(2)}) collective-permute-start(bf16[2048,128]{1,0:T(8,128)(2,1)S(1)} %bitcast.287), channel_id=1, source_target_pairs={{0,4},{1,5},{2,6},{3,7},{4,0},{5,1},{6,2},{7,3},{8,12},{9,13},{10,... | collective-permute-start | bytes 1572872 | tf_op jit(solution)/shard_map/ppermute | solution.py:160
  93.3 133.7 %all-to-all-start.2 = ((bf16[32,128,256]{1,2,0:T(8,128)(2,1)}), bf16[32,128,256]{1,2,0:T(8,128)(2,1)}, u32[]{:S(2)}, u32[]{:S(2)}) async-start(bf16[32,128,256]{1,2,0:T(8,128)(2,1)} %bitcast.49), calls=%async_computation.2 | async-start | bytes 4194304 | tf_op jit(solution)/shard_map/all_to_all | solution.py:100
  101.9 54.4 %collective-permute-start.5 = (bf16[2048,128]{1,0:T(8,128)(2,1)S(1)}, bf16[2048,128]{1,0:T(8,128)(2,1)S(1)}, u32[]{:S(2)}, u32[]{:S(2)}) collective-permute-start(bf16[2048,128]{1,0:T(8,128)(2,1)S(1)} %bitcast.284), channel_id=1, source_target_pairs={{0,1},{1,0},{2,3},{3,2},{4,5},{5,4},{6,7},{7,6},{8,9},{9,8},{10,11... | collective-permute-start | bytes 1572872 | tf_op jit(solution)/shard_map/ppermute | solution.py:161
  107.1 71.8 %collective-permute-start.4 = (bf16[4096,128]{1,0:T(8,128)(2,1)}, bf16[4096,128]{1,0:T(8,128)(2,1)}, u32[]{:S(2)}, u32[]{:S(2)}) collective-permute-start(bf16[4096,128]{1,0:T(8,128)(2,1)} %pad_maximum_fusion.6), channel_id=1, source_target_pairs={{0,1},{1,0},{2,3},{3,2},{4,5},{5,4},{6,7},{7,6},{8,9},{9,8},{10,11... | collective-permute-start | bytes 3145736 | tf_op jit(solution)/shard_map/ppermute | solution.py:160
  157.5 23.5 %collective-permute-start.6 = (bf16[4096,128]{1,0:T(8,128)(2,1)}, bf16[4096,128]{1,0:T(8,128)(2,1)}, u32[]{:S(2)}, u32[]{:S(2)}) collective-permute-start(bf16[4096,128]{1,0:T(8,128)(2,1)} %pad_maximum_fusion.7), channel_id=1, source_target_pairs={{0,4},{1,5},{2,6},{3,7},{4,0},{5,1},{6,2},{7,3},{8,12},{9,13},{10,... | collective-permute-start | bytes 3145736 | tf_op jit(solution)/shard_map/ppermute | solution.py:161
  162.7 18.3 %copy-start.10 = (bf16[2048,128]{1,0:T(8,128)(2,1)S(1)}, bf16[2048,128]{1,0:T(8,128)(2,1)}, u32[]{:S(2)}) copy-start(bf16[2048,128]{1,0:T(8,128)(2,1)} %copy-done.9) | copy-start | bytes 1572868
  185.2 27.2 %collective-permute-start.7 = (bf16[32,512,128]{2,1,0:T(8,128)(2,1)}, bf16[32,512,128]{2,1,0:T(8,128)(2,1)}, u32[]{:S(2)}, u32[]{:S(2)}) collective-permute-start(bf16[32,512,128]{2,1,0:T(8,128)(2,1)} %pad_maximum_fusion.1), channel_id=1, source_target_pairs={{0,32},{32,0},{64,96},{96,64},{128,160},{160,128},{192,224},{224,1... | collective-permute-start | bytes 12582920 | tf_op jit(solution)/shard_map/ppermute | solution.py:115
  227.0 17.5 %all-to-all-start.1 = ((bf16[32,2,1024]{2,1,0:T(2,128)(2,1)}), bf16[32,2,1024]{2,1,0:T(2,128)(2,1)S(1)}, u32[]{:S(2)}, u32[]{:S(2)}) async-start(bf16[32,2,1024]{2,1,0:T(2,128)(2,1)} %reshape.284), calls=%async_computation.1 | async-start | bytes 262144 | tf_op jit(solution)/shard_map/all_to_all | solution.py:246
  269.0 10.3 %collective-permute-start.8 = (bf16[16,4096]{1,0:T(8,128)(2,1)S(1)}, bf16[16,4096]{1,0:T(8,128)(2,1)S(1)}, u32[]{:S(2)}, u32[]{:S(2)}) collective-permute-start(bf16[16,4096]{1,0:T(8,128)(2,1)S(1)} %get-tuple-element.18), channel_id=1, source_target_pairs={{0,16},{1,17},{2,18},{3,19},{4,20},{5,21},{6,22},{7,23},{8,24},{9,... | collective-permute-start | bytes 393224 | tf_op jit(solution)/shard_map/ppermute | solution.py:155
  279.4 15.5 %collective-permute-start.9 = (bf16[32,4096]{1,0:T(8,128)(2,1)S(1)}, bf16[32,4096]{1,0:T(8,128)(2,1)S(1)}, u32[]{:S(2)}, u32[]{:S(2)}) collective-permute-start(bf16[32,4096]{1,0:T(8,128)(2,1)S(1)} %pad_maximum_fusion.18), channel_id=1, source_target_pairs={{0,8},{1,9},{2,10},{3,11},{4,12},{5,13},{6,14},{7,15},{8,0},{9,1},... | collective-permute-start | bytes 786440 | tf_op jit(solution)/shard_map/ppermute | solution.py:155
  294.9 26.4 %collective-permute-start.10 = (bf16[64,4096]{1,0:T(8,128)(2,1)S(1)}, bf16[64,4096]{1,0:T(8,128)(2,1)S(1)}, u32[]{:S(2)}, u32[]{:S(2)}) collective-permute-start(bf16[64,4096]{1,0:T(8,128)(2,1)S(1)} %pad_maximum_fusion.12), channel_id=1, source_target_pairs={{0,2},{1,3},{2,0},{3,1},{4,6},{5,7},{6,4},{7,5},{8,10},{9,11},{10,... | collective-permute-start | bytes 1572872 | tf_op jit(solution)/shard_map/ppermute | solution.py:155
  321.5 13.7 %collective-permute-start.11 = (bf16[64,4096]{1,0:T(8,128)(2,1)S(1)}, bf16[64,4096]{1,0:T(8,128)(2,1)S(1)}, u32[]{:S(2)}, u32[]{:S(2)}) collective-permute-start(bf16[64,4096]{1,0:T(8,128)(2,1)S(1)} %get-tuple-element.31), channel_id=1, source_target_pairs={{0,4},{1,5},{2,6},{3,7},{4,0},{5,1},{6,2},{7,3},{8,12},{9,13},{10,... | collective-permute-start | bytes 1572872 | tf_op jit(solution)/shard_map/ppermute | solution.py:160
  323.9 14.3 %collective-permute-start.13 = (bf16[64,4096]{1,0:T(8,128)(2,1)S(1)}, bf16[64,4096]{1,0:T(8,128)(2,1)}, u32[]{:S(2)}, u32[]{:S(2)}) collective-permute-start(bf16[64,4096]{1,0:T(8,128)(2,1)S(1)} %get-tuple-element.32), channel_id=1, source_target_pairs={{0,1},{1,0},{2,3},{3,2},{4,5},{5,4},{6,7},{7,6},{8,9},{9,8},{10,11... | collective-permute-start | bytes 1572872 | tf_op jit(solution)/shard_map/ppermute | solution.py:161
  335.2 24.1 %collective-permute-start.12 = (bf16[128,4096]{1,0:T(8,128)(2,1)S(1)}, bf16[128,4096]{1,0:T(8,128)(2,1)}, u32[]{:S(2)}, u32[]{:S(2)}) collective-permute-start(bf16[128,4096]{1,0:T(8,128)(2,1)S(1)} %pad_maximum_fusion.9), channel_id=1, source_target_pairs={{0,1},{1,0},{2,3},{3,2},{4,5},{5,4},{6,7},{7,6},{8,9},{9,8},{10,11... | collective-permute-start | bytes 3145736 | tf_op jit(solution)/shard_map/ppermute | solution.py:160
  340.4 24.9 %collective-permute-start.14 = (bf16[128,4096]{1,0:T(8,128)(2,1)}, bf16[128,4096]{1,0:T(8,128)(2,1)}, u32[]{:S(2)}, u32[]{:S(2)}) collective-permute-start(bf16[128,4096]{1,0:T(8,128)(2,1)} %pad_maximum_fusion.10), channel_id=1, source_target_pairs={{0,4},{1,5},{2,6},{3,7},{4,0},{5,1},{6,2},{7,3},{8,12},{9,13},{10,... | collective-permute-start | bytes 3145736 | tf_op jit(solution)/shard_map/ppermute | solution.py:161
  369.0 5.9 %collective-permute-start.15 = (f32[264,256]{1,0:T(8,128)S(1)}, f32[264,256]{1,0:T(8,128)S(1)}, u32[]{:S(2)}, u32[]{:S(2)}) collective-permute-start(f32[264,256]{1,0:T(8,128)S(1)} %slice_select_fusion), channel_id=1, source_target_pairs={{0,32},{32,0},{64,96},{96,64},{128,160},{160,128},{192,224},{224,1... | collective-permute-start | bytes 811016 | tf_op jit(solution)/shard_map/ppermute | solution.py:207
  375.1 6.8 %collective-permute-start.16 = (f32[132,256]{1,0:T(8,128)S(1)}, f32[132,256]{1,0:T(8,128)S(1)}, u32[]{:S(2)}, u32[]{:S(2)}) collective-permute-start(f32[132,256]{1,0:T(8,128)S(1)} %slice_select_fusion.1), channel_id=1, source_target_pairs={{0,128},{32,160},{64,192},{96,224},{128,0},{160,32},{192,64},{224,... | collective-permute-start | bytes 405512 | tf_op jit(solution)/shard_map/ppermute | solution.py:207
  381.9 7.0 %collective-permute-start.17 = (f32[66,256]{1,0:T(8,128)S(1)}, f32[66,256]{1,0:T(8,128)S(1)}, u32[]{:S(2)}, u32[]{:S(2)}) collective-permute-start(f32[66,256]{1,0:T(8,128)S(1)} %slice_select_fusion.2), channel_id=1, source_target_pairs={{0,256},{32,288},{64,320},{96,352},{128,384},{160,416},{192,448},{... | collective-permute-start | bytes 202760 | tf_op jit(solution)/shard_map/ppermute | solution.py:207
  388.9 8.7 %collective-permute-start.18 = (f32[33,256]{1,0:T(8,128)S(1)}, f32[33,256]{1,0:T(8,128)S(1)}, u32[]{:S(2)}, u32[]{:S(2)}) collective-permute-start(f32[33,256]{1,0:T(8,128)S(1)} %slice_select_fusion.3), channel_id=1, source_target_pairs={{0,64},{32,96},{64,0},{96,32},{128,192},{160,224},{192,128},{224,1... | collective-permute-start | bytes 101384 | tf_op jit(solution)/shard_map/ppermute | solution.py:207
  397.6 8.7 %collective-permute-start.19 = (f32[33,256]{1,0:T(8,128)S(1)}, f32[33,256]{1,0:T(8,128)S(1)}, u32[]{:S(2)}, u32[]{:S(2)}) collective-permute-start(f32[33,256]{1,0:T(8,128)S(1)} %select_add_fusion.3), channel_id=1, source_target_pairs={{0,64},{32,96},{64,0},{96,32},{128,192},{160,224},{192,128},{224,1... | collective-permute-start | bytes 101384 | tf_op jit(solution)/shard_map/ppermute | solution.py:209
  406.2 6.6 %collective-permute-start.20 = (f32[66,256]{1,0:T(8,128)S(1)}, f32[66,256]{1,0:T(8,128)S(1)}, u32[]{:S(2)}, u32[]{:S(2)}) collective-permute-start(f32[66,256]{1,0:T(8,128)S(1)} %maximum_select_fusion.3), channel_id=1, source_target_pairs={{0,256},{32,288},{64,320},{96,352},{128,384},{160,416},{192,448},{... | collective-permute-start | bytes 202760 | tf_op jit(solution)/shard_map/ppermute | solution.py:209
  411.9 15.7 %copy-start.12 = (bf16[1,4096,16]{1,2,0:T(8,128)(2,1)S(1)}, bf16[1,4096,16]{1,2,0:T(8,128)(2,1)}, u32[]{:S(2)}) copy-start(bf16[1,4096,16]{1,2,0:T(8,128)(2,1)} %unstack.21) | copy-start | bytes 393220
  411.9 15.7 %copy-start.14 = (bf16[1,4096,16]{1,2,0:T(8,128)(2,1)S(1)}, bf16[1,4096,16]{1,2,0:T(8,128)(2,1)}, u32[]{:S(2)}) copy-start(bf16[1,4096,16]{1,2,0:T(8,128)(2,1)} %unstack.23) | copy-start | bytes 393220
  412.9 6.6 %collective-permute-start.21 = (f32[132,256]{1,0:T(8,128)S(1)}, f32[132,256]{1,0:T(8,128)S(1)}, u32[]{:S(2)}, u32[]{:S(2)}) collective-permute-start(f32[132,256]{1,0:T(8,128)S(1)} %maximum_select_fusion.2), channel_id=1, source_target_pairs={{0,128},{32,160},{64,192},{96,224},{128,0},{160,32},{192,64},{224,... | collective-permute-start | bytes 405512 | tf_op jit(solution)/shard_map/ppermute | solution.py:209
  416.3 14.7 %copy-start.1 = (bf16[512,256]{1,0:T(8,128)(2,1)S(1)}, bf16[512,256]{1,0:T(8,128)(2,1)}, u32[]{:S(2)}) copy-start(bf16[512,256]{1,0:T(8,128)(2,1)} %param.15) | copy-start | bytes 786436
  419.5 9.2 %collective-permute-start.22 = (f32[264,256]{1,0:T(8,128)S(1)}, f32[264,256]{1,0:T(8,128)S(1)}, u32[]{:S(2)}, u32[]{:S(2)}) collective-permute-start(f32[264,256]{1,0:T(8,128)S(1)} %maximum_select_fusion.1), channel_id=1, source_target_pairs={{0,32},{32,0},{64,96},{96,64},{128,160},{160,128},{192,224},{224,1... | collective-permute-start | bytes 811016 | tf_op jit(solution)/shard_map/ppermute | solution.py:209
  (12 other events, 31.0 us)

commit v8 on v7

--- a/solution.py
+++ b/solution.py
@@ -108,9 +108,8 @@
     piece = lax.dynamic_slice_in_dim(out_weight, core * half, half, axis=1)
     piece, tie = lax.optimization_barrier((piece, tie))
     split = channels // 2
-    first, second = paired_gather(piece, "ctx", masks)
-    first = first.reshape(-1, split, half)
-    second = second.reshape(-1, split, half)
+    first = doubling_gather(piece[:split], "ctx", masks).reshape(-1, split, half)
+    second = doubling_gather(piece[split:], "ctx", other_masks(masks)).reshape(-1, split, half)
     held = jnp.concatenate([first, second], axis=1)
     other = lax.ppermute(held, "dp", axis_pairs(lax.axis_size("dp"), 1))
     full = jnp.concatenate([held, other], axis=2)

time: 437 us -> 424 us (0.970)
  waiting for transfers between devices: 206 us -> 180 us
  local copies, waits for them, and re-layouts: 31.1 us -> 44.2 us
  starting transfers between devices: 121 us -> 128 us
  other arithmetic: 33.1 us -> 26.6 us
    ppermute x0 -> x10, waiting for transfers between devices: none -> 73.2 us  [doubling_gather(): lax.ppermute(held, axis, axis_pairs(size, mask))]
    ppermute x4 -> x2, waiting for transfers between devices: 49.9 us -> 1.44 us  [paired_gather(): lax.ppermute(second, axis, axis_pairs(size, other))]
    ppermute x0 -> x10, starting transfers between devices: none -> 37.1 us  [doubling_gather(): lax.ppermute(held, axis, axis_pairs(size, mask))]
    ppermute x6 -> x3, waiting for transfers between devices: 82 us -> 45.1 us  [paired_gather(): lax.ppermute(held, axis, axis_pairs(size, mask))]
    ppermute x6 -> x3, starting transfers between devices: 24.9 us -> 6.67 us  [paired_gather(): lax.ppermute(held, axis, axis_pairs(size, mask))]
    ppermute x4 -> x2, waiting for transfers between devices: 40.9 us -> 25 us  [paired_gather(): lax.ppermute(first, axis, axis_pairs(size, mask))]
    unnamed x49 -> x46, local copies, waits for them, and re-layouts: 5.36 us -> 14.1 us
    concatenate x0 -> x4, local copies, waits for them, and re-layouts: none -> 5.8 us  [doubling_gather(): jnp.concatenate([held, lax.ppermute(held, axis, axis_pairs(size, mask))],...]
  transfers between devices with their start and end apart: 26 -> 29, of which waited for: 22 -> 21; matrix products, arithmetic and copies ran while one was open for 16% -> 17% of each run, Pallas kernels for 0% -> 0%
where the time goes in v8:
time: 424 us; the launch traced here: 419 us
  waiting for transfers between devices  180 us (42%)
  starting transfers between devices  128 us (30%)
  local copies, waits for them, and re-layouts  44.2 us (10%)
  matrix products  37.5 us (9%)
  other arithmetic  26.6 us (6%)
    ppermute x10, waiting for transfers between devices, doubling_gather(): lax.ppermute(held, axis, axis_pairs(size, mask))  73.2 us
    ppermute x3, waiting for transfers between devices, paired_gather(): lax.ppermute(held, axis, axis_pairs(size, mask))  45.1 us
    ppermute x10, starting transfers between devices, doubling_gather(): lax.ppermute(held, axis, axis_pairs(size, mask))  37.1 us
    ppermute x2, waiting for transfers between devices, paired_gather(): lax.ppermute(first, axis, axis_pairs(size, mask))  25 us
    ppermute x4, starting transfers between devices, summed_over_dp(): other = lax.ppermute(held, 'dp', axis_pairs(size, mask))  21.2 us
    dot_general x24, matrix products, single(): return jnp.einsum('ckm,mj->ckj', data, table, precision=HIGHEST)  19.9 us
    ppermute x4, starting transfers between devices, summed_over_dp(): held = keep + lax.ppermute(send, 'dp', axis_pairs(size, mask))  17.4 us
    all_to_all x1, waiting for transfers between devices, body(): lax.all_to_all(jnp.stack([queries, keys, values]), 'ctx', split_axis=3, c...  15 us
  transfers between devices with their start and end apart: 29, of which 21 were waited for; matrix products, arithmetic and copies ran while one was open for 17% of the time, Pallas kernels for 0%

profile of v8, /device:TPU:1, one launch (start us, length us, event | category | flops | bytes accessed | tf_op | source)
XLA Modules:
  0.0 418.7 jit_solution(1881020055895588874)
XLA Ops:
  2.8 14.3 %all-to-all-start = ((bf16[3,1,128,512]{2,0,1,3:T(4,128)(2,1)}), bf16[3,1,128,512]{2,0,1,3:T(4,128)(2,1)S(1)}, u32[]{:S(2)}, u32[]{:S(2)}) async-start(bf16[3,1,128,512]{2,0,1,3:T(4,128)(2,1)} %copy.81), calls=%async_computation | async-start | bytes 1048576 | tf_op jit(solution)/shard_map/all_to_all | solution.py:224
  17.2 15.0 %all-to-all-done = bf16[3,1,128,512]{2,0,1,3:T(4,128)(2,1)S(1)} async-done(((bf16[3,1,128,512]{2,0,1,3:T(4,128)(2,1)}), bf16[3,1,128,512]{2,0,1,3:T(4,128)(2,1)S(1)}, u32[]{:S(2)}, u32[]{:S(2)}) %all-to-all-start) | async-done | bytes 393248 | tf_op jit(solution)/shard_map/all_to_all | solution.py:224
  33.3 5.2 %collective-permute-start = (bf16[256,128]{1,0:T(8,128)(2,1)S(1)}, bf16[256,128]{1,0:T(8,128)(2,1)S(1)}, u32[]{:S(2)}, u32[]{:S(2)}) collective-permute-start(bf16[256,128]{1,0:T(8,128)(2,1)S(1)} %get-tuple-element.59), channel_id=1, source_target_pairs={{0,16},{1,17},{2,18},{3,19},{4,20},{5,21},{6,22},{7,23},{8,24},{9,... | collective-permute-start | bytes 196616 | tf_op jit(solution)/shard_map/ppermute | solution.py:168
  38.6 3.9 collective-permute-start.5
  42.5 4.5 %collective-permute-start.1 = (bf16[512,128]{1,0:T(8,128)(2,1)S(1)}, bf16[512,128]{1,0:T(8,128)(2,1)S(1)}, u32[]{:S(2)}, u32[]{:S(2)}) collective-permute-start(bf16[512,128]{1,0:T(8,128)(2,1)S(1)} %pad_maximum_fusion.16), channel_id=1, source_target_pairs={{0,8},{1,9},{2,10},{3,11},{4,12},{5,13},{6,14},{7,15},{8,0},{9,1},... | collective-permute-start | bytes 393224 | tf_op jit(solution)/shard_map/ppermute | solution.py:168
  47.0 4.1 copy.78
  51.1 6.5 %all-to-all-start.2 = ((bf16[32,128,256]{1,2,0:T(8,128)(2,1)}), bf16[32,128,256]{1,2,0:T(8,128)(2,1)}, u32[]{:S(2)}, u32[]{:S(2)}) async-start(bf16[32,128,256]{1,2,0:T(8,128)(2,1)} %bitcast.46), calls=%async_computation.2 | async-start | bytes 4194304 | tf_op jit(solution)/shard_map/all_to_all | solution.py:100
  57.7 4.0 collective-permute-start.6
  61.7 4.0 collective-permute-start.2
  67.0 43.8 %collective-permute-done.6 = bf16[512,128]{1,0:T(8,128)(2,1)S(1)} collective-permute-done((bf16[512,128]{1,0:T(8,128)(2,1)S(1)}, bf16[512,128]{1,0:T(8,128)(2,1)S(1)}, u32[]{:S(2)}, u32[]{:S(2)}) %collective-permute-start.6) | collective-permute-done | bytes 131104 | tf_op jit(solution)/shard_map/ppermute | solution.py:168
  112.8 5.2 %collective-permute-done.2 = bf16[1024,128]{1,0:T(8,128)(2,1)S(1)} collective-permute-done((bf16[1024,128]{1,0:T(8,128)(2,1)S(1)}, bf16[1024,128]{1,0:T(8,128)(2,1)S(1)}, u32[]{:S(2)}, u32[]{:S(2)}) %collective-permute-start.2) | collective-permute-done | bytes 262176 | tf_op jit(solution)/shard_map/ppermute | solution.py:168
  118.0 6.3 %collective-permute-start.3 = (bf16[2048,128]{1,0:T(8,128)(2,1)S(1)}, bf16[2048,128]{1,0:T(8,128)(2,1)S(1)}, u32[]{:S(2)}, u32[]{:S(2)}) collective-permute-start(bf16[2048,128]{1,0:T(8,128)(2,1)S(1)} %pad_maximum_fusion.6), channel_id=1, source_target_pairs={{0,4},{1,5},{2,6},{3,7},{4,0},{5,1},{6,2},{7,3},{8,12},{9,13},{10,... | collective-permute-start | bytes 1572872 | tf_op jit(solution)/shard_map/ppermute | solution.py:168
  125.1 4.1 collective-permute-done.7
  138.0 3.8 collective-permute-done.8
  148.1 16.3 %collective-permute-done.4 = bf16[4096,128]{1,0:T(8,128)(2,1)} collective-permute-done((bf16[4096,128]{1,0:T(8,128)(2,1)}, bf16[4096,128]{1,0:T(8,128)(2,1)}, u32[]{:S(2)}, u32[]{:S(2)}) %collective-permute-start.4) | collective-permute-done | bytes 1048608 | tf_op jit(solution)/shard_map/ppermute | solution.py:168
  172.0 5.8 %collective-permute-start.10 = (bf16[32,512,128]{2,1,0:T(8,128)(2,1)}, bf16[32,512,128]{2,1,0:T(8,128)(2,1)}, u32[]{:S(2)}, u32[]{:S(2)}) collective-permute-start(bf16[32,512,128]{2,1,0:T(8,128)(2,1)} %pad_maximum_fusion.1), channel_id=1, source_target_pairs={{0,32},{32,0},{64,96},{96,64},{128,160},{160,128},{192,224},{224,1... | collective-permute-start | bytes 12582920 | tf_op jit(solution)/shard_map/ppermute | solution.py:114
  183.1 4.1 copy.80
  213.4 7.4 %all-to-all-start.1 = ((bf16[32,2,1024]{2,1,0:T(2,128)(2,1)}), bf16[32,2,1024]{2,1,0:T(2,128)(2,1)S(1)}, u32[]{:S(2)}, u32[]{:S(2)}) async-start(bf16[32,2,1024]{2,1,0:T(2,128)(2,1)} %reshape.280), calls=%async_computation.1 | async-start | bytes 262144 | tf_op jit(solution)/shard_map/all_to_all | solution.py:245
  221.7 4.1 copy.94
  225.7 5.1 %all-to-all-done.1 = bf16[32,2,1024]{2,1,0:T(2,128)(2,1)S(1)} async-done(((bf16[32,2,1024]{2,1,0:T(2,128)(2,1)}), bf16[32,2,1024]{2,1,0:T(2,128)(2,1)S(1)}, u32[]{:S(2)}, u32[]{:S(2)}) %all-to-all-start.1) | async-done | bytes 131104 | tf_op jit(solution)/shard_map/all_to_all | solution.py:245
  258.0 7.6 %collective-permute-done.11 = bf16[16,4096]{1,0:T(8,128)(2,1)S(1)} collective-permute-done((bf16[16,4096]{1,0:T(8,128)(2,1)S(1)}, bf16[16,4096]{1,0:T(8,128)(2,1)S(1)}, u32[]{:S(2)}, u32[]{:S(2)}) %collective-permute-start.11) | collective-permute-done | bytes 131104 | tf_op jit(solution)/shard_map/ppermute | solution.py:154
  267.7 13.3 %collective-permute-done.12 = bf16[32,4096]{1,0:T(8,128)(2,1)S(1)} collective-permute-done((bf16[32,4096]{1,0:T(8,128)(2,1)S(1)}, bf16[32,4096]{1,0:T(8,128)(2,1)S(1)}, u32[]{:S(2)}, u32[]{:S(2)}) %collective-permute-start.12) | collective-permute-done | bytes 262176 | tf_op jit(solution)/shard_map/ppermute | solution.py:154
  283.0 24.2 %collective-permute-done.13 = bf16[64,4096]{1,0:T(8,128)(2,1)S(1)} collective-permute-done((bf16[64,4096]{1,0:T(8,128)(2,1)S(1)}, bf16[64,4096]{1,0:T(8,128)(2,1)S(1)}, u32[]{:S(2)}, u32[]{:S(2)}) %collective-permute-start.13) | collective-permute-done | bytes 524320 | tf_op jit(solution)/shard_map/ppermute | solution.py:154
  312.7 7.9 %collective-permute-done.14 = bf16[64,4096]{1,0:T(8,128)(2,1)S(1)} collective-permute-done((bf16[64,4096]{1,0:T(8,128)(2,1)S(1)}, bf16[64,4096]{1,0:T(8,128)(2,1)S(1)}, u32[]{:S(2)}, u32[]{:S(2)}) %collective-permute-start.14) | collective-permute-done | bytes 524320 | tf_op jit(solution)/shard_map/ppermute | solution.py:159
  330.4 17.1 %collective-permute-done.15 = bf16[128,4096]{1,0:T(8,128)(2,1)} collective-permute-done((bf16[128,4096]{1,0:T(8,128)(2,1)}, bf16[128,4096]{1,0:T(8,128)(2,1)}, u32[]{:S(2)}, u32[]{:S(2)}) %collective-permute-start.15) | collective-permute-done | bytes 1048608 | tf_op jit(solution)/shard_map/ppermute | solution.py:159
  356.0 4.4 %collective-permute-start.18 = (f32[264,256]{1,0:T(8,128)S(1)}, f32[264,256]{1,0:T(8,128)S(1)}, u32[]{:S(2)}, u32[]{:S(2)}) collective-permute-start(f32[264,256]{1,0:T(8,128)S(1)} %slice_select_fusion), channel_id=1, source_target_pairs={{0,32},{32,0},{64,96},{96,64},{128,160},{160,128},{192,224},{224,1... | collective-permute-start | bytes 811016 | tf_op jit(solution)/shard_map/ppermute | solution.py:206
  361.7 3.8 collective-permute-start.19
  369.2 4.0 collective-permute-start.20
  375.8 5.2 %collective-permute-start.21 = (f32[33,256]{1,0:T(8,128)S(1)}, f32[33,256]{1,0:T(8,128)S(1)}, u32[]{:S(2)}, u32[]{:S(2)}) collective-permute-start(f32[33,256]{1,0:T(8,128)S(1)} %slice_select_fusion.3), channel_id=1, source_target_pairs={{0,64},{32,96},{64,0},{96,32},{128,192},{160,224},{192,128},{224,1... | collective-permute-start | bytes 101384 | tf_op jit(solution)/shard_map/ppermute | solution.py:206
  384.5 5.2 %collective-permute-start.22 = (f32[33,256]{1,0:T(8,128)S(1)}, f32[33,256]{1,0:T(8,128)S(1)}, u32[]{:S(2)}, u32[]{:S(2)}) collective-permute-start(f32[33,256]{1,0:T(8,128)S(1)} %select_add_fusion.3), channel_id=1, source_target_pairs={{0,64},{32,96},{64,0},{96,32},{128,192},{160,224},{192,128},{224,1... | collective-permute-start | bytes 101384 | tf_op jit(solution)/shard_map/ppermute | solution.py:208
  393.1 4.0 collective-permute-start.23
  406.3 8.9 %collective-permute-start.25 = (f32[264,256]{1,0:T(8,128)S(1)}, f32[264,256]{1,0:T(8,128)S(1)}, u32[]{:S(2)}, u32[]{:S(2)}) collective-permute-start(f32[264,256]{1,0:T(8,128)S(1)} %maximum_select_fusion.1), channel_id=1, source_target_pairs={{0,32},{32,0},{64,96},{96,64},{128,160},{160,128},{192,224},{224,1... | collective-permute-start | bytes 811016 | tf_op jit(solution)/shard_map/ppermute | solution.py:208
  (209 shorter events, 143.6 us)
Async XLA Ops:
  0.6 16.5 %copy-start = (bf16[512,256]{1,0:T(8,128)(2,1)S(1)}, bf16[512,256]{1,0:T(8,128)(2,1)}, u32[]{:S(2)}) copy-start(bf16[512,256]{1,0:T(8,128)(2,1)} %param.15) | copy-start | bytes 786436
  2.8 29.3 %all-to-all-start = ((bf16[3,1,128,512]{2,0,1,3:T(4,128)(2,1)}), bf16[3,1,128,512]{2,0,1,3:T(4,128)(2,1)S(1)}, u32[]{:S(2)}, u32[]{:S(2)}) async-start(bf16[3,1,128,512]{2,0,1,3:T(4,128)(2,1)} %copy.81), calls=%async_computation | async-start | bytes 1048576 | tf_op jit(solution)/shard_map/all_to_all | solution.py:224
  33.3 9.2 %collective-permute-start = (bf16[256,128]{1,0:T(8,128)(2,1)S(1)}, bf16[256,128]{1,0:T(8,128)(2,1)S(1)}, u32[]{:S(2)}, u32[]{:S(2)}) collective-permute-start(bf16[256,128]{1,0:T(8,128)(2,1)S(1)} %get-tuple-element.59), channel_id=1, source_target_pairs={{0,16},{1,17},{2,18},{3,19},{4,20},{5,21},{6,22},{7,23},{8,24},{9,... | collective-permute-start | bytes 196616 | tf_op jit(solution)/shard_map/ppermute | solution.py:168
  38.6 19.1 %collective-permute-start.5 = (bf16[256,128]{1,0:T(8,128)(2,1)S(1)}, bf16[256,128]{1,0:T(8,128)(2,1)S(1)}, u32[]{:S(2)}, u32[]{:S(2)}) collective-permute-start(bf16[256,128]{1,0:T(8,128)(2,1)S(1)} %get-tuple-element.58), channel_id=1, source_target_pairs={{0,16},{1,17},{2,18},{3,19},{4,20},{5,21},{6,22},{7,23},{8,24},{9,... | collective-permute-start | bytes 196616 | tf_op jit(solution)/shard_map/ppermute | solution.py:168
  42.5 19.1 %collective-permute-start.1 = (bf16[512,128]{1,0:T(8,128)(2,1)S(1)}, bf16[512,128]{1,0:T(8,128)(2,1)S(1)}, u32[]{:S(2)}, u32[]{:S(2)}) collective-permute-start(bf16[512,128]{1,0:T(8,128)(2,1)S(1)} %pad_maximum_fusion.16), channel_id=1, source_target_pairs={{0,8},{1,9},{2,10},{3,11},{4,12},{5,13},{6,14},{7,15},{8,0},{9,1},... | collective-permute-start | bytes 393224 | tf_op jit(solution)/shard_map/ppermute | solution.py:168
  51.1 162.2 %all-to-all-start.2 = ((bf16[32,128,256]{1,2,0:T(8,128)(2,1)}), bf16[32,128,256]{1,2,0:T(8,128)(2,1)}, u32[]{:S(2)}, u32[]{:S(2)}) async-start(bf16[32,128,256]{1,2,0:T(8,128)(2,1)} %bitcast.46), calls=%async_computation.2 | async-start | bytes 4194304 | tf_op jit(solution)/shard_map/all_to_all | solution.py:100
  57.7 53.1 %collective-permute-start.6 = (bf16[512,128]{1,0:T(8,128)(2,1)S(1)}, bf16[512,128]{1,0:T(8,128)(2,1)S(1)}, u32[]{:S(2)}, u32[]{:S(2)}) collective-permute-start(bf16[512,128]{1,0:T(8,128)(2,1)S(1)} %pad_maximum_fusion.17), channel_id=1, source_target_pairs={{0,8},{1,9},{2,10},{3,11},{4,12},{5,13},{6,14},{7,15},{8,0},{9,1},... | collective-permute-start | bytes 393224 | tf_op jit(solution)/shard_map/ppermute | solution.py:168
  61.7 56.2 %collective-permute-start.2 = (bf16[1024,128]{1,0:T(8,128)(2,1)S(1)}, bf16[1024,128]{1,0:T(8,128)(2,1)S(1)}, u32[]{:S(2)}, u32[]{:S(2)}) collective-permute-start(bf16[1024,128]{1,0:T(8,128)(2,1)S(1)} %pad_maximum_fusion.13), channel_id=1, source_target_pairs={{0,2},{1,3},{2,0},{3,1},{4,6},{5,7},{6,4},{7,5},{8,10},{9,11},{10,... | collective-permute-start | bytes 786440 | tf_op jit(solution)/shard_map/ppermute | solution.py:168
  110.8 18.3 %collective-permute-start.7 = (bf16[1024,128]{1,0:T(8,128)(2,1)S(1)}, bf16[1024,128]{1,0:T(8,128)(2,1)S(1)}, u32[]{:S(2)}, u32[]{:S(2)}) collective-permute-start(bf16[1024,128]{1,0:T(8,128)(2,1)S(1)} %pad_maximum_fusion.14), channel_id=1, source_target_pairs={{0,2},{1,3},{2,0},{3,1},{4,6},{5,7},{6,4},{7,5},{8,10},{9,11},{10,... | collective-permute-start | bytes 786440 | tf_op jit(solution)/shard_map/ppermute | solution.py:168
  118.0 14.8 %collective-permute-start.3 = (bf16[2048,128]{1,0:T(8,128)(2,1)S(1)}, bf16[2048,128]{1,0:T(8,128)(2,1)S(1)}, u32[]{:S(2)}, u32[]{:S(2)}) collective-permute-start(bf16[2048,128]{1,0:T(8,128)(2,1)S(1)} %pad_maximum_fusion.6), channel_id=1, source_target_pairs={{0,4},{1,5},{2,6},{3,7},{4,0},{5,1},{6,2},{7,3},{8,12},{9,13},{10,... | collective-permute-start | bytes 1572872 | tf_op jit(solution)/shard_map/ppermute | solution.py:168
  129.2 12.6 %collective-permute-start.8 = (bf16[2048,128]{1,0:T(8,128)(2,1)S(1)}, bf16[2048,128]{1,0:T(8,128)(2,1)S(1)}, u32[]{:S(2)}, u32[]{:S(2)}) collective-permute-start(bf16[2048,128]{1,0:T(8,128)(2,1)S(1)} %pad_maximum_fusion.7), channel_id=1, source_target_pairs={{0,1},{1,0},{2,3},{3,2},{4,5},{5,4},{6,7},{7,6},{8,9},{9,8},{10,11... | collective-permute-start | bytes 1572872 | tf_op jit(solution)/shard_map/ppermute | solution.py:168
  133.9 30.5 %collective-permute-start.4 = (bf16[4096,128]{1,0:T(8,128)(2,1)}, bf16[4096,128]{1,0:T(8,128)(2,1)}, u32[]{:S(2)}, u32[]{:S(2)}) collective-permute-start(bf16[4096,128]{1,0:T(8,128)(2,1)} %get-tuple-element.41), channel_id=1, source_target_pairs={{0,1},{1,0},{2,3},{3,2},{4,5},{5,4},{6,7},{7,6},{8,9},{9,8},{10,11... | collective-permute-start | bytes 3145736 | tf_op jit(solution)/shard_map/ppermute | solution.py:168
  142.7 24.0 %collective-permute-start.9 = (bf16[4096,128]{1,0:T(8,128)(2,1)}, bf16[4096,128]{1,0:T(8,128)(2,1)}, u32[]{:S(2)}, u32[]{:S(2)}) collective-permute-start(bf16[4096,128]{1,0:T(8,128)(2,1)} %get-tuple-element.43), channel_id=1, source_target_pairs={{0,4},{1,5},{2,6},{3,7},{4,0},{5,1},{6,2},{7,3},{8,12},{9,13},{10,... | collective-permute-start | bytes 3145736 | tf_op jit(solution)/shard_map/ppermute | solution.py:168
  148.1 18.6 %copy-start.3 = (bf16[8192,128]{1,0:T(8,128)(2,1)S(1)}, bf16[8192,128]{1,0:T(8,128)(2,1)}, u32[]{:S(2)}) copy-start(bf16[8192,128]{1,0:T(8,128)(2,1)} %copy-done.2) | copy-start | bytes 6291460
  172.0 26.8 %collective-permute-start.10 = (bf16[32,512,128]{2,1,0:T(8,128)(2,1)}, bf16[32,512,128]{2,1,0:T(8,128)(2,1)}, u32[]{:S(2)}, u32[]{:S(2)}) collective-permute-start(bf16[32,512,128]{2,1,0:T(8,128)(2,1)} %pad_maximum_fusion.1), channel_id=1, source_target_pairs={{0,32},{32,0},{64,96},{96,64},{128,160},{160,128},{192,224},{224,1... | collective-permute-start | bytes 12582920 | tf_op jit(solution)/shard_map/ppermute | solution.py:114
  213.4 17.4 %all-to-all-start.1 = ((bf16[32,2,1024]{2,1,0:T(2,128)(2,1)}), bf16[32,2,1024]{2,1,0:T(2,128)(2,1)S(1)}, u32[]{:S(2)}, u32[]{:S(2)}) async-start(bf16[32,2,1024]{2,1,0:T(2,128)(2,1)} %reshape.280), calls=%async_computation.1 | async-start | bytes 262144 | tf_op jit(solution)/shard_map/all_to_all | solution.py:245
  255.3 10.3 %collective-permute-start.11 = (bf16[16,4096]{1,0:T(8,128)(2,1)S(1)}, bf16[16,4096]{1,0:T(8,128)(2,1)S(1)}, u32[]{:S(2)}, u32[]{:S(2)}) collective-permute-start(bf16[16,4096]{1,0:T(8,128)(2,1)S(1)} %get-tuple-element.18), channel_id=1, source_target_pairs={{0,16},{1,17},{2,18},{3,19},{4,20},{5,21},{6,22},{7,23},{8,24},{9,... | collective-permute-start | bytes 393224 | tf_op jit(solution)/shard_map/ppermute | solution.py:154
  265.6 15.4 %collective-permute-start.12 = (bf16[32,4096]{1,0:T(8,128)(2,1)S(1)}, bf16[32,4096]{1,0:T(8,128)(2,1)S(1)}, u32[]{:S(2)}, u32[]{:S(2)}) collective-permute-start(bf16[32,4096]{1,0:T(8,128)(2,1)S(1)} %pad_maximum_fusion.15), channel_id=1, source_target_pairs={{0,8},{1,9},{2,10},{3,11},{4,12},{5,13},{6,14},{7,15},{8,0},{9,1},... | collective-permute-start | bytes 786440 | tf_op jit(solution)/shard_map/ppermute | solution.py:154
  281.0 26.1 %collective-permute-start.13 = (bf16[64,4096]{1,0:T(8,128)(2,1)S(1)}, bf16[64,4096]{1,0:T(8,128)(2,1)S(1)}, u32[]{:S(2)}, u32[]{:S(2)}) collective-permute-start(bf16[64,4096]{1,0:T(8,128)(2,1)S(1)} %pad_maximum_fusion.8), channel_id=1, source_target_pairs={{0,2},{1,3},{2,0},{3,1},{4,6},{5,7},{6,4},{7,5},{8,10},{9,11},{10,... | collective-permute-start | bytes 1572872 | tf_op jit(solution)/shard_map/ppermute | solution.py:154
  307.3 13.3 %collective-permute-start.14 = (bf16[64,4096]{1,0:T(8,128)(2,1)S(1)}, bf16[64,4096]{1,0:T(8,128)(2,1)S(1)}, u32[]{:S(2)}, u32[]{:S(2)}) collective-permute-start(bf16[64,4096]{1,0:T(8,128)(2,1)S(1)} %get-tuple-element.31), channel_id=1, source_target_pairs={{0,4},{1,5},{2,6},{3,7},{4,0},{5,1},{6,2},{7,3},{8,12},{9,13},{10,... | collective-permute-start | bytes 1572872 | tf_op jit(solution)/shard_map/ppermute | solution.py:159
  310.2 15.9 %collective-permute-start.16 = (bf16[64,4096]{1,0:T(8,128)(2,1)S(1)}, bf16[64,4096]{1,0:T(8,128)(2,1)S(1)}, u32[]{:S(2)}, u32[]{:S(2)}) collective-permute-start(bf16[64,4096]{1,0:T(8,128)(2,1)S(1)} %get-tuple-element.32), channel_id=1, source_target_pairs={{0,1},{1,0},{2,3},{3,2},{4,5},{5,4},{6,7},{7,6},{8,9},{9,8},{10,11... | collective-permute-start | bytes 1572872 | tf_op jit(solution)/shard_map/ppermute | solution.py:160
  322.5 25.0 %collective-permute-start.15 = (bf16[128,4096]{1,0:T(8,128)(2,1)}, bf16[128,4096]{1,0:T(8,128)(2,1)}, u32[]{:S(2)}, u32[]{:S(2)}) collective-permute-start(bf16[128,4096]{1,0:T(8,128)(2,1)} %pad_maximum_fusion.4), channel_id=1, source_target_pairs={{0,1},{1,0},{2,3},{3,2},{4,5},{5,4},{6,7},{7,6},{8,9},{9,8},{10,11... | collective-permute-start | bytes 3145736 | tf_op jit(solution)/shard_map/ppermute | solution.py:159
  327.2 25.3 %collective-permute-start.17 = (bf16[128,4096]{1,0:T(8,128)(2,1)}, bf16[128,4096]{1,0:T(8,128)(2,1)}, u32[]{:S(2)}, u32[]{:S(2)}) collective-permute-start(bf16[128,4096]{1,0:T(8,128)(2,1)} %pad_maximum_fusion.5), channel_id=1, source_target_pairs={{0,4},{1,5},{2,6},{3,7},{4,0},{5,1},{6,2},{7,3},{8,12},{9,13},{10,... | collective-permute-start | bytes 3145736 | tf_op jit(solution)/shard_map/ppermute | solution.py:160
  356.0 5.6 %collective-permute-start.18 = (f32[264,256]{1,0:T(8,128)S(1)}, f32[264,256]{1,0:T(8,128)S(1)}, u32[]{:S(2)}, u32[]{:S(2)}) collective-permute-start(f32[264,256]{1,0:T(8,128)S(1)} %slice_select_fusion), channel_id=1, source_target_pairs={{0,32},{32,0},{64,96},{96,64},{128,160},{160,128},{192,224},{224,1... | collective-permute-start | bytes 811016 | tf_op jit(solution)/shard_map/ppermute | solution.py:206
  361.7 7.4 %collective-permute-start.19 = (f32[132,256]{1,0:T(8,128)S(1)}, f32[132,256]{1,0:T(8,128)S(1)}, u32[]{:S(2)}, u32[]{:S(2)}) collective-permute-start(f32[132,256]{1,0:T(8,128)S(1)} %slice_select_fusion.1), channel_id=1, source_target_pairs={{0,128},{32,160},{64,192},{96,224},{128,0},{160,32},{192,64},{224,... | collective-permute-start | bytes 405512 | tf_op jit(solution)/shard_map/ppermute | solution.py:206
  369.2 6.6 %collective-permute-start.20 = (f32[66,256]{1,0:T(8,128)S(1)}, f32[66,256]{1,0:T(8,128)S(1)}, u32[]{:S(2)}, u32[]{:S(2)}) collective-permute-start(f32[66,256]{1,0:T(8,128)S(1)} %slice_select_fusion.2), channel_id=1, source_target_pairs={{0,256},{32,288},{64,320},{96,352},{128,384},{160,416},{192,448},{... | collective-permute-start | bytes 202760 | tf_op jit(solution)/shard_map/ppermute | solution.py:206
  375.8 8.7 %collective-permute-start.21 = (f32[33,256]{1,0:T(8,128)S(1)}, f32[33,256]{1,0:T(8,128)S(1)}, u32[]{:S(2)}, u32[]{:S(2)}) collective-permute-start(f32[33,256]{1,0:T(8,128)S(1)} %slice_select_fusion.3), channel_id=1, source_target_pairs={{0,64},{32,96},{64,0},{96,32},{128,192},{160,224},{192,128},{224,1... | collective-permute-start | bytes 101384 | tf_op jit(solution)/shard_map/ppermute | solution.py:206
  384.5 8.7 %collective-permute-start.22 = (f32[33,256]{1,0:T(8,128)S(1)}, f32[33,256]{1,0:T(8,128)S(1)}, u32[]{:S(2)}, u32[]{:S(2)}) collective-permute-start(f32[33,256]{1,0:T(8,128)S(1)} %select_add_fusion.3), channel_id=1, source_target_pairs={{0,64},{32,96},{64,0},{96,32},{128,192},{160,224},{192,128},{224,1... | collective-permute-start | bytes 101384 | tf_op jit(solution)/shard_map/ppermute | solution.py:208
  393.1 6.6 %collective-permute-start.23 = (f32[66,256]{1,0:T(8,128)S(1)}, f32[66,256]{1,0:T(8,128)S(1)}, u32[]{:S(2)}, u32[]{:S(2)}) collective-permute-start(f32[66,256]{1,0:T(8,128)S(1)} %maximum_select_fusion.3), channel_id=1, source_target_pairs={{0,256},{32,288},{64,320},{96,352},{128,384},{160,416},{192,448},{... | collective-permute-start | bytes 202760 | tf_op jit(solution)/shard_map/ppermute | solution.py:208
  399.8 6.5 %collective-permute-start.24 = (f32[132,256]{1,0:T(8,128)S(1)}, f32[132,256]{1,0:T(8,128)S(1)}, u32[]{:S(2)}, u32[]{:S(2)}) collective-permute-start(f32[132,256]{1,0:T(8,128)S(1)} %maximum_select_fusion.2), channel_id=1, source_target_pairs={{0,128},{32,160},{64,192},{96,224},{128,0},{160,32},{192,64},{224,... | collective-permute-start | bytes 405512 | tf_op jit(solution)/shard_map/ppermute | solution.py:208
  403.6 14.9 %copy-start.1 = (bf16[512,256]{1,0:T(8,128)(2,1)S(1)}, bf16[512,256]{1,0:T(8,128)(2,1)}, u32[]{:S(2)}) copy-start(bf16[512,256]{1,0:T(8,128)(2,1)} %param.15) | copy-start | bytes 786436
  406.3 10.0 %collective-permute-start.25 = (f32[264,256]{1,0:T(8,128)S(1)}, f32[264,256]{1,0:T(8,128)S(1)}, u32[]{:S(2)}, u32[]{:S(2)}) collective-permute-start(f32[264,256]{1,0:T(8,128)S(1)} %maximum_select_fusion.1), channel_id=1, source_target_pairs={{0,32},{32,0},{64,96},{96,64},{128,160},{160,128},{192,224},{224,1... | collective-permute-start | bytes 811016 | tf_op jit(solution)/shard_map/ppermute | solution.py:208
  (10 other events, 20.6 us)

commit v9 on v8

--- a/solution.py
+++ b/solution.py
@@ -262,12 +262,15 @@
     conv_out = leading_part(
         inverse_transform(*complex_product(prod_re, prod_im, taps_re, taps_im), tables), seq_len
     )
-    grad_product = leading_part(
-        inverse_transform(*complex_product(taps_re, -taps_im, grad_re, grad_im), tables), seq_len
-    )
-    grad_taps = leading_part(
-        inverse_transform(*complex_product(prod_re, -prod_im, grad_re, grad_im), tables), seq_len
-    )
+    product_re, product_im = complex_product(taps_re, -taps_im, grad_re, grad_im)
+    lag_re, lag_im = complex_product(prod_re, -prod_im, grad_re, grad_im)
+    both = leading_part(
+        inverse_transform(
+            jnp.concatenate([product_re, lag_re]), jnp.concatenate([product_im, lag_im]), tables
+        ),
+        seq_len,
+    )
+    grad_product, grad_taps = both[: product_re.shape[0]], both[product_re.shape[0] :]
     gated_t = (query_full * conv_out).astype(jnp.bfloat16)
     grad_queries = (grad_gated_full * conv_out).T.astype(jnp.bfloat16)[None]
     grad_keys = (grad_product * value_full).T.astype(jnp.bfloat16)[None]

time: 424 us -> 420 us (level)
  waiting for transfers between devices: 180 us -> 165 us
  other arithmetic: 26.6 us -> 33.6 us
    all_to_all x1, waiting for transfers between devices: 15 us -> 1.52 us  [body(): lax.all_to_all(jnp.stack([queries, keys, values]), 'ctx', split_axis=3, c...]
    unnamed x46 -> x73, local copies, waits for them, and re-layouts: 14.1 us -> 12 us
    dot_general x24 -> x20, matrix products: 19.9 us -> 21.5 us  [single(): return jnp.einsum('ckm,mj->ckj', data, table, precision=HIGHEST)]
  transfers between devices with their start and end apart: 29 -> 29, of which waited for: 21 -> 23; matrix products, arithmetic and copies ran while one was open for 17% -> 23% of each run, Pallas kernels for 0% -> 0%
where the time goes in v9:
time: 420 us; the launch traced here: 413 us
  waiting for transfers between devices  165 us (39%)
  starting transfers between devices  130 us (31%)
  local copies, waits for them, and re-layouts  43.5 us (10%)
  matrix products  38.1 us (9%)
  other arithmetic  33.6 us (8%)
    ppermute x10, waiting for transfers between devices, doubling_gather(): lax.ppermute(held, axis, axis_pairs(size, mask))  75 us
    ppermute x3, waiting for transfers between devices, paired_gather(): lax.ppermute(held, axis, axis_pairs(size, mask))  42.7 us
    ppermute x10, starting transfers between devices, doubling_gather(): lax.ppermute(held, axis, axis_pairs(size, mask))  39.7 us
    ppermute x4, starting transfers between devices, summed_over_dp(): other = lax.ppermute(held, 'dp', axis_pairs(size, mask))  23.2 us
    ppermute x2, waiting for transfers between devices, paired_gather(): lax.ppermute(first, axis, axis_pairs(size, mask))  23.2 us
    dot_general x20, matrix products, single(): return jnp.einsum('ckm,mj->ckj', data, table, precision=HIGHEST)  21.5 us
    ppermute x4, starting transfers between devices, summed_over_dp(): held = keep + lax.ppermute(send, 'dp', axis_pairs(size, mask))  19.4 us
    all_to_all x1, starting transfers between devices, body(): lax.all_to_all(jnp.stack([queries, keys, values]), 'ctx', split_axis=3, c...  14.3 us
  transfers between devices with their start and end apart: 29, of which 23 were waited for; matrix products, arithmetic and copies ran while one was open for 23% of the time, Pallas kernels for 0%

profile of v9, /device:TPU:1, one launch (start us, length us, event | category | flops | bytes accessed | tf_op | source)
XLA Modules:
  0.0 412.9 jit_solution(16075525777736988747)
XLA Ops:
  3.0 14.3 %all-to-all-start = ((bf16[3,1,128,512]{2,0,1,3:T(4,128)(2,1)}), bf16[3,1,128,512]{2,0,1,3:T(4,128)(2,1)S(1)}, u32[]{:S(2)}, u32[]{:S(2)}) async-start(bf16[3,1,128,512]{2,0,1,3:T(4,128)(2,1)} %copy.81), calls=%async_computation | async-start | bytes 1048576 | tf_op jit(solution)/shard_map/all_to_all | solution.py:224
  20.0 3.2 copy.79
  32.3 8.1 %all-to-all-start.2 = ((bf16[32,128,256]{1,2,0:T(8,128)(2,1)}), bf16[32,128,256]{1,2,0:T(8,128)(2,1)}, u32[]{:S(2)}, u32[]{:S(2)}) async-start(bf16[32,128,256]{1,2,0:T(8,128)(2,1)} %bitcast.46), calls=%async_computation.2 | async-start | bytes 4194304 | tf_op jit(solution)/shard_map/all_to_all | solution.py:100
  42.3 7.0 %collective-permute-start = (bf16[256,128]{1,0:T(8,128)(2,1)S(1)}, bf16[256,128]{1,0:T(8,128)(2,1)S(1)}, u32[]{:S(2)}, u32[]{:S(2)}) collective-permute-start(bf16[256,128]{1,0:T(8,128)(2,1)S(1)} %get-tuple-element.60), channel_id=1, source_target_pairs={{0,16},{1,17},{2,18},{3,19},{4,20},{5,21},{6,22},{7,23},{8,24},{9,... | collective-permute-start | bytes 196616 | tf_op jit(solution)/shard_map/ppermute | solution.py:168
  52.1 39.0 %collective-permute-done = bf16[256,128]{1,0:T(8,128)(2,1)S(1)} collective-permute-done((bf16[256,128]{1,0:T(8,128)(2,1)S(1)}, bf16[256,128]{1,0:T(8,128)(2,1)S(1)}, u32[]{:S(2)}, u32[]{:S(2)}) %collective-permute-start) | collective-permute-done | bytes 65568 | tf_op jit(solution)/shard_map/ppermute | solution.py:168
  91.0 5.1 %collective-permute-start.1 = (bf16[512,128]{1,0:T(8,128)(2,1)S(1)}, bf16[512,128]{1,0:T(8,128)(2,1)S(1)}, u32[]{:S(2)}, u32[]{:S(2)}) collective-permute-start(bf16[512,128]{1,0:T(8,128)(2,1)S(1)} %pad_maximum_fusion.22), channel_id=1, source_target_pairs={{0,8},{1,9},{2,10},{3,11},{4,12},{5,13},{6,14},{7,15},{8,0},{9,1},... | collective-permute-start | bytes 393224 | tf_op jit(solution)/shard_map/ppermute | solution.py:168
  100.3 12.8 %collective-permute-start.2 = (bf16[1024,128]{1,0:T(8,128)(2,1)S(1)}, bf16[1024,128]{1,0:T(8,128)(2,1)S(1)}, u32[]{:S(2)}, u32[]{:S(2)}) collective-permute-start(bf16[1024,128]{1,0:T(8,128)(2,1)S(1)} %pad_maximum_fusion.19), channel_id=1, source_target_pairs={{0,2},{1,3},{2,0},{3,1},{4,6},{5,7},{6,4},{7,5},{8,10},{9,11},{10,... | collective-permute-start | bytes 786440 | tf_op jit(solution)/shard_map/ppermute | solution.py:168
  116.2 12.3 %collective-permute-done.2 = bf16[1024,128]{1,0:T(8,128)(2,1)S(1)} collective-permute-done((bf16[1024,128]{1,0:T(8,128)(2,1)S(1)}, bf16[1024,128]{1,0:T(8,128)(2,1)S(1)}, u32[]{:S(2)}, u32[]{:S(2)}) %collective-permute-start.2) | collective-permute-done | bytes 262176 | tf_op jit(solution)/shard_map/ppermute | solution.py:168
  137.0 5.6 %collective-permute-done.3 = bf16[2048,128]{1,0:T(8,128)(2,1)S(1)} collective-permute-done((bf16[2048,128]{1,0:T(8,128)(2,1)S(1)}, bf16[2048,128]{1,0:T(8,128)(2,1)S(1)}, u32[]{:S(2)}, u32[]{:S(2)}) %collective-permute-start.3) | collective-permute-done | bytes 524320 | tf_op jit(solution)/shard_map/ppermute | solution.py:168
  154.7 3.2 select_bitcast_fusion
  157.9 13.3 %collective-permute-done.4 = bf16[4096,128]{1,0:T(8,128)(2,1)} collective-permute-done((bf16[4096,128]{1,0:T(8,128)(2,1)}, bf16[4096,128]{1,0:T(8,128)(2,1)}, u32[]{:S(2)}, u32[]{:S(2)}) %collective-permute-start.4) | collective-permute-done | bytes 1048608 | tf_op jit(solution)/shard_map/ppermute | solution.py:168
  174.5 4.8 %pad_maximum_fusion.1 = bf16[32,512,128]{2,1,0:T(8,128)(2,1)} fusion(bf16[32,256,128]{2,1,0:T(8,128)(2,1)} %bitcast.10, bf16[32,256,128]{2,1,0:T(8,128)(2,1)} %bitcast.9), kind=kLoop, calls=%fused_computation.9 | loop fusion | flops 8388608 | bytes 8388608 | tf_op jit(solution)/shard_map/concatenate | solution.py:113
  179.4 6.0 %collective-permute-start.10 = (bf16[32,512,128]{2,1,0:T(8,128)(2,1)}, bf16[32,512,128]{2,1,0:T(8,128)(2,1)}, u32[]{:S(2)}, u32[]{:S(2)}) collective-permute-start(bf16[32,512,128]{2,1,0:T(8,128)(2,1)} %pad_maximum_fusion.1), channel_id=1, source_target_pairs={{0,32},{32,0},{64,96},{96,64},{128,160},{160,128},{192,224},{224,1... | collective-permute-start | bytes 12582920 | tf_op jit(solution)/shard_map/ppermute | solution.py:114
  188.8 3.3 copy.88
  204.7 4.9 %pad_maximum_fusion = bf16[32,512,256]{2,1,0:T(8,128)(2,1)S(1)} fusion(bf16[32,512,128]{2,1,0:T(8,128)(2,1)} %collective-permute-done.10, bf16[32,256,128]{2,1,0:T(8,128)(2,1)} %bitcast.10, bf16[32,256,128]{2,1,0:T(8,128)(2,1)} %bitcast.9), kind=kLoop, calls=%fused_computation.4 | loop fusion | flops 25165824 | bytes 16777216 | tf_op jit(solution)/shard_map/concatenate | solution.py:115
  220.7 3.9 all-to-all-start.1
  225.4 4.1 copy.94
  229.5 5.4 %all-to-all-done.1 = bf16[32,2,1024]{2,1,0:T(2,128)(2,1)S(1)} async-done(((bf16[32,2,1024]{2,1,0:T(2,128)(2,1)}), bf16[32,2,1024]{2,1,0:T(2,128)(2,1)S(1)}, u32[]{:S(2)}, u32[]{:S(2)}) %all-to-all-start.1) | async-done | bytes 131104 | tf_op jit(solution)/shard_map/all_to_all | solution.py:245
  249.4 8.0 %collective-permute-done.11 = bf16[16,4096]{1,0:T(8,128)(2,1)S(1)} collective-permute-done((bf16[16,4096]{1,0:T(8,128)(2,1)S(1)}, bf16[16,4096]{1,0:T(8,128)(2,1)S(1)}, u32[]{:S(2)}, u32[]{:S(2)}) %collective-permute-start.11) | collective-permute-done | bytes 131104 | tf_op jit(solution)/shard_map/ppermute | solution.py:154
  262.0 11.8 %collective-permute-done.12 = bf16[32,4096]{1,0:T(8,128)(2,1)S(1)} collective-permute-done((bf16[32,4096]{1,0:T(8,128)(2,1)S(1)}, bf16[32,4096]{1,0:T(8,128)(2,1)S(1)}, u32[]{:S(2)}, u32[]{:S(2)}) %collective-permute-start.12) | collective-permute-done | bytes 262176 | tf_op jit(solution)/shard_map/ppermute | solution.py:154
  278.2 22.9 %collective-permute-done.13 = bf16[64,4096]{1,0:T(8,128)(2,1)S(1)} collective-permute-done((bf16[64,4096]{1,0:T(8,128)(2,1)S(1)}, bf16[64,4096]{1,0:T(8,128)(2,1)S(1)}, u32[]{:S(2)}, u32[]{:S(2)}) %collective-permute-start.13) | collective-permute-done | bytes 524320 | tf_op jit(solution)/shard_map/ppermute | solution.py:154
  308.5 7.1 %collective-permute-done.14 = bf16[64,4096]{1,0:T(8,128)(2,1)S(1)} collective-permute-done((bf16[64,4096]{1,0:T(8,128)(2,1)S(1)}, bf16[64,4096]{1,0:T(8,128)(2,1)S(1)}, u32[]{:S(2)}, u32[]{:S(2)}) %collective-permute-start.14) | collective-permute-done | bytes 524320 | tf_op jit(solution)/shard_map/ppermute | solution.py:159
  327.2 16.0 %collective-permute-done.15 = bf16[128,4096]{1,0:T(8,128)(2,1)} collective-permute-done((bf16[128,4096]{1,0:T(8,128)(2,1)}, bf16[128,4096]{1,0:T(8,128)(2,1)}, u32[]{:S(2)}, u32[]{:S(2)}) %collective-permute-start.15) | collective-permute-done | bytes 1048608 | tf_op jit(solution)/shard_map/ppermute | solution.py:159
  350.8 4.6 %collective-permute-start.18 = (f32[264,256]{1,0:T(8,128)S(1)}, f32[264,256]{1,0:T(8,128)S(1)}, u32[]{:S(2)}, u32[]{:S(2)}) collective-permute-start(f32[264,256]{1,0:T(8,128)S(1)} %slice_select_fusion), channel_id=1, source_target_pairs={{0,32},{32,0},{64,96},{96,64},{128,160},{160,128},{192,224},{224,1... | collective-permute-start | bytes 811016 | tf_op jit(solution)/shard_map/ppermute | solution.py:206
  356.7 3.2 collective-permute-start.19
  359.9 3.6 collective-permute-done.19
  363.5 4.6 %collective-permute-start.20 = (f32[66,256]{1,0:T(8,128)S(1)}, f32[66,256]{1,0:T(8,128)S(1)}, u32[]{:S(2)}, u32[]{:S(2)}) collective-permute-start(f32[66,256]{1,0:T(8,128)S(1)} %slice_select_fusion.2), channel_id=1, source_target_pairs={{0,256},{32,288},{64,320},{96,352},{128,384},{160,416},{192,448},{... | collective-permute-start | bytes 202760 | tf_op jit(solution)/shard_map/ppermute | solution.py:206
  370.3 7.1 %collective-permute-start.21 = (f32[33,256]{1,0:T(8,128)S(1)}, f32[33,256]{1,0:T(8,128)S(1)}, u32[]{:S(2)}, u32[]{:S(2)}) collective-permute-start(f32[33,256]{1,0:T(8,128)S(1)} %slice_select_fusion.3), channel_id=1, source_target_pairs={{0,64},{32,96},{64,0},{96,32},{128,192},{160,224},{192,128},{224,1... | collective-permute-start | bytes 101384 | tf_op jit(solution)/shard_map/ppermute | solution.py:206
  378.9 7.1 %collective-permute-start.22 = (f32[33,256]{1,0:T(8,128)S(1)}, f32[33,256]{1,0:T(8,128)S(1)}, u32[]{:S(2)}, u32[]{:S(2)}) collective-permute-start(f32[33,256]{1,0:T(8,128)S(1)} %select_add_fusion.3), channel_id=1, source_target_pairs={{0,64},{32,96},{64,0},{96,32},{128,192},{160,224},{192,128},{224,1... | collective-permute-start | bytes 101384 | tf_op jit(solution)/shard_map/ppermute | solution.py:208
  387.6 4.6 %collective-permute-start.23 = (f32[66,256]{1,0:T(8,128)S(1)}, f32[66,256]{1,0:T(8,128)S(1)}, u32[]{:S(2)}, u32[]{:S(2)}) collective-permute-start(f32[66,256]{1,0:T(8,128)S(1)} %maximum_select_fusion.3), channel_id=1, source_target_pairs={{0,256},{32,288},{64,320},{96,352},{128,384},{160,416},{192,448},{... | collective-permute-start | bytes 202760 | tf_op jit(solution)/shard_map/ppermute | solution.py:208
  397.4 3.4 collective-permute-done.24
  400.9 8.4 %collective-permute-start.25 = (f32[264,256]{1,0:T(8,128)S(1)}, f32[264,256]{1,0:T(8,128)S(1)}, u32[]{:S(2)}, u32[]{:S(2)}) collective-permute-start(f32[264,256]{1,0:T(8,128)S(1)} %maximum_select_fusion.1), channel_id=1, source_target_pairs={{0,32},{32,0},{64,96},{96,64},{128,160},{160,128},{192,224},{224,1... | collective-permute-start | bytes 811016 | tf_op jit(solution)/shard_map/ppermute | solution.py:208
  (230 shorter events, 142.4 us)
Async XLA Ops:
  0.6 24.8 %copy-start = (bf16[512,256]{1,0:T(8,128)(2,1)S(1)}, bf16[512,256]{1,0:T(8,128)(2,1)}, u32[]{:S(2)}) copy-start(bf16[512,256]{1,0:T(8,128)(2,1)} %param.15) | copy-start | bytes 786436
  3.0 29.3 %all-to-all-start = ((bf16[3,1,128,512]{2,0,1,3:T(4,128)(2,1)}), bf16[3,1,128,512]{2,0,1,3:T(4,128)(2,1)S(1)}, u32[]{:S(2)}, u32[]{:S(2)}) async-start(bf16[3,1,128,512]{2,0,1,3:T(4,128)(2,1)} %copy.81), calls=%async_computation | async-start | bytes 1048576 | tf_op jit(solution)/shard_map/all_to_all | solution.py:224
  32.3 188.4 %all-to-all-start.2 = ((bf16[32,128,256]{1,2,0:T(8,128)(2,1)}), bf16[32,128,256]{1,2,0:T(8,128)(2,1)}, u32[]{:S(2)}, u32[]{:S(2)}) async-start(bf16[32,128,256]{1,2,0:T(8,128)(2,1)} %bitcast.46), calls=%async_computation.2 | async-start | bytes 4194304 | tf_op jit(solution)/shard_map/all_to_all | solution.py:100
  40.7 158.2 %copy-start.11 = (bf16[1,4096,16]{1,2,0:T(8,128)(2,1)}, bf16[1,4096,16]{1,2,0:T(8,128)(2,1)S(1)}, u32[]{:S(2)}) copy-start(bf16[1,4096,16]{1,2,0:T(8,128)(2,1)S(1)} %unstack.21) | copy-start | bytes 393220
  42.3 48.7 %collective-permute-start = (bf16[256,128]{1,0:T(8,128)(2,1)S(1)}, bf16[256,128]{1,0:T(8,128)(2,1)S(1)}, u32[]{:S(2)}, u32[]{:S(2)}) collective-permute-start(bf16[256,128]{1,0:T(8,128)(2,1)S(1)} %get-tuple-element.60), channel_id=1, source_target_pairs={{0,16},{1,17},{2,18},{3,19},{4,20},{5,21},{6,22},{7,23},{8,24},{9,... | collective-permute-start | bytes 196616 | tf_op jit(solution)/shard_map/ppermute | solution.py:168
  49.9 46.3 %collective-permute-start.5 = (bf16[256,128]{1,0:T(8,128)(2,1)S(1)}, bf16[256,128]{1,0:T(8,128)(2,1)S(1)}, u32[]{:S(2)}, u32[]{:S(2)}) collective-permute-start(bf16[256,128]{1,0:T(8,128)(2,1)S(1)} %get-tuple-element.59), channel_id=1, source_target_pairs={{0,16},{1,17},{2,18},{3,19},{4,20},{5,21},{6,22},{7,23},{8,24},{9,... | collective-permute-start | bytes 196616 | tf_op jit(solution)/shard_map/ppermute | solution.py:168
  91.0 9.2 %collective-permute-start.1 = (bf16[512,128]{1,0:T(8,128)(2,1)S(1)}, bf16[512,128]{1,0:T(8,128)(2,1)S(1)}, u32[]{:S(2)}, u32[]{:S(2)}) collective-permute-start(bf16[512,128]{1,0:T(8,128)(2,1)S(1)} %pad_maximum_fusion.22), channel_id=1, source_target_pairs={{0,8},{1,9},{2,10},{3,11},{4,12},{5,13},{6,14},{7,15},{8,0},{9,1},... | collective-permute-start | bytes 393224 | tf_op jit(solution)/shard_map/ppermute | solution.py:168
  96.2 18.1 %collective-permute-start.6 = (bf16[512,128]{1,0:T(8,128)(2,1)S(1)}, bf16[512,128]{1,0:T(8,128)(2,1)S(1)}, u32[]{:S(2)}, u32[]{:S(2)}) collective-permute-start(bf16[512,128]{1,0:T(8,128)(2,1)S(1)} %pad_maximum_fusion.23), channel_id=1, source_target_pairs={{0,8},{1,9},{2,10},{3,11},{4,12},{5,13},{6,14},{7,15},{8,0},{9,1},... | collective-permute-start | bytes 393224 | tf_op jit(solution)/shard_map/ppermute | solution.py:168
  100.3 28.3 %collective-permute-start.2 = (bf16[1024,128]{1,0:T(8,128)(2,1)S(1)}, bf16[1024,128]{1,0:T(8,128)(2,1)S(1)}, u32[]{:S(2)}, u32[]{:S(2)}) collective-permute-start(bf16[1024,128]{1,0:T(8,128)(2,1)S(1)} %pad_maximum_fusion.19), channel_id=1, source_target_pairs={{0,2},{1,3},{2,0},{3,1},{4,6},{5,7},{6,4},{7,5},{8,10},{9,11},{10,... | collective-permute-start | bytes 786440 | tf_op jit(solution)/shard_map/ppermute | solution.py:168
  114.3 19.8 %collective-permute-start.7 = (bf16[1024,128]{1,0:T(8,128)(2,1)S(1)}, bf16[1024,128]{1,0:T(8,128)(2,1)S(1)}, u32[]{:S(2)}, u32[]{:S(2)}) collective-permute-start(bf16[1024,128]{1,0:T(8,128)(2,1)S(1)} %pad_maximum_fusion.20), channel_id=1, source_target_pairs={{0,2},{1,3},{2,0},{3,1},{4,6},{5,7},{6,4},{7,5},{8,10},{9,11},{10,... | collective-permute-start | bytes 786440 | tf_op jit(solution)/shard_map/ppermute | solution.py:168
  128.6 14.0 %collective-permute-start.3 = (bf16[2048,128]{1,0:T(8,128)(2,1)S(1)}, bf16[2048,128]{1,0:T(8,128)(2,1)S(1)}, u32[]{:S(2)}, u32[]{:S(2)}) collective-permute-start(bf16[2048,128]{1,0:T(8,128)(2,1)S(1)} %pad_maximum_fusion.12), channel_id=1, source_target_pairs={{0,4},{1,5},{2,6},{3,7},{4,0},{5,1},{6,2},{7,3},{8,12},{9,13},{10,... | collective-permute-start | bytes 1572872 | tf_op jit(solution)/shard_map/ppermute | solution.py:168
  134.2 14.5 %collective-permute-start.8 = (bf16[2048,128]{1,0:T(8,128)(2,1)S(1)}, bf16[2048,128]{1,0:T(8,128)(2,1)S(1)}, u32[]{:S(2)}, u32[]{:S(2)}) collective-permute-start(bf16[2048,128]{1,0:T(8,128)(2,1)S(1)} %pad_maximum_fusion.13), channel_id=1, source_target_pairs={{0,1},{1,0},{2,3},{3,2},{4,5},{5,4},{6,7},{7,6},{8,9},{9,8},{10,11... | collective-permute-start | bytes 1572872 | tf_op jit(solution)/shard_map/ppermute | solution.py:168
  143.6 27.6 %collective-permute-start.4 = (bf16[4096,128]{1,0:T(8,128)(2,1)}, bf16[4096,128]{1,0:T(8,128)(2,1)}, u32[]{:S(2)}, u32[]{:S(2)}) collective-permute-start(bf16[4096,128]{1,0:T(8,128)(2,1)} %get-tuple-element.42), channel_id=1, source_target_pairs={{0,1},{1,0},{2,3},{3,2},{4,5},{5,4},{6,7},{7,6},{8,9},{9,8},{10,11... | collective-permute-start | bytes 3145736 | tf_op jit(solution)/shard_map/ppermute | solution.py:168
  149.7 23.8 %collective-permute-start.9 = (bf16[4096,128]{1,0:T(8,128)(2,1)}, bf16[4096,128]{1,0:T(8,128)(2,1)S(1)}, u32[]{:S(2)}, u32[]{:S(2)}) collective-permute-start(bf16[4096,128]{1,0:T(8,128)(2,1)} %get-tuple-element.44), channel_id=1, source_target_pairs={{0,4},{1,5},{2,6},{3,7},{4,0},{5,1},{6,2},{7,3},{8,12},{9,13},{10,... | collective-permute-start | bytes 3145736 | tf_op jit(solution)/shard_map/ppermute | solution.py:168
  179.4 25.3 %collective-permute-start.10 = (bf16[32,512,128]{2,1,0:T(8,128)(2,1)}, bf16[32,512,128]{2,1,0:T(8,128)(2,1)}, u32[]{:S(2)}, u32[]{:S(2)}) collective-permute-start(bf16[32,512,128]{2,1,0:T(8,128)(2,1)} %pad_maximum_fusion.1), channel_id=1, source_target_pairs={{0,32},{32,0},{64,96},{96,64},{128,160},{160,128},{192,224},{224,1... | collective-permute-start | bytes 12582920 | tf_op jit(solution)/shard_map/ppermute | solution.py:114
  220.7 14.2 %all-to-all-start.1 = ((bf16[32,2,1024]{2,1,0:T(2,128)(2,1)}), bf16[32,2,1024]{2,1,0:T(2,128)(2,1)S(1)}, u32[]{:S(2)}, u32[]{:S(2)}) async-start(bf16[32,2,1024]{2,1,0:T(2,128)(2,1)} %reshape.276), calls=%async_computation.1 | async-start | bytes 262144 | tf_op jit(solution)/shard_map/all_to_all | solution.py:245
  246.7 10.8 %collective-permute-start.11 = (bf16[16,4096]{1,0:T(8,128)(2,1)S(1)}, bf16[16,4096]{1,0:T(8,128)(2,1)S(1)}, u32[]{:S(2)}, u32[]{:S(2)}) collective-permute-start(bf16[16,4096]{1,0:T(8,128)(2,1)S(1)} %get-tuple-element.18), channel_id=1, source_target_pairs={{0,16},{1,17},{2,18},{3,19},{4,20},{5,21},{6,22},{7,23},{8,24},{9,... | collective-permute-start | bytes 393224 | tf_op jit(solution)/shard_map/ppermute | solution.py:154
  257.4 16.3 %collective-permute-start.12 = (bf16[32,4096]{1,0:T(8,128)(2,1)S(1)}, bf16[32,4096]{1,0:T(8,128)(2,1)S(1)}, u32[]{:S(2)}, u32[]{:S(2)}) collective-permute-start(bf16[32,4096]{1,0:T(8,128)(2,1)S(1)} %pad_maximum_fusion.21), channel_id=1, source_target_pairs={{0,8},{1,9},{2,10},{3,11},{4,12},{5,13},{6,14},{7,15},{8,0},{9,1},... | collective-permute-start | bytes 786440 | tf_op jit(solution)/shard_map/ppermute | solution.py:154
  273.8 27.3 %collective-permute-start.13 = (bf16[64,4096]{1,0:T(8,128)(2,1)S(1)}, bf16[64,4096]{1,0:T(8,128)(2,1)S(1)}, u32[]{:S(2)}, u32[]{:S(2)}) collective-permute-start(bf16[64,4096]{1,0:T(8,128)(2,1)S(1)} %pad_maximum_fusion.14), channel_id=1, source_target_pairs={{0,2},{1,3},{2,0},{3,1},{4,6},{5,7},{6,4},{7,5},{8,10},{9,11},{10,... | collective-permute-start | bytes 1572872 | tf_op jit(solution)/shard_map/ppermute | solution.py:154
  301.3 14.3 %collective-permute-start.14 = (bf16[64,4096]{1,0:T(8,128)(2,1)S(1)}, bf16[64,4096]{1,0:T(8,128)(2,1)S(1)}, u32[]{:S(2)}, u32[]{:S(2)}) collective-permute-start(bf16[64,4096]{1,0:T(8,128)(2,1)S(1)} %get-tuple-element.34), channel_id=1, source_target_pairs={{0,4},{1,5},{2,6},{3,7},{4,0},{5,1},{6,2},{7,3},{8,12},{9,13},{10,... | collective-permute-start | bytes 1572872 | tf_op jit(solution)/shard_map/ppermute | solution.py:159
  306.5 14.3 %collective-permute-start.16 = (bf16[64,4096]{1,0:T(8,128)(2,1)S(1)}, bf16[64,4096]{1,0:T(8,128)(2,1)S(1)}, u32[]{:S(2)}, u32[]{:S(2)}) collective-permute-start(bf16[64,4096]{1,0:T(8,128)(2,1)S(1)} %get-tuple-element.35), channel_id=1, source_target_pairs={{0,1},{1,0},{2,3},{3,2},{4,5},{5,4},{6,7},{7,6},{8,9},{9,8},{10,11... | collective-permute-start | bytes 1572872 | tf_op jit(solution)/shard_map/ppermute | solution.py:160
  316.8 26.5 %collective-permute-start.15 = (bf16[128,4096]{1,0:T(8,128)(2,1)}, bf16[128,4096]{1,0:T(8,128)(2,1)}, u32[]{:S(2)}, u32[]{:S(2)}) collective-permute-start(bf16[128,4096]{1,0:T(8,128)(2,1)} %pad_maximum_fusion.6), channel_id=1, source_target_pairs={{0,1},{1,0},{2,3},{3,2},{4,5},{5,4},{6,7},{7,6},{8,9},{9,8},{10,11... | collective-permute-start | bytes 3145736 | tf_op jit(solution)/shard_map/ppermute | solution.py:159
  322.7 25.1 %collective-permute-start.17 = (bf16[128,4096]{1,0:T(8,128)(2,1)}, bf16[128,4096]{1,0:T(8,128)(2,1)}, u32[]{:S(2)}, u32[]{:S(2)}) collective-permute-start(bf16[128,4096]{1,0:T(8,128)(2,1)} %pad_maximum_fusion.7), channel_id=1, source_target_pairs={{0,4},{1,5},{2,6},{3,7},{4,0},{5,1},{6,2},{7,3},{8,12},{9,13},{10,... | collective-permute-start | bytes 3145736 | tf_op jit(solution)/shard_map/ppermute | solution.py:160
  350.8 5.7 %collective-permute-start.18 = (f32[264,256]{1,0:T(8,128)S(1)}, f32[264,256]{1,0:T(8,128)S(1)}, u32[]{:S(2)}, u32[]{:S(2)}) collective-permute-start(f32[264,256]{1,0:T(8,128)S(1)} %slice_select_fusion), channel_id=1, source_target_pairs={{0,32},{32,0},{64,96},{96,64},{128,160},{160,128},{192,224},{224,1... | collective-permute-start | bytes 811016 | tf_op jit(solution)/shard_map/ppermute | solution.py:206
  356.7 6.8 %collective-permute-start.19 = (f32[132,256]{1,0:T(8,128)S(1)}, f32[132,256]{1,0:T(8,128)S(1)}, u32[]{:S(2)}, u32[]{:S(2)}) collective-permute-start(f32[132,256]{1,0:T(8,128)S(1)} %slice_select_fusion.1), channel_id=1, source_target_pairs={{0,128},{32,160},{64,192},{96,224},{128,0},{160,32},{192,64},{224,... | collective-permute-start | bytes 405512 | tf_op jit(solution)/shard_map/ppermute | solution.py:206
  363.4 49.3 %copy-start.1 = (bf16[512,256]{1,0:T(8,128)(2,1)S(1)}, bf16[512,256]{1,0:T(8,128)(2,1)}, u32[]{:S(2)}) copy-start(bf16[512,256]{1,0:T(8,128)(2,1)} %param.15) | copy-start | bytes 786436
  363.5 6.7 %collective-permute-start.20 = (f32[66,256]{1,0:T(8,128)S(1)}, f32[66,256]{1,0:T(8,128)S(1)}, u32[]{:S(2)}, u32[]{:S(2)}) collective-permute-start(f32[66,256]{1,0:T(8,128)S(1)} %slice_select_fusion.2), channel_id=1, source_target_pairs={{0,256},{32,288},{64,320},{96,352},{128,384},{160,416},{192,448},{... | collective-permute-start | bytes 202760 | tf_op jit(solution)/shard_map/ppermute | solution.py:206
  370.3 8.7 %collective-permute-start.21 = (f32[33,256]{1,0:T(8,128)S(1)}, f32[33,256]{1,0:T(8,128)S(1)}, u32[]{:S(2)}, u32[]{:S(2)}) collective-permute-start(f32[33,256]{1,0:T(8,128)S(1)} %slice_select_fusion.3), channel_id=1, source_target_pairs={{0,64},{32,96},{64,0},{96,32},{128,192},{160,224},{192,128},{224,1... | collective-permute-start | bytes 101384 | tf_op jit(solution)/shard_map/ppermute | solution.py:206
  378.9 8.7 %collective-permute-start.22 = (f32[33,256]{1,0:T(8,128)S(1)}, f32[33,256]{1,0:T(8,128)S(1)}, u32[]{:S(2)}, u32[]{:S(2)}) collective-permute-start(f32[33,256]{1,0:T(8,128)S(1)} %select_add_fusion.3), channel_id=1, source_target_pairs={{0,64},{32,96},{64,0},{96,32},{128,192},{160,224},{192,128},{224,1... | collective-permute-start | bytes 101384 | tf_op jit(solution)/shard_map/ppermute | solution.py:208
  387.6 6.6 %collective-permute-start.23 = (f32[66,256]{1,0:T(8,128)S(1)}, f32[66,256]{1,0:T(8,128)S(1)}, u32[]{:S(2)}, u32[]{:S(2)}) collective-permute-start(f32[66,256]{1,0:T(8,128)S(1)} %maximum_select_fusion.3), channel_id=1, source_target_pairs={{0,256},{32,288},{64,320},{96,352},{128,384},{160,416},{192,448},{... | collective-permute-start | bytes 202760 | tf_op jit(solution)/shard_map/ppermute | solution.py:208
  394.2 6.6 %collective-permute-start.24 = (f32[132,256]{1,0:T(8,128)S(1)}, f32[132,256]{1,0:T(8,128)S(1)}, u32[]{:S(2)}, u32[]{:S(2)}) collective-permute-start(f32[132,256]{1,0:T(8,128)S(1)} %maximum_select_fusion.2), channel_id=1, source_target_pairs={{0,128},{32,160},{64,192},{96,224},{128,0},{160,32},{192,64},{224,... | collective-permute-start | bytes 405512 | tf_op jit(solution)/shard_map/ppermute | solution.py:208
  400.9 9.6 %collective-permute-start.25 = (f32[264,256]{1,0:T(8,128)S(1)}, f32[264,256]{1,0:T(8,128)S(1)}, u32[]{:S(2)}, u32[]{:S(2)}) collective-permute-start(f32[264,256]{1,0:T(8,128)S(1)} %maximum_select_fusion.1), channel_id=1, source_target_pairs={{0,32},{32,0},{64,96},{96,64},{128,160},{160,128},{192,224},{224,1... | collective-permute-start | bytes 811016 | tf_op jit(solution)/shard_map/ppermute | solution.py:208
  (24 other events, 169.8 us)
